TPU v7x, 512 devices: a whole 4x4x16 slice. The times are simulated.
512 devices in a mesh: lon: 64 (over x, z_hi, y, core), lat: 8 (over z_lo).
Axes of the slice: x: 4, y: 4, z: 16 (z_hi: 2, z_lo: 8; z = z_hi * 8 + z_lo), core: 2. Of those that a mesh axis runs over, the one named last changes fastest.
Arguments:
- state: float32 [4, 25, 64, 8192], P(None, None, 'lat', 'lon'), may hold values from -6 to 6
- sea_mask: int32 [64, 8192], P('lat', 'lon'), may hold values 0 or 1
- levels: int32 [64, 8192], P('lat', 'lon'), may hold values from 1 to 25
Outputs:
- new_state: float32 [4, 25, 64, 8192], P(None, None, 'lat', 'lon')
All inputs are finite; a program needn't handle non-finite values. No bound on the sum of `sea_mask` on one device may be relied on, other than what follows from the above.
Results may differ from a plain program's by a relative error of at most 0.00002.
Values sent between devices are 32-bit elements; how exact they have to be, the bound alone decides.
No kernel may reach another device: no remote copies, remote signals or barrier semaphores. Data moves between devices by JAX's collectives and lax.ppermute only.
A program may use at most 64 MiB of HBM per device.

v0:
```python
import jax
import jax.numpy as jnp
from jax import lax
from jax.sharding import PartitionSpec as P

TIME_INCREMENT = 0.1
SCALAR_MIXING = 0.4
VISCOSITY = 0.4
THERMAL = 0.2
HALINE = 0.8
GRAVITY = 0.1


def extended_2(x, sides, width, wrap):
    for axis, dim in sides:
        peers, length = (lax.axis_size(axis), x.shape[dim])
        up = [(i, (i + 1) % peers) for i in range(peers if wrap else peers - 1)]
        down = [(j, i) for i, j in up]
        last = lax.slice_in_dim(x, length - width, length, axis=dim)
        first = lax.slice_in_dim(x, 0, width, axis=dim)
        before = lax.ppermute(last, axis, up)
        after = lax.ppermute(first, axis, down)
        x = jnp.concatenate([before, x, after], axis=dim)
    return x


def inner_region(field, row_shift, col_shift):
    n_rows = field.shape[-2]
    n_cols = field.shape[-1]
    return field[
        ..., 2 + row_shift : n_rows - 2 + row_shift, 2 + col_shift : n_cols - 2 + col_shift
    ]


def diff_lon(field):
    return (
        8.0 * (inner_region(field, 0, 1) - inner_region(field, 0, -1))
        - (inner_region(field, 0, 2) - inner_region(field, 0, -2))
    ) / 12.0


def diff_lat(field):
    return (
        8.0 * (inner_region(field, 1, 0) - inner_region(field, -1, 0))
        - (inner_region(field, 2, 0) - inner_region(field, -2, 0))
    ) / 12.0


def second_derivative_sum(field):
    return (
        inner_region(field, 0, 1)
        + inner_region(field, 0, -1)
        + inner_region(field, 1, 0)
        + inner_region(field, -1, 0)
        - 4.0 * inner_region(field, 0, 0)
    )


def coriolis(row_index, total):
    mirrored = jnp.where(row_index >= total, 2 * total - 1 - row_index, row_index)
    return (1.2 * jnp.sin(-1.3 + 2.8 * (mirrored.astype(jnp.float32) + 0.5) / total))[:, None]


def advance_solution(
    heat_content_level,
    saltiness_grid,
    eastward_flow,
    northward_flow,
    weight_of_column,
    sea_cells_count,
    earth_rotation_term,
):
    east = inner_region(eastward_flow, 0, 0)
    north = inner_region(northward_flow, 0, 0)

    def running_solution(field):
        return east * diff_lon(field) + north * diff_lat(field)

    next_heat_level = sea_cells_count * (
        inner_region(heat_content_level, 0, 0)
        + TIME_INCREMENT
        * (
            SCALAR_MIXING * second_derivative_sum(heat_content_level)
            - running_solution(heat_content_level)
        )
    )
    next_saltiness = sea_cells_count * (
        inner_region(saltiness_grid, 0, 0)
        + TIME_INCREMENT
        * (SCALAR_MIXING * second_derivative_sum(saltiness_grid) - running_solution(saltiness_grid))
    )
    next_eastward_flow = sea_cells_count * (
        east
        + TIME_INCREMENT
        * (
            earth_rotation_term * north
            - diff_lon(weight_of_column)
            - running_solution(eastward_flow)
            + VISCOSITY * second_derivative_sum(eastward_flow)
        )
    )
    next_northward_flow = sea_cells_count * (
        north
        + TIME_INCREMENT
        * (
            -earth_rotation_term * east
            - diff_lat(weight_of_column)
            - running_solution(northward_flow)
            + VISCOSITY * second_derivative_sum(northward_flow)
        )
    )
    return jnp.stack([next_heat_level, next_saltiness, next_eastward_flow, next_northward_flow])


def advance_block(extended, sea_cells_count, row_index, total):
    weight_of_column = GRAVITY * jnp.cumsum(HALINE * extended[1] - THERMAL * extended[0], axis=0)
    return advance_solution(
        extended[0],
        extended[1],
        extended[2],
        extended[3],
        weight_of_column,
        sea_cells_count,
        coriolis(row_index, total),
    )


def partner_rows(top_rows):
    lon_count = lax.axis_size("lon")
    n_fields, n_levels, n_rows, n_cols = top_rows.shape
    blocks = top_rows.reshape(n_fields, n_levels, n_rows, lon_count, n_cols // lon_count)
    by_tile = lax.all_to_all(blocks, "lon", split_axis=3, concat_axis=3, tiled=True)
    reversed_tiles = jnp.flip(by_tile, axis=3)
    returned = lax.all_to_all(reversed_tiles, "lon", split_axis=3, concat_axis=3, tiled=True)
    return returned.reshape(n_fields, n_levels, n_rows, n_cols)


def extend_tile(fields, margin, fold_signs):
    tile_rows = fields.shape[2]
    mirror = partner_rows(fields[:, :, tile_rows - margin :, :])
    folded = jnp.flip(mirror, axis=(2, 3)) * fold_signs
    with_fold = jnp.concatenate([fields, folded], axis=2)
    lon_wide = extended_2(with_fold, (("lon", 3),), margin, True)
    extended = extended_2(lon_wide[:, :, :tile_rows, :], (("lat", 2),), margin, False)
    at_top = lax.axis_index("lat") == lax.axis_size("lat") - 1
    upper = jnp.where(
        at_top, lon_wide[:, :, tile_rows:, :], extended[:, :, tile_rows + margin :, :]
    )
    return jnp.concatenate([extended[:, :, : tile_rows + margin, :], upper], axis=2)


def shards(state, sea_mask, levels):
    level_count = state.shape[1]
    tile_rows = state.shape[2]
    depth_index = jnp.arange(level_count, dtype=jnp.int32)[:, None, None]
    sea_cells_count = ((sea_mask[None] == 1) & (depth_index < levels[None])).astype(jnp.float32)
    total = lax.axis_size("lat") * tile_rows
    first_row = lax.axis_index("lat") * tile_rows
    own_rows = first_row + jnp.arange(tile_rows, dtype=jnp.int32)
    fold_signs = jnp.array([1.0, 1.0, -1.0, -1.0], dtype=jnp.float32).reshape(4, 1, 1, 1)
    for step in range(2):
        extended = extend_tile(state, 2, fold_signs)
        state = advance_block(extended, sea_cells_count, own_rows, total)
    return state


def solution(mesh):
    return jax.shard_map(
        shards,
        mesh=mesh,
        in_specs=(P(None, None, "lat", "lon"), P("lat", "lon"), P("lat", "lon")),
        out_specs=P(None, None, "lat", "lon"),
        check_vma=False,
    )
```

profile of v0, /device:TPU:32, one launch (start us, length us, event | category | flops | bytes accessed | tf_op | source)
XLA Modules:
  0.0 210.6 jit_solution(8528074787556256290)
XLA Ops:
  0.0 1.0 slice.378
  1.5 1.2 reshape.39
  2.7 41.5 %all_to_all.20 = f32[64,1,400]{2,1,0:T(1,128)S(1)} all-to-all(f32[64,1,400]{2,1,0:T(1,128)S(1)} %reshape.39), channel_id=1, replica_groups=mesh['lon'=64,'lat'=8] {'lon'}, dimensions={0} | all-to-all | bytes 204800 | tf_op jit(solution)/shard_map/all_to_all | solution.py:132
  46.7 1.8 reshape.41
  48.6 4.7 %all-to-all-start.1 = ((f32[64,1,400]{2,1,0:T(1,128)}), f32[64,1,400]{2,1,0:T(1,128)S(1)}, u32[]{:S(2)}, u32[]{:S(2)}) async-start(f32[64,1,400]{2,1,0:T(1,128)} %reshape.41), calls=%async_computation.1 | async-start | bytes 262144 | tf_op jit(solution)/shard_map/all_to_all | solution.py:134
  53.3 20.5 %all-to-all-done.1 = f32[64,1,400]{2,1,0:T(1,128)S(1)} async-done(((f32[64,1,400]{2,1,0:T(1,128)}), f32[64,1,400]{2,1,0:T(1,128)S(1)}, u32[]{:S(2)}, u32[]{:S(2)}) %all-to-all-start.1) | async-done | bytes 102432 | tf_op jit(solution)/shard_map/all_to_all | solution.py:134
  73.9 0.9 reduce.1
  77.7 3.1 %collective-permute-start.1 = (f32[4,25,10,2]{1,0,3,2:T(4,128)S(1)}, f32[4,25,10,2]{1,0,3,2:T(4,128)S(1)}, u32[]{:S(2)}, u32[]{:S(2)}) collective-permute-start(f32[4,25,10,2]{1,0,3,2:T(4,128)S(1)} %copy.14), channel_id=1, source_target_pairs={{8,0},{16,8},{24,16},{32,24},{40,32},{48,40},{56,48},{64,56},{72,6... | collective-permute-start | bytes 24008 | tf_op jit(solution)/shard_map/ppermute | solution.py:22
  80.9 1.9 collective-permute-start
  82.8 16.8 %collective-permute-done = f32[4,25,10,2]{1,0,3,2:T(4,128)S(1)} collective-permute-done((f32[4,25,10,2]{1,0,3,2:T(4,128)S(1)}, f32[4,25,10,2]{1,0,3,2:T(4,128)S(1)}, u32[]{:S(2)}, u32[]{:S(2)}) %collective-permute-start) | collective-permute-done | bytes 8032 | tf_op jit(solution)/shard_map/ppermute | solution.py:21
  100.7 0.9 pad_maximum_fusion.10
  101.6 1.9 collective-permute-start.2
  103.5 4.1 %collective-permute-start.3 = (f32[4,25,2,132]{3,2,1,0:T(2,128)S(1)}, f32[4,25,2,132]{3,2,1,0:T(2,128)S(1)}, u32[]{:S(2)}, u32[]{:S(2)}) collective-permute-start(f32[4,25,2,132]{3,2,1,0:T(2,128)S(1)} %get-tuple-element.8), channel_id=1, source_target_pairs={{1,0},{2,1},{3,2},{4,3},{5,4},{6,5},{7,6},{9,8},{10,9},{11,10},{12... | collective-permute-start | bytes 316808 | tf_op jit(solution)/shard_map/ppermute | solution.py:22
  108.4 2.7 %collective-permute-done.3 = f32[4,25,2,132]{3,2,1,0:T(2,128)S(1)} collective-permute-done((f32[4,25,2,132]{3,2,1,0:T(2,128)S(1)}, f32[4,25,2,132]{3,2,1,0:T(2,128)S(1)}, u32[]{:S(2)}, u32[]{:S(2)}) %collective-permute-start.3) | collective-permute-done | bytes 105632 | tf_op jit(solution)/shard_map/ppermute | solution.py:22
  114.8 1.2 reshape.43
  116.0 30.5 %all_to_all.21 = f32[64,1,400]{2,1,0:T(1,128)S(1)} all-to-all(f32[64,1,400]{2,1,0:T(1,128)S(1)} %reshape.43), channel_id=1, replica_groups=mesh['lon'=64,'lat'=8] {'lon'}, dimensions={0} | all-to-all | bytes 204800 | tf_op jit(solution)/shard_map/all_to_all | solution.py:132
  148.5 1.2 reshape.45
  149.7 22.5 %all_to_all.22 = f32[64,1,400]{2,1,0:T(1,128)S(1)} all-to-all(f32[64,1,400]{2,1,0:T(1,128)S(1)} %reshape.45), channel_id=1, replica_groups=mesh['lon'=64,'lat'=8] {'lon'}, dimensions={0} | all-to-all | bytes 204800 | tf_op jit(solution)/shard_map/all_to_all | solution.py:134
  175.6 1.9 collective-permute-start.4
  178.0 16.8 %collective-permute-start.5 = (f32[4,25,10,2]{1,0,3,2:T(4,128)S(1)}, f32[4,25,10,2]{1,0,3,2:T(4,128)S(1)}, u32[]{:S(2)}, u32[]{:S(2)}) collective-permute-start(f32[4,25,10,2]{1,0,3,2:T(4,128)S(1)} %copy.22), channel_id=1, source_target_pairs={{8,0},{16,8},{24,16},{32,24},{40,32},{48,40},{56,48},{64,56},{72,6... | collective-permute-start | bytes 24008 | tf_op jit(solution)/shard_map/ppermute | solution.py:22
  196.7 0.9 pad_maximum_fusion.8
  197.6 1.9 collective-permute-start.6
  199.6 3.9 %collective-permute-start.7 = (f32[4,25,2,132]{3,2,1,0:T(2,128)S(1)}, f32[4,25,2,132]{3,2,1,0:T(2,128)S(1)}, u32[]{:S(2)}, u32[]{:S(2)}) collective-permute-start(f32[4,25,2,132]{3,2,1,0:T(2,128)S(1)} %get-tuple-element.6), channel_id=1, source_target_pairs={{1,0},{2,1},{3,2},{4,3},{5,4},{6,5},{7,6},{9,8},{10,9},{11,10},{12... | collective-permute-start | bytes 316808 | tf_op jit(solution)/shard_map/ppermute | solution.py:22
  204.3 2.9 %collective-permute-done.7 = f32[4,25,2,132]{3,2,1,0:T(2,128)S(1)} collective-permute-done((f32[4,25,2,132]{3,2,1,0:T(2,128)S(1)}, f32[4,25,2,132]{3,2,1,0:T(2,128)S(1)}, u32[]{:S(2)}, u32[]{:S(2)}) %collective-permute-start.7) | collective-permute-done | bytes 105632 | tf_op jit(solution)/shard_map/ppermute | solution.py:22
  (70 shorter events, 23.1 us)
Async XLA Ops:
  2.7 50.7 %copy-start.2 = (s32[8,128]{1,0:T(8,128)S(1)}, s32[8,128]{1,0:T(8,128)}, u32[]{:S(2)}) copy-start(s32[8,128]{1,0:T(8,128)} %param.5) | copy-start | bytes 12292
  48.6 28.0 %copy-start.3 = (f32[4]{0:T(128)S(1)}, f32[4]{0:T(128)}, u32[]{:S(2)}) copy-start(f32[4]{0:T(128)} %constant.76.clone) | copy-start | bytes 52
  48.6 28.1 %copy-start = (f32[4,25,8,128]{3,2,1,0:T(8,128)S(1)}, f32[4,25,8,128]{3,2,1,0:T(8,128)}, u32[]{:S(2)}) copy-start(f32[4,25,8,128]{3,2,1,0:T(8,128)} %param.4) | copy-start | bytes 1228804
  48.6 25.3 %all-to-all-start.1 = ((f32[64,1,400]{2,1,0:T(1,128)}), f32[64,1,400]{2,1,0:T(1,128)S(1)}, u32[]{:S(2)}, u32[]{:S(2)}) async-start(f32[64,1,400]{2,1,0:T(1,128)} %reshape.41), calls=%async_computation.1 | async-start | bytes 262144 | tf_op jit(solution)/shard_map/all_to_all | solution.py:134
  77.7 22.4 %collective-permute-start.1 = (f32[4,25,10,2]{1,0,3,2:T(4,128)S(1)}, f32[4,25,10,2]{1,0,3,2:T(4,128)S(1)}, u32[]{:S(2)}, u32[]{:S(2)}) collective-permute-start(f32[4,25,10,2]{1,0,3,2:T(4,128)S(1)} %copy.14), channel_id=1, source_target_pairs={{8,0},{16,8},{24,16},{32,24},{40,32},{48,40},{56,48},{64,56},{72,6... | collective-permute-start | bytes 24008 | tf_op jit(solution)/shard_map/ppermute | solution.py:22
  80.9 18.8 %collective-permute-start = (f32[4,25,10,2]{1,0,3,2:T(4,128)S(1)}, f32[4,25,10,2]{1,0,3,2:T(4,128)S(1)}, u32[]{:S(2)}, u32[]{:S(2)}) collective-permute-start(f32[4,25,10,2]{1,0,3,2:T(4,128)S(1)} %copy.13), channel_id=1, source_target_pairs={{0,8},{8,16},{16,24},{24,32},{32,40},{40,48},{48,56},{56,64},{64,7... | collective-permute-start | bytes 24008 | tf_op jit(solution)/shard_map/ppermute | solution.py:21
  101.6 10.0 %collective-permute-start.2 = (f32[4,25,2,132]{3,2,1,0:T(2,128)S(1)}, f32[4,25,2,132]{3,2,1,0:T(2,128)S(1)}, u32[]{:S(2)}, u32[]{:S(2)}) collective-permute-start(f32[4,25,2,132]{3,2,1,0:T(2,128)S(1)} %get-tuple-element.7), channel_id=1, source_target_pairs={{0,1},{1,2},{2,3},{3,4},{4,5},{5,6},{6,7},{8,9},{9,10},{10,11},{11... | collective-permute-start | bytes 316808 | tf_op jit(solution)/shard_map/ppermute | solution.py:21
  103.5 7.7 %collective-permute-start.3 = (f32[4,25,2,132]{3,2,1,0:T(2,128)S(1)}, f32[4,25,2,132]{3,2,1,0:T(2,128)S(1)}, u32[]{:S(2)}, u32[]{:S(2)}) collective-permute-start(f32[4,25,2,132]{3,2,1,0:T(2,128)S(1)} %get-tuple-element.8), channel_id=1, source_target_pairs={{1,0},{2,1},{3,2},{4,3},{5,4},{6,5},{7,6},{9,8},{10,9},{11,10},{12... | collective-permute-start | bytes 316808 | tf_op jit(solution)/shard_map/ppermute | solution.py:22
  112.1 0.7 copy-start.1
  175.6 19.1 %collective-permute-start.4 = (f32[4,25,10,2]{1,0,3,2:T(4,128)S(1)}, f32[4,25,10,2]{1,0,3,2:T(4,128)S(1)}, u32[]{:S(2)}, u32[]{:S(2)}) collective-permute-start(f32[4,25,10,2]{1,0,3,2:T(4,128)S(1)} %copy.21), channel_id=1, source_target_pairs={{0,8},{8,16},{16,24},{24,32},{32,40},{40,48},{48,56},{56,64},{64,7... | collective-permute-start | bytes 24008 | tf_op jit(solution)/shard_map/ppermute | solution.py:21
  178.0 18.2 %collective-permute-start.5 = (f32[4,25,10,2]{1,0,3,2:T(4,128)S(1)}, f32[4,25,10,2]{1,0,3,2:T(4,128)S(1)}, u32[]{:S(2)}, u32[]{:S(2)}) collective-permute-start(f32[4,25,10,2]{1,0,3,2:T(4,128)S(1)} %copy.22), channel_id=1, source_target_pairs={{8,0},{16,8},{24,16},{32,24},{40,32},{48,40},{56,48},{64,56},{72,6... | collective-permute-start | bytes 24008 | tf_op jit(solution)/shard_map/ppermute | solution.py:22
  197.6 10.0 %collective-permute-start.6 = (f32[4,25,2,132]{3,2,1,0:T(2,128)S(1)}, f32[4,25,2,132]{3,2,1,0:T(2,128)S(1)}, u32[]{:S(2)}, u32[]{:S(2)}) collective-permute-start(f32[4,25,2,132]{3,2,1,0:T(2,128)S(1)} %get-tuple-element.5), channel_id=1, source_target_pairs={{0,1},{1,2},{2,3},{3,4},{4,5},{5,6},{6,7},{8,9},{9,10},{10,11},{11... | collective-permute-start | bytes 316808 | tf_op jit(solution)/shard_map/ppermute | solution.py:21
  199.6 7.7 %collective-permute-start.7 = (f32[4,25,2,132]{3,2,1,0:T(2,128)S(1)}, f32[4,25,2,132]{3,2,1,0:T(2,128)S(1)}, u32[]{:S(2)}, u32[]{:S(2)}) collective-permute-start(f32[4,25,2,132]{3,2,1,0:T(2,128)S(1)} %get-tuple-element.6), channel_id=1, source_target_pairs={{1,0},{2,1},{3,2},{4,3},{5,4},{6,5},{7,6},{9,8},{10,9},{11,10},{12... | collective-permute-start | bytes 316808 | tf_op jit(solution)/shard_map/ppermute | solution.py:22
where the time goes:
time: 211 us
  blocking collectives  94.5 us (45%)
  waiting for transfers between devices  43.9 us (21%)
  starting transfers between devices  40.4 us (19%)
  local copies, waits for them, and re-layouts  18.3 us (9%)
  other arithmetic  13.1 us (6%)
    all_to_all x2, blocking collectives, partner_rows(): lax.all_to_all(blocks, 'lon', split_axis=3, concat_axis=3, tiled=True)  72 us
    ppermute x4, starting transfers between devices, extended_2(): after = lax.ppermute(first, axis, down)  28 us
    all_to_all x1, blocking collectives, partner_rows(): lax.all_to_all(reversed_tiles, 'lon', split_axis=3, concat_axis=3, tiled=...  22.5 us
    all_to_all x1, waiting for transfers between devices, partner_rows(): lax.all_to_all(reversed_tiles, 'lon', split_axis=3, concat_axis=3, tiled=...  20.5 us
    ppermute x4, waiting for transfers between devices, extended_2(): before = lax.ppermute(last, axis, up)  16.8 us
    unnamed x18, local copies, waits for them, and re-layouts  9.89 us
    ppermute x4, starting transfers between devices, extended_2(): before = lax.ppermute(last, axis, up)  7.68 us
    ppermute x4, waiting for transfers between devices, extended_2(): after = lax.ppermute(first, axis, down)  6.56 us
  transfers between devices with their start and end apart: 9, of which 5 were waited for; matrix products, arithmetic and copies ran while one was open for 2% of the time, Pallas kernels for 0%

commit v1 on v0

v1 whole, which is shorter than its diff:
```python
import jax
import jax.numpy as jnp
from jax import lax
from jax.sharding import PartitionSpec as P

TIME_INCREMENT = 0.1
SCALAR_MIXING = 0.4
VISCOSITY = 0.4
THERMAL = 0.2
HALINE = 0.8
GRAVITY = 0.1
MARGIN = 2


def coriolis(row_index, total):
    mirrored = jnp.where(row_index >= total, 2 * total - 1 - row_index, row_index)
    return (1.2 * jnp.sin(-1.3 + 2.8 * (mirrored.astype(jnp.float32) + 0.5) / total))[:, None]


def exchange(x, fold_signs):
    n_lon = lax.axis_size("lon")
    n_lat = lax.axis_size("lat")
    east_ward = [(i, (i + 1) % n_lon) for i in range(n_lon)]
    west_ward = [(j, i) for i, j in east_ward]
    west = lax.ppermute(x[..., -MARGIN:], "lon", east_ward)
    east = lax.ppermute(x[..., :MARGIN], "lon", west_ward)
    north_ward = [(i, i + 1) for i in range(n_lat - 1)]
    south_ward = [(j, i) for i, j in north_ward]
    south = lax.ppermute(x[:, :, -MARGIN:, :], "lat", north_ward)
    north = lax.ppermute(x[:, :, :MARGIN, :], "lat", south_ward)
    top = n_lat - 1
    pairs = [(l * n_lat + top, (n_lon - 1 - l) * n_lat + top) for l in range(n_lon)]
    mirror = lax.ppermute(x[:, :, -MARGIN:, :], ("lon", "lat"), pairs)
    folded = jnp.flip(mirror, axis=(2, 3)) * fold_signs
    north = jnp.where(lax.axis_index("lat") == n_lat - 1, folded, north)
    return west, east, south, north


def step(x, wet, cor, fold_signs):
    rows_n, cols_n = x.shape[2], x.shape[3]
    west, east, south, north = exchange(x, fold_signs)
    rows = jnp.concatenate([south, x, north], axis=2)
    cols = jnp.concatenate([west, x, east], axis=3)

    def at_col(f, s):
        return f[..., MARGIN + s : MARGIN + s + cols_n]

    def at_row(f, s):
        return f[..., MARGIN + s : MARGIN + s + rows_n, :]

    def dx(f):
        return (8.0 * (at_col(f, 1) - at_col(f, -1)) - (at_col(f, 2) - at_col(f, -2))) / 12.0

    def dy(f):
        return (8.0 * (at_row(f, 1) - at_row(f, -1)) - (at_row(f, 2) - at_row(f, -2))) / 12.0

    def lap(fc, fr, f):
        return at_col(fc, 1) + at_col(fc, -1) + at_row(fr, 1) + at_row(fr, -1) - 4.0 * f

    p_rows = GRAVITY * jnp.cumsum(HALINE * rows[1] - THERMAL * rows[0], axis=0)
    p_cols = GRAVITY * jnp.cumsum(HALINE * cols[1] - THERMAL * cols[0], axis=0)
    east_v, north_v = x[2], x[3]

    def adv(i):
        return east_v * dx(cols[i]) + north_v * dy(rows[i])

    heat = wet * (x[0] + TIME_INCREMENT * (SCALAR_MIXING * lap(cols[0], rows[0], x[0]) - adv(0)))
    salt = wet * (x[1] + TIME_INCREMENT * (SCALAR_MIXING * lap(cols[1], rows[1], x[1]) - adv(1)))
    u = wet * (
        east_v
        + TIME_INCREMENT
        * (cor * north_v - dx(p_cols) - adv(2) + VISCOSITY * lap(cols[2], rows[2], east_v))
    )
    v = wet * (
        north_v
        + TIME_INCREMENT
        * (-cor * east_v - dy(p_rows) - adv(3) + VISCOSITY * lap(cols[3], rows[3], north_v))
    )
    return jnp.stack([heat, salt, u, v])


def shards(state, sea_mask, levels):
    level_count = state.shape[1]
    tile_rows = state.shape[2]
    depth_index = jnp.arange(level_count, dtype=jnp.int32)[:, None, None]
    wet = ((sea_mask[None] == 1) & (depth_index < levels[None])).astype(jnp.float32)
    total = lax.axis_size("lat") * tile_rows
    own_rows = lax.axis_index("lat") * tile_rows + jnp.arange(tile_rows, dtype=jnp.int32)
    cor = coriolis(own_rows, total)
    fold_signs = jnp.array([1.0, 1.0, -1.0, -1.0], dtype=jnp.float32).reshape(4, 1, 1, 1)
    for _ in range(2):
        state = step(state, wet, cor, fold_signs)
    return state


def solution(mesh):
    return jax.shard_map(
        shards,
        mesh=mesh,
        in_specs=(P(None, None, "lat", "lon"), P("lat", "lon"), P("lat", "lon")),
        out_specs=P(None, None, "lat", "lon"),
        check_vma=False,
    )
```

time: 211 us -> 94.6 us (0.45)
  the two profiles are of different devices: /device:TPU:32 before, /device:TPU:95 now
where the time goes in v1:
time: 94.6 us; the launch traced here: 94.2 us
  waiting for transfers between devices  44 us (47%)
  starting transfers between devices  41.5 us (44%)
  local copies, waits for them, and re-layouts  4.24 us (4%)
  other arithmetic  4.16 us (4%)
    ppermute x2, waiting for transfers between devices, exchange(): west = lax.ppermute(x[..., -MARGIN:], 'lon', east_ward)  23.4 us
    ppermute x2, starting transfers between devices, exchange(): west = lax.ppermute(x[..., -MARGIN:], 'lon', east_ward)  23.3 us
    ppermute x2, waiting for transfers between devices, exchange(): east = lax.ppermute(x[..., :MARGIN], 'lon', west_ward)  20.6 us
    ppermute x2, starting transfers between devices, exchange(): north = lax.ppermute(x[:, :, :MARGIN, :], 'lat', south_ward)  7.62 us
    ppermute x2, starting transfers between devices, exchange(): south = lax.ppermute(x[:, :, -MARGIN:, :], 'lat', north_ward)  5.47 us
    ppermute x2, starting transfers between devices, exchange(): east = lax.ppermute(x[..., :MARGIN], 'lon', west_ward)  3.84 us
  transfers between devices with their start and end apart: 10, of which 4 were waited for; matrix products, arithmetic and copies ran while one was open for 3% of the time, Pallas kernels for 0%

profile of v1, /device:TPU:95, one launch (start us, length us, event | category | flops | bytes accessed | tf_op | source)
XLA Modules:
  0.0 94.2 jit_solution(16222748270475659234)
XLA Ops:
  0.0 1.2 %fusion.159 = (f32[4,25,2,128]{3,2,1,0:T(2,128)S(1)}, f32[4,25,2,128]{3,2,1,0:T(2,128)S(1)}) fusion(f32[4,25,8,128]{3,2,1,0:T(8,128)} %param.4), kind=kLoop, calls=%fused_computation.220 | loop fusion | bytes 409600 | tf_op jit(solution)/shard_map/slice | solution.py:29
  1.3 0.7 collective-permute-start.3
  1.9 3.5 %collective-permute-start.2 = (f32[4,25,2,128]{3,2,1,0:T(2,128)S(1)}, f32[4,25,2,128]{3,2,1,0:T(2,128)S(1)}, u32[]{:S(2)}, u32[]{:S(2)}) collective-permute-start(f32[4,25,2,128]{3,2,1,0:T(2,128)S(1)} %get-tuple-element.27), channel_id=1, source_target_pairs={{0,1},{1,2},{2,3},{3,4},{4,5},{5,6},{6,7},{8,9},{9,10},{10,11},{11... | collective-permute-start | bytes 307208 | tf_op jit(solution)/shard_map/ppermute | solution.py:29
  5.5 1.9 %collective-permute-start.4 = (f32[4,25,2,128]{3,2,1,0:T(2,128)S(1)}, f32[4,25,2,128]{3,2,1,0:T(2,128)S(1)}, u32[]{:S(2)}, u32[]{:S(2)}) collective-permute-start(f32[4,25,2,128]{3,2,1,0:T(2,128)S(1)} %get-tuple-element.28), channel_id=1, source_target_pairs={{1,0},{2,1},{3,2},{4,3},{5,4},{6,5},{7,6},{9,8},{10,9},{11,10},{12... | collective-permute-start | bytes 307208 | tf_op jit(solution)/shard_map/ppermute | solution.py:30
  7.6 14.2 %collective-permute-start = (f32[4,25,8,2]{3,2,1,0:T(8,128)S(1)}, f32[4,25,8,2]{3,2,1,0:T(8,128)S(1)}, u32[]{:S(2)}, u32[]{:S(2)}) collective-permute-start(f32[4,25,8,2]{3,2,1,0:T(8,128)S(1)} %get-tuple-element.25), channel_id=1, source_target_pairs={{0,8},{8,16},{16,24},{24,32},{32,40},{40,48},{48,56},{56,64},{64,7... | collective-permute-start | bytes 19208 | tf_op jit(solution)/shard_map/ppermute | solution.py:25
  21.9 1.9 %collective-permute-start.1 = (f32[4,25,8,2]{3,2,1,0:T(8,128)S(1)}, f32[4,25,8,2]{3,2,1,0:T(8,128)S(1)}, u32[]{:S(2)}, u32[]{:S(2)}) collective-permute-start(f32[4,25,8,2]{3,2,1,0:T(8,128)S(1)} %get-tuple-element.26), channel_id=1, source_target_pairs={{8,0},{16,8},{24,16},{32,24},{40,32},{48,40},{56,48},{64,56},{72,6... | collective-permute-start | bytes 19208 | tf_op jit(solution)/shard_map/ppermute | solution.py:26
  23.9 0.6 copy-done.2
  24.5 14.7 %collective-permute-done = f32[4,25,8,2]{3,2,1,0:T(8,128)S(1)} collective-permute-done((f32[4,25,8,2]{3,2,1,0:T(8,128)S(1)}, f32[4,25,8,2]{3,2,1,0:T(8,128)S(1)}, u32[]{:S(2)}, u32[]{:S(2)}) %collective-permute-start) | collective-permute-done | bytes 6432 | tf_op jit(solution)/shard_map/ppermute | solution.py:25
  39.3 6.2 %collective-permute-done.1 = f32[4,25,8,2]{3,2,1,0:T(8,128)S(1)} collective-permute-done((f32[4,25,8,2]{3,2,1,0:T(8,128)S(1)}, f32[4,25,8,2]{3,2,1,0:T(8,128)S(1)}, u32[]{:S(2)}, u32[]{:S(2)}) %collective-permute-start.1) | collective-permute-done | bytes 6432 | tf_op jit(solution)/shard_map/ppermute | solution.py:26
  45.5 0.4 pad_maximum_fusion
  46.1 0.4 rev.7
  47.2 0.6 copy-done.1
  48.1 0.2 fusion.94
  48.8 9.0 %collective-permute-start.5 = (f32[4,25,8,2]{3,2,1,0:T(8,128)S(1)}, f32[4,25,8,2]{3,2,1,0:T(8,128)S(1)}, u32[]{:S(2)}, u32[]{:S(2)}) collective-permute-start(f32[4,25,8,2]{3,2,1,0:T(8,128)S(1)} %get-tuple-element.21), channel_id=1, source_target_pairs={{0,8},{8,16},{16,24},{24,32},{32,40},{40,48},{48,56},{56,64},{64,7... | collective-permute-start | bytes 19208 | tf_op jit(solution)/shard_map/ppermute | solution.py:25
  57.8 1.9 %collective-permute-start.6 = (f32[4,25,8,2]{3,2,1,0:T(8,128)S(1)}, f32[4,25,8,2]{3,2,1,0:T(8,128)S(1)}, u32[]{:S(2)}, u32[]{:S(2)}) collective-permute-start(f32[4,25,8,2]{3,2,1,0:T(8,128)S(1)} %get-tuple-element.22), channel_id=1, source_target_pairs={{8,0},{16,8},{24,16},{32,24},{40,32},{48,40},{56,48},{64,56},{72,6... | collective-permute-start | bytes 19208 | tf_op jit(solution)/shard_map/ppermute | solution.py:26
  59.8 0.7 collective-permute-start.8
  60.5 1.9 %collective-permute-start.7 = (f32[4,25,2,128]{3,2,1,0:T(2,128)S(1)}, f32[4,25,2,128]{3,2,1,0:T(2,128)S(1)}, u32[]{:S(2)}, u32[]{:S(2)}) collective-permute-start(f32[4,25,2,128]{3,2,1,0:T(2,128)S(1)} %get-tuple-element.23), channel_id=1, source_target_pairs={{0,1},{1,2},{2,3},{3,4},{4,5},{5,6},{6,7},{8,9},{9,10},{10,11},{11... | collective-permute-start | bytes 307208 | tf_op jit(solution)/shard_map/ppermute | solution.py:29
  62.4 5.7 %collective-permute-start.9 = (f32[4,25,2,128]{3,2,1,0:T(2,128)S(1)}, f32[4,25,2,128]{3,2,1,0:T(2,128)S(1)}, u32[]{:S(2)}, u32[]{:S(2)}) collective-permute-start(f32[4,25,2,128]{3,2,1,0:T(2,128)S(1)} %get-tuple-element.24), channel_id=1, source_target_pairs={{1,0},{2,1},{3,2},{4,3},{5,4},{6,5},{7,6},{9,8},{10,9},{11,10},{12... | collective-permute-start | bytes 307208 | tf_op jit(solution)/shard_map/ppermute | solution.py:30
  68.1 8.6 %collective-permute-done.5 = f32[4,25,8,2]{3,2,1,0:T(8,128)S(1)} collective-permute-done((f32[4,25,8,2]{3,2,1,0:T(8,128)S(1)}, f32[4,25,8,2]{3,2,1,0:T(8,128)S(1)}, u32[]{:S(2)}, u32[]{:S(2)}) %collective-permute-start.5) | collective-permute-done | bytes 6432 | tf_op jit(solution)/shard_map/ppermute | solution.py:25
  76.7 14.4 %collective-permute-done.6 = f32[4,25,8,2]{3,2,1,0:T(8,128)S(1)} collective-permute-done((f32[4,25,8,2]{3,2,1,0:T(8,128)S(1)}, f32[4,25,8,2]{3,2,1,0:T(8,128)S(1)}, u32[]{:S(2)}, u32[]{:S(2)}) %collective-permute-start.6) | collective-permute-done | bytes 6432 | tf_op jit(solution)/shard_map/ppermute | solution.py:26
  91.2 0.4 pad_maximum_fusion.2
  91.8 0.4 rev.8
  93.0 0.2 fusion.38
  93.5 0.8 pad_maximum_fusion.5
  (37 shorter events, 3.1 us)
Async XLA Ops:
  0.0 7.4 %copy-start = (f32[4,25,8,128]{3,2,1,0:T(8,128)S(1)}, f32[4,25,8,128]{3,2,1,0:T(8,128)}, u32[]{:S(2)}) copy-start(f32[4,25,8,128]{3,2,1,0:T(8,128)} %param.4) | copy-start | bytes 1228804
  1.3 44.8 %collective-permute-start.3 = (f32[4,25,2,128]{3,2,1,0:T(2,128)S(1)}, f32[4,25,2,128]{3,2,1,0:T(2,128)S(1)}, u32[]{:S(2)}, u32[]{:S(2)}) collective-permute-start(f32[4,25,2,128]{3,2,1,0:T(2,128)S(1)} %get-tuple-element.27), channel_id=1, source_target_pairs={{7,511},{15,503},{23,495},{31,487},{39,479},{47,471},{55,463},{63,... | collective-permute-start | bytes 307208 | tf_op jit(solution)/shard_map/ppermute | solution.py:33
  1.9 44.9 %collective-permute-start.2 = (f32[4,25,2,128]{3,2,1,0:T(2,128)S(1)}, f32[4,25,2,128]{3,2,1,0:T(2,128)S(1)}, u32[]{:S(2)}, u32[]{:S(2)}) collective-permute-start(f32[4,25,2,128]{3,2,1,0:T(2,128)S(1)} %get-tuple-element.27), channel_id=1, source_target_pairs={{0,1},{1,2},{2,3},{3,4},{4,5},{5,6},{6,7},{8,9},{9,10},{10,11},{11... | collective-permute-start | bytes 307208 | tf_op jit(solution)/shard_map/ppermute | solution.py:29
  5.5 41.0 %collective-permute-start.4 = (f32[4,25,2,128]{3,2,1,0:T(2,128)S(1)}, f32[4,25,2,128]{3,2,1,0:T(2,128)S(1)}, u32[]{:S(2)}, u32[]{:S(2)}) collective-permute-start(f32[4,25,2,128]{3,2,1,0:T(2,128)S(1)} %get-tuple-element.28), channel_id=1, source_target_pairs={{1,0},{2,1},{3,2},{4,3},{5,4},{6,5},{7,6},{9,8},{10,9},{11,10},{12... | collective-permute-start | bytes 307208 | tf_op jit(solution)/shard_map/ppermute | solution.py:30
  7.6 31.7 %collective-permute-start = (f32[4,25,8,2]{3,2,1,0:T(8,128)S(1)}, f32[4,25,8,2]{3,2,1,0:T(8,128)S(1)}, u32[]{:S(2)}, u32[]{:S(2)}) collective-permute-start(f32[4,25,8,2]{3,2,1,0:T(8,128)S(1)} %get-tuple-element.25), channel_id=1, source_target_pairs={{0,8},{8,16},{16,24},{24,32},{32,40},{40,48},{48,56},{56,64},{64,7... | collective-permute-start | bytes 19208 | tf_op jit(solution)/shard_map/ppermute | solution.py:25
  21.9 23.6 %collective-permute-start.1 = (f32[4,25,8,2]{3,2,1,0:T(8,128)S(1)}, f32[4,25,8,2]{3,2,1,0:T(8,128)S(1)}, u32[]{:S(2)}, u32[]{:S(2)}) collective-permute-start(f32[4,25,8,2]{3,2,1,0:T(8,128)S(1)} %get-tuple-element.26), channel_id=1, source_target_pairs={{8,0},{16,8},{24,16},{32,24},{40,32},{48,40},{56,48},{64,56},{72,6... | collective-permute-start | bytes 19208 | tf_op jit(solution)/shard_map/ppermute | solution.py:26
  23.8 0.7 copy-start.2
  46.1 0.7 copy-start.3
  47.1 0.7 copy-start.1
  48.8 27.9 %collective-permute-start.5 = (f32[4,25,8,2]{3,2,1,0:T(8,128)S(1)}, f32[4,25,8,2]{3,2,1,0:T(8,128)S(1)}, u32[]{:S(2)}, u32[]{:S(2)}) collective-permute-start(f32[4,25,8,2]{3,2,1,0:T(8,128)S(1)} %get-tuple-element.21), channel_id=1, source_target_pairs={{0,8},{8,16},{16,24},{24,32},{32,40},{40,48},{48,56},{56,64},{64,7... | collective-permute-start | bytes 19208 | tf_op jit(solution)/shard_map/ppermute | solution.py:25
  57.8 33.4 %collective-permute-start.6 = (f32[4,25,8,2]{3,2,1,0:T(8,128)S(1)}, f32[4,25,8,2]{3,2,1,0:T(8,128)S(1)}, u32[]{:S(2)}, u32[]{:S(2)}) collective-permute-start(f32[4,25,8,2]{3,2,1,0:T(8,128)S(1)} %get-tuple-element.22), channel_id=1, source_target_pairs={{8,0},{16,8},{24,16},{32,24},{40,32},{48,40},{56,48},{64,56},{72,6... | collective-permute-start | bytes 19208 | tf_op jit(solution)/shard_map/ppermute | solution.py:26
  59.8 31.9 %collective-permute-start.8 = (f32[4,25,2,128]{3,2,1,0:T(2,128)S(1)}, f32[4,25,2,128]{3,2,1,0:T(2,128)S(1)}, u32[]{:S(2)}, u32[]{:S(2)}) collective-permute-start(f32[4,25,2,128]{3,2,1,0:T(2,128)S(1)} %get-tuple-element.23), channel_id=1, source_target_pairs={{7,511},{15,503},{23,495},{31,487},{39,479},{47,471},{55,463},{63,... | collective-permute-start | bytes 307208 | tf_op jit(solution)/shard_map/ppermute | solution.py:33
  60.5 31.8 %collective-permute-start.7 = (f32[4,25,2,128]{3,2,1,0:T(2,128)S(1)}, f32[4,25,2,128]{3,2,1,0:T(2,128)S(1)}, u32[]{:S(2)}, u32[]{:S(2)}) collective-permute-start(f32[4,25,2,128]{3,2,1,0:T(2,128)S(1)} %get-tuple-element.23), channel_id=1, source_target_pairs={{0,1},{1,2},{2,3},{3,4},{4,5},{5,6},{6,7},{8,9},{9,10},{10,11},{11... | collective-permute-start | bytes 307208 | tf_op jit(solution)/shard_map/ppermute | solution.py:29
  62.4 29.8 %collective-permute-start.9 = (f32[4,25,2,128]{3,2,1,0:T(2,128)S(1)}, f32[4,25,2,128]{3,2,1,0:T(2,128)S(1)}, u32[]{:S(2)}, u32[]{:S(2)}) collective-permute-start(f32[4,25,2,128]{3,2,1,0:T(2,128)S(1)} %get-tuple-element.24), channel_id=1, source_target_pairs={{1,0},{2,1},{3,2},{4,3},{5,4},{6,5},{7,6},{9,8},{10,9},{11,10},{12... | collective-permute-start | bytes 307208 | tf_op jit(solution)/shard_map/ppermute | solution.py:30

commit v2 on v1

--- a/solution.py
+++ b/solution.py
@@ -24,15 +24,24 @@
     west_ward = [(j, i) for i, j in east_ward]
     west = lax.ppermute(x[..., -MARGIN:], "lon", east_ward)
     east = lax.ppermute(x[..., :MARGIN], "lon", west_ward)
-    north_ward = [(i, i + 1) for i in range(n_lat - 1)]
-    south_ward = [(j, i) for i, j in north_ward]
-    south = lax.ppermute(x[:, :, -MARGIN:, :], "lat", north_ward)
-    north = lax.ppermute(x[:, :, :MARGIN, :], "lat", south_ward)
+    lat = lax.axis_index("lat")
+    odd = lat % 2 == 1
+    top_rows = x[:, :, -MARGIN:, :]
+    bottom_rows = x[:, :, :MARGIN, :]
+    to_odd = lax.ppermute(
+        jnp.where(odd, bottom_rows, top_rows),
+        ("lon", "lat"),
+        [(l * n_lat + i, l * n_lat + (i ^ 1)) for l in range(n_lon) for i in range(n_lat)],
+    )
+    inner = [(i, i + 1) for i in range(1, n_lat - 1, 2)]
+    inner = inner + [(j, i) for i, j in inner]
     top = n_lat - 1
-    pairs = [(l * n_lat + top, (n_lon - 1 - l) * n_lat + top) for l in range(n_lon)]
-    mirror = lax.ppermute(x[:, :, -MARGIN:, :], ("lon", "lat"), pairs)
-    folded = jnp.flip(mirror, axis=(2, 3)) * fold_signs
-    north = jnp.where(lax.axis_index("lat") == n_lat - 1, folded, north)
+    pairs = [(l * n_lat + i, l * n_lat + j) for l in range(n_lon) for i, j in inner]
+    pairs = pairs + [(l * n_lat + top, (n_lon - 1 - l) * n_lat + top) for l in range(n_lon)]
+    to_even = lax.ppermute(jnp.where(odd, top_rows, bottom_rows), ("lon", "lat"), pairs)
+    folded = jnp.flip(to_even, axis=(2, 3)) * fold_signs
+    north = jnp.where(odd, jnp.where(lat == top, folded, to_even), to_odd)
+    south = jnp.where(odd, to_odd, to_even)
     return west, east, south, north
 
 

time: 94.6 us -> 97.5 us (1.031)
  the two profiles are of different devices: /device:TPU:95 before, /device:TPU:59 now
where the time goes in v2:
time: 97.5 us; the launch traced here: 97.2 us
  waiting for transfers between devices  58.8 us (60%)
  starting transfers between devices  30.2 us (31%)
  other arithmetic  5.57 us (6%)
  local copies, waits for them, and re-layouts  2.3 us (2%)
    ppermute x2, waiting for transfers between devices, exchange(): east = lax.ppermute(x[..., :MARGIN], 'lon', west_ward)  32.8 us
    ppermute x2, waiting for transfers between devices, exchange(): west = lax.ppermute(x[..., -MARGIN:], 'lon', east_ward)  26 us
    ppermute x2, starting transfers between devices, exchange(): west = lax.ppermute(x[..., -MARGIN:], 'lon', east_ward)  16.1 us
    ppermute x2, starting transfers between devices, exchange(): lax.ppermute(jnp.where(odd, top_rows, bottom_rows), ('lon', 'lat'), pairs)  5.47 us
    ppermute x2, starting transfers between devices, exchange(): east = lax.ppermute(x[..., :MARGIN], 'lon', west_ward)  4.33 us
    ppermute x2, starting transfers between devices, exchange(): lax.ppermute(jnp.where(odd, bottom_rows, top_rows), ('lon', 'lat'), [(l *...  4.29 us
  transfers between devices with their start and end apart: 8, of which 4 were waited for; matrix products, arithmetic and copies ran while one was open for 2% of the time, Pallas kernels for 0%

profile of v2, /device:TPU:59, one launch (start us, length us, event | category | flops | bytes accessed | tf_op | source)
XLA Modules:
  0.0 97.2 jit_solution(9124566083665443243)
XLA Ops:
  0.0 1.3 %broadcast_select_fusion.4 = (f32[4,25,2,128]{3,2,1,0:T(2,128)S(1)}, f32[4,25,2,128]{3,2,1,0:T(2,128)S(1)}) fusion(pred[]{:T(512)S(6)} %eq.20, f32[4,25,8,128]{3,2,1,0:T(8,128)} %param.4), kind=kLoop, calls=%fused_computation.204 | loop fusion | flops 51200 | bytes 409601 | tf_op jit(solution)/shard_map/jit(_where)/select_n | solution.py:41
  1.3 3.5 %collective-permute-start.3 = (f32[4,25,2,128]{3,2,1,0:T(2,128)S(1)}, f32[4,25,2,128]{3,2,1,0:T(2,128)S(1)}, u32[]{:S(2)}, u32[]{:S(2)}) collective-permute-start(f32[4,25,2,128]{3,2,1,0:T(2,128)S(1)} %get-tuple-element.27), channel_id=1, source_target_pairs={{1,2},{3,4},{5,6},{2,1},{4,3},{6,5},{9,10},{11,12},{13,14},{10,9},... | collective-permute-start | bytes 307208 | tf_op jit(solution)/shard_map/ppermute | solution.py:41
  4.8 1.9 %collective-permute-start.2 = (f32[4,25,2,128]{3,2,1,0:T(2,128)S(1)}, f32[4,25,2,128]{3,2,1,0:T(2,128)S(1)}, u32[]{:S(2)}, u32[]{:S(2)}) collective-permute-start(f32[4,25,2,128]{3,2,1,0:T(2,128)S(1)} %get-tuple-element.28), channel_id=1, source_target_pairs={{0,1},{1,0},{2,3},{3,2},{4,5},{5,4},{6,7},{7,6},{8,9},{9,8},{10,11... | collective-permute-start | bytes 307208 | tf_op jit(solution)/shard_map/ppermute | solution.py:31
  7.0 14.1 %collective-permute-start = (f32[4,25,8,2]{3,2,1,0:T(8,128)S(1)}, f32[4,25,8,2]{3,2,1,0:T(8,128)S(1)}, u32[]{:S(2)}, u32[]{:S(2)}) collective-permute-start(f32[4,25,8,2]{3,2,1,0:T(8,128)S(1)} %get-tuple-element.25), channel_id=1, source_target_pairs={{0,8},{8,16},{16,24},{24,32},{32,40},{40,48},{48,56},{56,64},{64,7... | collective-permute-start | bytes 19208 | tf_op jit(solution)/shard_map/ppermute | solution.py:25
  21.1 1.9 %collective-permute-start.1 = (f32[4,25,8,2]{3,2,1,0:T(8,128)S(1)}, f32[4,25,8,2]{3,2,1,0:T(8,128)S(1)}, u32[]{:S(2)}, u32[]{:S(2)}) collective-permute-start(f32[4,25,8,2]{3,2,1,0:T(8,128)S(1)} %get-tuple-element.26), channel_id=1, source_target_pairs={{8,0},{16,8},{24,16},{32,24},{40,32},{48,40},{56,48},{64,56},{72,6... | collective-permute-start | bytes 19208 | tf_op jit(solution)/shard_map/ppermute | solution.py:26
  23.2 13.2 %collective-permute-done = f32[4,25,8,2]{3,2,1,0:T(8,128)S(1)} collective-permute-done((f32[4,25,8,2]{3,2,1,0:T(8,128)S(1)}, f32[4,25,8,2]{3,2,1,0:T(8,128)S(1)}, u32[]{:S(2)}, u32[]{:S(2)}) %collective-permute-start) | collective-permute-done | bytes 6432 | tf_op jit(solution)/shard_map/ppermute | solution.py:25
  36.3 18.1 %collective-permute-done.1 = f32[4,25,8,2]{3,2,1,0:T(8,128)S(1)} collective-permute-done((f32[4,25,8,2]{3,2,1,0:T(8,128)S(1)}, f32[4,25,8,2]{3,2,1,0:T(8,128)S(1)}, u32[]{:S(2)}, u32[]{:S(2)}) %collective-permute-start.1) | collective-permute-done | bytes 6432 | tf_op jit(solution)/shard_map/ppermute | solution.py:26
  54.4 0.4 pad_maximum_fusion
  55.0 0.4 rev.7
  55.4 0.2 copy-done.3
  56.1 0.6 copy-done.1
  57.1 0.2 fusion.94
  57.3 0.2 fusion.78
  57.8 1.9 %collective-permute-start.4 = (f32[4,25,8,2]{3,2,1,0:T(8,128)S(1)}, f32[4,25,8,2]{3,2,1,0:T(8,128)S(1)}, u32[]{:S(2)}, u32[]{:S(2)}) collective-permute-start(f32[4,25,8,2]{3,2,1,0:T(8,128)S(1)} %get-tuple-element.21), channel_id=1, source_target_pairs={{0,8},{8,16},{16,24},{24,32},{32,40},{40,48},{48,56},{56,64},{64,7... | collective-permute-start | bytes 19208 | tf_op jit(solution)/shard_map/ppermute | solution.py:25
  59.7 2.4 %collective-permute-start.5 = (f32[4,25,8,2]{3,2,1,0:T(8,128)S(1)}, f32[4,25,8,2]{3,2,1,0:T(8,128)S(1)}, u32[]{:S(2)}, u32[]{:S(2)}) collective-permute-start(f32[4,25,8,2]{3,2,1,0:T(8,128)S(1)} %get-tuple-element.22), channel_id=1, source_target_pairs={{8,0},{16,8},{24,16},{32,24},{40,32},{48,40},{56,48},{64,56},{72,6... | collective-permute-start | bytes 19208 | tf_op jit(solution)/shard_map/ppermute | solution.py:26
  62.2 1.9 %collective-permute-start.7 = (f32[4,25,2,128]{3,2,1,0:T(2,128)S(1)}, f32[4,25,2,128]{3,2,1,0:T(2,128)S(1)}, u32[]{:S(2)}, u32[]{:S(2)}) collective-permute-start(f32[4,25,2,128]{3,2,1,0:T(2,128)S(1)} %get-tuple-element.23), channel_id=1, source_target_pairs={{1,2},{3,4},{5,6},{2,1},{4,3},{6,5},{9,10},{11,12},{13,14},{10,9},... | collective-permute-start | bytes 307208 | tf_op jit(solution)/shard_map/ppermute | solution.py:41
  64.1 2.4 %collective-permute-start.6 = (f32[4,25,2,128]{3,2,1,0:T(2,128)S(1)}, f32[4,25,2,128]{3,2,1,0:T(2,128)S(1)}, u32[]{:S(2)}, u32[]{:S(2)}) collective-permute-start(f32[4,25,2,128]{3,2,1,0:T(2,128)S(1)} %get-tuple-element.24), channel_id=1, source_target_pairs={{0,1},{1,0},{2,3},{3,2},{4,5},{5,4},{6,7},{7,6},{8,9},{9,8},{10,11... | collective-permute-start | bytes 307208 | tf_op jit(solution)/shard_map/ppermute | solution.py:31
  66.5 12.8 %collective-permute-done.4 = f32[4,25,8,2]{3,2,1,0:T(8,128)S(1)} collective-permute-done((f32[4,25,8,2]{3,2,1,0:T(8,128)S(1)}, f32[4,25,8,2]{3,2,1,0:T(8,128)S(1)}, u32[]{:S(2)}, u32[]{:S(2)}) %collective-permute-start.4) | collective-permute-done | bytes 6432 | tf_op jit(solution)/shard_map/ppermute | solution.py:25
  79.3 14.7 %collective-permute-done.5 = f32[4,25,8,2]{3,2,1,0:T(8,128)S(1)} collective-permute-done((f32[4,25,8,2]{3,2,1,0:T(8,128)S(1)}, f32[4,25,8,2]{3,2,1,0:T(8,128)S(1)}, u32[]{:S(2)}, u32[]{:S(2)}) %collective-permute-start.5) | collective-permute-done | bytes 6432 | tf_op jit(solution)/shard_map/ppermute | solution.py:26
  94.1 0.4 pad_maximum_fusion.2
  94.7 0.4 rev.8
  95.9 0.2 fusion.38
  96.2 0.2 fusion.21
  96.4 0.8 pad_maximum_fusion.5
  (33 shorter events, 2.5 us)
Async XLA Ops:
  0.0 6.7 %copy-start = (f32[4,25,8,128]{3,2,1,0:T(8,128)S(1)}, f32[4,25,8,128]{3,2,1,0:T(8,128)}, u32[]{:S(2)}) copy-start(f32[4,25,8,128]{3,2,1,0:T(8,128)} %param.4) | copy-start | bytes 1228804
  1.3 53.7 %collective-permute-start.3 = (f32[4,25,2,128]{3,2,1,0:T(2,128)S(1)}, f32[4,25,2,128]{3,2,1,0:T(2,128)S(1)}, u32[]{:S(2)}, u32[]{:S(2)}) collective-permute-start(f32[4,25,2,128]{3,2,1,0:T(2,128)S(1)} %get-tuple-element.27), channel_id=1, source_target_pairs={{1,2},{3,4},{5,6},{2,1},{4,3},{6,5},{9,10},{11,12},{13,14},{10,9},... | collective-permute-start | bytes 307208 | tf_op jit(solution)/shard_map/ppermute | solution.py:41
  4.8 50.6 %collective-permute-start.2 = (f32[4,25,2,128]{3,2,1,0:T(2,128)S(1)}, f32[4,25,2,128]{3,2,1,0:T(2,128)S(1)}, u32[]{:S(2)}, u32[]{:S(2)}) collective-permute-start(f32[4,25,2,128]{3,2,1,0:T(2,128)S(1)} %get-tuple-element.28), channel_id=1, source_target_pairs={{0,1},{1,0},{2,3},{3,2},{4,5},{5,4},{6,7},{7,6},{8,9},{9,8},{10,11... | collective-permute-start | bytes 307208 | tf_op jit(solution)/shard_map/ppermute | solution.py:31
  6.9 16.1 %copy-start.2 = (s32[8,128]{1,0:T(8,128)S(1)}, s32[8,128]{1,0:T(8,128)}, u32[]{:S(2)}) copy-start(s32[8,128]{1,0:T(8,128)} %param.5) | copy-start | bytes 12292
  7.0 29.4 %collective-permute-start = (f32[4,25,8,2]{3,2,1,0:T(8,128)S(1)}, f32[4,25,8,2]{3,2,1,0:T(8,128)S(1)}, u32[]{:S(2)}, u32[]{:S(2)}) collective-permute-start(f32[4,25,8,2]{3,2,1,0:T(8,128)S(1)} %get-tuple-element.25), channel_id=1, source_target_pairs={{0,8},{8,16},{16,24},{24,32},{32,40},{40,48},{48,56},{56,64},{64,7... | collective-permute-start | bytes 19208 | tf_op jit(solution)/shard_map/ppermute | solution.py:25
  21.1 33.3 %collective-permute-start.1 = (f32[4,25,8,2]{3,2,1,0:T(8,128)S(1)}, f32[4,25,8,2]{3,2,1,0:T(8,128)S(1)}, u32[]{:S(2)}, u32[]{:S(2)}) collective-permute-start(f32[4,25,8,2]{3,2,1,0:T(8,128)S(1)} %get-tuple-element.26), channel_id=1, source_target_pairs={{8,0},{16,8},{24,16},{32,24},{40,32},{48,40},{56,48},{64,56},{72,6... | collective-permute-start | bytes 19208 | tf_op jit(solution)/shard_map/ppermute | solution.py:26
  55.0 0.7 copy-start.3
  56.0 0.7 copy-start.1
  57.8 21.6 %collective-permute-start.4 = (f32[4,25,8,2]{3,2,1,0:T(8,128)S(1)}, f32[4,25,8,2]{3,2,1,0:T(8,128)S(1)}, u32[]{:S(2)}, u32[]{:S(2)}) collective-permute-start(f32[4,25,8,2]{3,2,1,0:T(8,128)S(1)} %get-tuple-element.21), channel_id=1, source_target_pairs={{0,8},{8,16},{16,24},{24,32},{32,40},{40,48},{48,56},{56,64},{64,7... | collective-permute-start | bytes 19208 | tf_op jit(solution)/shard_map/ppermute | solution.py:25
  59.7 34.4 %collective-permute-start.5 = (f32[4,25,8,2]{3,2,1,0:T(8,128)S(1)}, f32[4,25,8,2]{3,2,1,0:T(8,128)S(1)}, u32[]{:S(2)}, u32[]{:S(2)}) collective-permute-start(f32[4,25,8,2]{3,2,1,0:T(8,128)S(1)} %get-tuple-element.22), channel_id=1, source_target_pairs={{8,0},{16,8},{24,16},{32,24},{40,32},{48,40},{56,48},{64,56},{72,6... | collective-permute-start | bytes 19208 | tf_op jit(solution)/shard_map/ppermute | solution.py:26
  62.2 32.5 %collective-permute-start.7 = (f32[4,25,2,128]{3,2,1,0:T(2,128)S(1)}, f32[4,25,2,128]{3,2,1,0:T(2,128)S(1)}, u32[]{:S(2)}, u32[]{:S(2)}) collective-permute-start(f32[4,25,2,128]{3,2,1,0:T(2,128)S(1)} %get-tuple-element.23), channel_id=1, source_target_pairs={{1,2},{3,4},{5,6},{2,1},{4,3},{6,5},{9,10},{11,12},{13,14},{10,9},... | collective-permute-start | bytes 307208 | tf_op jit(solution)/shard_map/ppermute | solution.py:41
  64.1 31.0 %collective-permute-start.6 = (f32[4,25,2,128]{3,2,1,0:T(2,128)S(1)}, f32[4,25,2,128]{3,2,1,0:T(2,128)S(1)}, u32[]{:S(2)}, u32[]{:S(2)}) collective-permute-start(f32[4,25,2,128]{3,2,1,0:T(2,128)S(1)} %get-tuple-element.24), channel_id=1, source_target_pairs={{0,1},{1,0},{2,3},{3,2},{4,5},{5,4},{6,7},{7,6},{8,9},{9,8},{10,11... | collective-permute-start | bytes 307208 | tf_op jit(solution)/shard_map/ppermute | solution.py:31

commit v3 on v2

v3 whole, which is shorter than its diff:
```python
import jax
import jax.numpy as jnp
from jax import lax
from jax.sharding import PartitionSpec as P

TIME_INCREMENT = 0.1
SCALAR_MIXING = 0.4
VISCOSITY = 0.4
THERMAL = 0.2
HALINE = 0.8
GRAVITY = 0.1
MARGIN = 2
WIDE = 2 * MARGIN


def coriolis(row_index, total):
    mirrored = jnp.where(row_index >= total, 2 * total - 1 - row_index, row_index)
    return (1.2 * jnp.sin(-1.3 + 2.8 * (mirrored.astype(jnp.float32) + 0.5) / total))[:, None]


def send(block, axes, pairs):
    moved = lax.ppermute(block.reshape(-1), axes, pairs)
    return moved.reshape(block.shape)


def gather_wide(x, signs):
    n_lon = lax.axis_size("lon")
    n_lat = lax.axis_size("lat")
    east_ward = [(i, (i + 1) % n_lon) for i in range(n_lon)]
    west_ward = [(j, i) for i, j in east_ward]
    west = send(x[..., -WIDE:], "lon", east_ward)
    east = send(x[..., :WIDE], "lon", west_ward)
    lon_wide = jnp.concatenate([west, x, east], axis=2)

    lat = lax.axis_index("lat")
    odd = lat % 2 == 1
    top_rows = lon_wide[:, -WIDE:, :]
    bottom_rows = lon_wide[:, :WIDE, :]
    to_odd = send(
        jnp.where(odd, bottom_rows, top_rows),
        ("lon", "lat"),
        [(l * n_lat + i, l * n_lat + (i ^ 1)) for l in range(n_lon) for i in range(n_lat)],
    )
    inner = [(i, i + 1) for i in range(1, n_lat - 1, 2)]
    inner = inner + [(j, i) for i, j in inner]
    top = n_lat - 1
    pairs = [(l * n_lat + i, l * n_lat + j) for l in range(n_lon) for i, j in inner]
    pairs = pairs + [(l * n_lat + top, (n_lon - 1 - l) * n_lat + top) for l in range(n_lon)]
    to_even = send(jnp.where(odd, top_rows, bottom_rows), ("lon", "lat"), pairs)
    folded = jnp.flip(to_even, axis=(1, 2)) * signs
    north = jnp.where(odd, jnp.where(lat == top, folded, to_even), to_odd)
    south = jnp.where(odd, to_odd, to_even)
    return jnp.concatenate([south, lon_wide, north], axis=1)


def advance(f, wet, cor):
    rows_n = f.shape[2] - 2 * MARGIN
    cols_n = f.shape[3] - 2 * MARGIN

    def at(g, dr, dc):
        return g[..., MARGIN + dr : MARGIN + dr + rows_n, MARGIN + dc : MARGIN + dc + cols_n]

    def dx(g):
        return (8.0 * (at(g, 0, 1) - at(g, 0, -1)) - (at(g, 0, 2) - at(g, 0, -2))) / 12.0

    def dy(g):
        return (8.0 * (at(g, 1, 0) - at(g, -1, 0)) - (at(g, 2, 0) - at(g, -2, 0))) / 12.0

    def lap(g):
        return at(g, 0, 1) + at(g, 0, -1) + at(g, 1, 0) + at(g, -1, 0) - 4.0 * at(g, 0, 0)

    pressure = GRAVITY * jnp.cumsum(HALINE * f[1] - THERMAL * f[0], axis=0)
    east_v, north_v = at(f[2], 0, 0), at(f[3], 0, 0)

    def adv(g):
        return east_v * dx(g) + north_v * dy(g)

    heat = wet * (at(f[0], 0, 0) + TIME_INCREMENT * (SCALAR_MIXING * lap(f[0]) - adv(f[0])))
    salt = wet * (at(f[1], 0, 0) + TIME_INCREMENT * (SCALAR_MIXING * lap(f[1]) - adv(f[1])))
    u = wet * (
        east_v
        + TIME_INCREMENT * (cor * north_v - dx(pressure) - adv(f[2]) + VISCOSITY * lap(f[2]))
    )
    v = wet * (
        north_v
        + TIME_INCREMENT * (-cor * east_v - dy(pressure) - adv(f[3]) + VISCOSITY * lap(f[3]))
    )
    return jnp.stack([heat, salt, u, v])


def shards(state, sea_mask, levels):
    n_fields, level_count, tile_rows, tile_cols = state.shape
    depth_index = jnp.arange(level_count, dtype=jnp.int32)[:, None, None]
    depth = jnp.where(sea_mask == 1, levels, 0).astype(jnp.float32)
    channels = jnp.concatenate([state.reshape(n_fields * level_count, tile_rows, tile_cols), depth[None]])
    signs = jnp.array([1.0, 1.0, -1.0, -1.0], dtype=jnp.float32)
    signs = jnp.concatenate([jnp.repeat(signs, level_count), jnp.ones((1,), jnp.float32)])
    wide = gather_wide(channels, signs[:, None, None])

    lat = lax.axis_index("lat")
    total = lax.axis_size("lat") * tile_rows
    first_row = lat * tile_rows

    grown = wide[:, MARGIN:-MARGIN, MARGIN:-MARGIN]
    grown_depth = grown[-1]
    grown_wet = (depth_index < grown_depth[None]).astype(jnp.float32)
    grown_rows = first_row - MARGIN + jnp.arange(tile_rows + 2 * MARGIN, dtype=jnp.int32)
    fields = wide[:-1].reshape(n_fields, level_count, *wide.shape[1:])
    once = advance(fields, grown_wet, coriolis(grown_rows, total))
    south_edge = (lat == 0) & (grown_rows < 0)
    once = jnp.where(south_edge[:, None], 0.0, once)

    wet = (depth_index < depth[None]).astype(jnp.float32)
    own_rows = first_row + jnp.arange(tile_rows, dtype=jnp.int32)
    return advance(once, wet, coriolis(own_rows, total))


def solution(mesh):
    return jax.shard_map(
        shards,
        mesh=mesh,
        in_specs=(P(None, None, "lat", "lon"), P("lat", "lon"), P("lat", "lon")),
        out_specs=P(None, None, "lat", "lon"),
        check_vma=False,
    )
```

time: 97.5 us -> 71.5 us (0.73)
  the two profiles are of different devices: /device:TPU:59 before, /device:TPU:224 now
where the time goes in v3:
time: 71.5 us; the launch traced here: 71.3 us
  waiting for transfers between devices  33.8 us (47%)
  starting transfers between devices  19.3 us (27%)
  other arithmetic  13.1 us (18%)
  local copies, waits for them, and re-layouts  4.77 us (7%)
    ppermute x4, waiting for transfers between devices, send(): moved = lax.ppermute(block.reshape(-1), axes, pairs)  33.8 us
    ppermute x4, starting transfers between devices, send(): moved = lax.ppermute(block.reshape(-1), axes, pairs)  19.3 us
    another operation x9, other arithmetic, advance(): return jnp.stack([heat, salt, u, v])  8.43 us
    reshape x4, local copies, waits for them, and re-layouts, send(): return moved.reshape(block.shape)  2.17 us
  transfers between devices with their start and end apart: 4, of which 2 were waited for; matrix products, arithmetic and copies ran while one was open for 4% of the time, Pallas kernels for 0%

profile of v3, /device:TPU:224, one launch (start us, length us, event | category | flops | bytes accessed | tf_op | source)
XLA Modules:
  0.0 71.3 jit_solution(4942406753163115203)
XLA Ops:
  0.0 0.8 %select_convert_fusion = f32[8,128]{1,0:T(8,128)S(1)} fusion(s32[8,128]{1,0:T(8,128)} %param.6, s32[8,128]{1,0:T(8,128)} %param.5), kind=kLoop, calls=%fused_computation.175 | loop fusion | flops 3072 | bytes 12288 | tf_op jit(solution)/shard_map/convert_element_type | solution.py:94
  0.8 1.3 %slice_maximum_fusion = (f32[101,8,4]{2,1,0:T(8,128)S(1)}, f32[101,8,4]{2,1,0:T(8,128)S(1)}) fusion(f32[1,8,128]{2,1,0:T(8,128)S(1)} %bitcast.44, f32[100,8,128]{2,1,0:T(8,128)} %bitcast.35), kind=kLoop, calls=%fused_computation.10 | loop fusion | flops 6464 | bytes 439552 | tf_op jit(solution)/shard_map/concatenate | solution.py:95
  2.3 12.3 %collective-permute-start.1 = (f32[3232]{0:T(1024)S(1)}, f32[3232]{0:T(1024)S(1)}, u32[]{:S(2)}, u32[]{:S(2)}) collective-permute-start(f32[3232]{0:T(1024)S(1)} %reshape.85), channel_id=1, source_target_pairs={{8,0},{16,8},{24,16},{32,24},{40,32},{48,40},{56,48},{64,56},{72,6... | collective-permute-start | bytes 38792 | tf_op jit(solution)/shard_map/ppermute | solution.py:22
  14.8 1.9 %collective-permute-start = (f32[3232]{0:T(1024)S(1)}, f32[3232]{0:T(1024)S(1)}, u32[]{:S(2)}, u32[]{:S(2)}) collective-permute-start(f32[3232]{0:T(1024)S(1)} %reshape.83), channel_id=1, source_target_pairs={{0,8},{8,16},{16,24},{24,32},{32,40},{40,48},{48,56},{56,64},{64,7... | collective-permute-start | bytes 38792 | tf_op jit(solution)/shard_map/ppermute | solution.py:22
  17.0 15.8 %collective-permute-done = f32[3232]{0:T(1024)S(1)} collective-permute-done((f32[3232]{0:T(1024)S(1)}, f32[3232]{0:T(1024)S(1)}, u32[]{:S(2)}, u32[]{:S(2)}) %collective-permute-start) | collective-permute-done | bytes 12960 | tf_op jit(solution)/shard_map/ppermute | solution.py:22
  32.8 0.4 reshape.84
  33.3 0.4 reshape.86
  34.3 0.5 reshape.89
  34.8 0.5 reshape.87
  35.2 3.0 %collective-permute-start.2 = (f32[54944]{0:T(1024)S(1)}, f32[54944]{0:T(1024)S(1)}, u32[]{:S(2)}, u32[]{:S(2)}) collective-permute-start(f32[54944]{0:T(1024)S(1)} %reshape.87), channel_id=1, source_target_pairs={{0,1},{1,0},{2,3},{3,2},{4,5},{5,4},{6,7},{7,6},{8,9},{9,8},{10,11... | collective-permute-start | bytes 659336 | tf_op jit(solution)/shard_map/ppermute | solution.py:22
  38.2 2.1 %collective-permute-start.3 = (f32[54944]{0:T(1024)S(1)}, f32[54944]{0:T(1024)S(1)}, u32[]{:S(2)}, u32[]{:S(2)}) collective-permute-start(f32[54944]{0:T(1024)S(1)} %reshape.89), channel_id=1, source_target_pairs={{1,2},{3,4},{5,6},{2,1},{4,3},{6,5},{9,10},{11,12},{13,14},{10,9},... | collective-permute-start | bytes 659336 | tf_op jit(solution)/shard_map/ppermute | solution.py:22
  40.5 18.0 %collective-permute-done.3 = f32[54944]{0:T(1024)S(1)} collective-permute-done((f32[54944]{0:T(1024)S(1)}, f32[54944]{0:T(1024)S(1)}, u32[]{:S(2)}, u32[]{:S(2)}) %collective-permute-start.3) | collective-permute-done | bytes 219808 | tf_op jit(solution)/shard_map/ppermute | solution.py:22
  58.4 0.7 reshape.90
  59.1 0.9 %reverse = f32[101,4,256]{2,1,0:T(4,128)S(1)} reverse(f32[101,4,256]{2,1,0:T(4,128)S(1)} %bitcast.43), dimensions={1,2} | reverse | bytes 827392
  60.0 0.7 reshape.88
  60.7 0.4 select_select_fusion
  61.2 0.8 %pad_maximum_fusion = f32[101,16,136]{2,1,0:T(8,128)S(1)} fusion(f32[101,4,136]{2,1,0:T(4,128)S(1)} %get-tuple-element.9, f32[101,8,4]{2,1,0:T(8,128)S(1)} %reshape.86, f32[1,8,128]{2,1,0:T(8,128)S(1)} %bitcast.47, f32[100,8,128]{2,1,0:T(8,128)S(1)} %bitcast.38, f32[101,8,4]{2,1,0:T(8,128)S(1)} %reshape.84, f32[101,4,136]{2,1,0:T(4,128)S(1)} %get-tuple-element.10), kind=kLoop, calls=%fused_computation | loop fusion | flops 1098880 | bytes 1758208 | tf_op jit(solution)/shard_map/concatenate | solution.py:53
  62.2 1.4 %fusion.1 = f32[1,25,12,132]{3,2,1,0:T(8,128)S(1)} fusion(f32[101,4,136]{2,1,0:T(4,128)S(1)} %get-tuple-element.10, f32[101,8,4]{2,1,0:T(8,128)S(1)} %reshape.86, f32[101,8,4]{2,1,0:T(8,128)S(1)} %reshape.84, f32[1,8,128]{2,1,0:T(8,128)S(1)} %bitcast.48, f32[100,8,128]{2,1,0:T(8,128)S(1)} %bitcast.39, f32[101,4,136]{2,1,0:T(4,128)S(1)} %get-tuple-element.9, ...), kind=kLoop, calls=%fused_computation.13 | loop fusion | flops 1267200 | bytes 2469540 | tf_op jit(solution)/shard_map/stack | solution.py:88
  63.6 1.4 %fusion = f32[1,25,12,132]{3,2,1,0:T(8,128)S(1)} fusion(f32[101,4,136]{2,1,0:T(4,128)S(1)} %get-tuple-element.10, f32[101,8,4]{2,1,0:T(8,128)S(1)} %reshape.86, f32[101,8,4]{2,1,0:T(8,128)S(1)} %reshape.84, f32[1,8,128]{2,1,0:T(8,128)S(1)} %bitcast.49, f32[100,8,128]{2,1,0:T(8,128)S(1)} %bitcast.40, f32[101,4,136]{2,1,0:T(4,128)S(1)} %get-tuple-element.9, ...), kind=kLoop, calls=%fused_computation.12 | loop fusion | flops 1267200 | bytes 2469540 | tf_op jit(solution)/shard_map/stack | solution.py:88
  65.0 1.6 %fusion.2 = f32[1,25,12,132]{3,2,1,0:T(8,128)S(1)} fusion(f32[101,4,136]{2,1,0:T(4,128)S(1)} %get-tuple-element.10, f32[101,8,4]{2,1,0:T(8,128)S(1)} %reshape.86, f32[101,8,4]{2,1,0:T(8,128)S(1)} %reshape.84, f32[1,8,128]{2,1,0:T(8,128)S(1)} %bitcast.50, f32[100,8,128]{2,1,0:T(8,128)S(1)} %bitcast.41, f32[101,4,136]{2,1,0:T(4,128)S(1)} %get-tuple-element.9, ...), kind=kLoop, calls=%fused_computation.14 | loop fusion | flops 1584000 | bytes 2944788 | tf_op jit(solution)/shard_map/stack | solution.py:88
  66.6 1.7 %fusion.3 = f32[1,25,12,132]{3,2,1,0:T(8,128)S(1)} fusion(f32[101,4,136]{2,1,0:T(4,128)S(1)} %get-tuple-element.10, f32[101,8,4]{2,1,0:T(8,128)S(1)} %reshape.86, f32[101,8,4]{2,1,0:T(8,128)S(1)} %reshape.84, f32[1,8,128]{2,1,0:T(8,128)S(1)} %bitcast.51, f32[100,8,128]{2,1,0:T(8,128)S(1)} %bitcast.42, f32[101,4,136]{2,1,0:T(4,128)S(1)} %get-tuple-element.9, ...), kind=kLoop, calls=%fused_computation.15 | loop fusion | flops 1584000 | bytes 2944788 | tf_op jit(solution)/shard_map/stack | solution.py:88
  69.2 0.4 fusion.66
  69.7 0.4 fusion.67
  70.5 0.8 %pad_maximum_fusion.11 = f32[4,25,8,128]{3,2,1,0:T(8,128)} fusion(f32[1,25,8,128]{3,2,1,0:T(8,128)S(1)} %fusion.67, f32[1,25,8,128]{3,2,1,0:T(8,128)S(1)} %fusion.66, f32[1,25,8,128]{3,2,1,0:T(8,128)S(1)} %fusion.65, f32[1,25,8,128]{3,2,1,0:T(8,128)S(1)} %fusion.64), kind=kLoop, calls=%fused_computation.93 | loop fusion | flops 307200 | bytes 819200 | tf_op jit(solution)/shard_map/stack | solution.py:88
  (24 shorter events, 2.9 us)
Async XLA Ops:
  0.0 16.9 %copy-start.1 = (f32[4]{0:T(128)S(1)}, f32[4]{0:T(128)}, u32[]{:S(2)}) copy-start(f32[4]{0:T(128)} %constant.115.clone) | copy-start | bytes 52
  0.0 33.7 %copy-start = (f32[4,25,8,128]{3,2,1,0:T(8,128)S(1)}, f32[4,25,8,128]{3,2,1,0:T(8,128)}, u32[]{:S(2)}) copy-start(f32[4,25,8,128]{3,2,1,0:T(8,128)} %param.4) | copy-start | bytes 1228804
  2.3 31.0 %collective-permute-start.1 = (f32[3232]{0:T(1024)S(1)}, f32[3232]{0:T(1024)S(1)}, u32[]{:S(2)}, u32[]{:S(2)}) collective-permute-start(f32[3232]{0:T(1024)S(1)} %reshape.85), channel_id=1, source_target_pairs={{8,0},{16,8},{24,16},{32,24},{40,32},{48,40},{56,48},{64,56},{72,6... | collective-permute-start | bytes 38792 | tf_op jit(solution)/shard_map/ppermute | solution.py:22
  14.8 18.0 %collective-permute-start = (f32[3232]{0:T(1024)S(1)}, f32[3232]{0:T(1024)S(1)}, u32[]{:S(2)}, u32[]{:S(2)}) collective-permute-start(f32[3232]{0:T(1024)S(1)} %reshape.83), channel_id=1, source_target_pairs={{0,8},{8,16},{16,24},{24,32},{32,40},{40,48},{48,56},{56,64},{64,7... | collective-permute-start | bytes 38792 | tf_op jit(solution)/shard_map/ppermute | solution.py:22
  35.2 24.8 %collective-permute-start.2 = (f32[54944]{0:T(1024)S(1)}, f32[54944]{0:T(1024)S(1)}, u32[]{:S(2)}, u32[]{:S(2)}) collective-permute-start(f32[54944]{0:T(1024)S(1)} %reshape.87), channel_id=1, source_target_pairs={{0,1},{1,0},{2,3},{3,2},{4,5},{5,4},{6,7},{7,6},{8,9},{9,8},{10,11... | collective-permute-start | bytes 659336 | tf_op jit(solution)/shard_map/ppermute | solution.py:22
  38.2 20.2 %collective-permute-start.3 = (f32[54944]{0:T(1024)S(1)}, f32[54944]{0:T(1024)S(1)}, u32[]{:S(2)}, u32[]{:S(2)}) collective-permute-start(f32[54944]{0:T(1024)S(1)} %reshape.89), channel_id=1, source_target_pairs={{1,2},{3,4},{5,6},{2,1},{4,3},{6,5},{9,10},{11,12},{13,14},{10,9},... | collective-permute-start | bytes 659336 | tf_op jit(solution)/shard_map/ppermute | solution.py:22

commit v4 on v3

--- a/solution.py
+++ b/solution.py
@@ -26,10 +26,18 @@
 def gather_wide(x, signs):
     n_lon = lax.axis_size("lon")
     n_lat = lax.axis_size("lat")
-    east_ward = [(i, (i + 1) % n_lon) for i in range(n_lon)]
-    west_ward = [(j, i) for i, j in east_ward]
-    west = send(x[..., -WIDE:], "lon", east_ward)
-    east = send(x[..., :WIDE], "lon", west_ward)
+    lon = lax.axis_index("lon")
+    lon_odd = lon % 2 == 1
+    east_cols = x[..., -WIDE:]
+    west_cols = x[..., :WIDE]
+    on_chip = send(
+        jnp.where(lon_odd, west_cols, east_cols), "lon", [(m, m ^ 1) for m in range(n_lon)]
+    )
+    across = [(m, (m + 1) % n_lon) for m in range(1, n_lon, 2)]
+    across = across + [(j, i) for i, j in across]
+    off_chip = send(jnp.where(lon_odd, east_cols, west_cols), "lon", across)
+    west = jnp.where(lon_odd, on_chip, off_chip)
+    east = jnp.where(lon_odd, off_chip, on_chip)
     lon_wide = jnp.concatenate([west, x, east], axis=2)
 
     lat = lax.axis_index("lat")

time: 71.5 us -> 59.3 us (0.83)
  waiting for transfers between devices: 33.8 us -> 11.2 us
  starting transfers between devices: 19.3 us -> 29.5 us
    ppermute x4, waiting for transfers between devices: 33.8 us -> 11.2 us  [send(): moved = lax.ppermute(block.reshape(-1), axes, pairs)]
    ppermute x4, starting transfers between devices: 19.3 us -> 29.5 us  [send(): moved = lax.ppermute(block.reshape(-1), axes, pairs)]
    select_n x0 -> x2, other arithmetic: none -> 1.55 us  [the longest x1 1.54 us: gather_wide(): jnp.where(lon_odd, west_cols, east_cols)]
    concatenate x1 -> x0, other arithmetic: 1.3 us -> none  [shards(): jnp.concatenate([state.reshape(n_fields * level_count, tile_rows, tile_co...]
    select_n x0 -> x2, local copies, waits for them, and re-layouts: none -> 0.85 us  [the longest x1 0.43 us: gather_wide(): east = jnp.where(lon_odd, off_chip, on_chip)]
    reshape x4 -> x2, local copies, waits for them, and re-layouts: 2.17 us -> 1.33 us  [send(): return moved.reshape(block.shape)]
where the time goes in v4:
time: 59.3 us; the launch traced here: 59.1 us
  starting transfers between devices  29.5 us (50%)
  other arithmetic  13.4 us (23%)
  waiting for transfers between devices  11.2 us (19%)
  local copies, waits for them, and re-layouts  4.78 us (8%)
    ppermute x4, starting transfers between devices, send(): moved = lax.ppermute(block.reshape(-1), axes, pairs)  29.5 us
    ppermute x4, waiting for transfers between devices, send(): moved = lax.ppermute(block.reshape(-1), axes, pairs)  11.2 us
    another operation x9, other arithmetic, advance(): return jnp.stack([heat, salt, u, v])  8.43 us
    select_n x1, other arithmetic, gather_wide(): jnp.where(lon_odd, west_cols, east_cols)  1.54 us
    reshape x4, local copies, waits for them, and re-layouts, send(): moved = lax.ppermute(block.reshape(-1), axes, pairs)  1.42 us
    reshape x2, local copies, waits for them, and re-layouts, send(): return moved.reshape(block.shape)  1.33 us
  transfers between devices with their start and end apart: 4, of which 2 were waited for; matrix products, arithmetic and copies ran while one was open for 4% of the time, Pallas kernels for 0%

profile of v4, /device:TPU:224, one launch (start us, length us, event | category | flops | bytes accessed | tf_op | source)
XLA Modules:
  0.0 59.1 jit_solution(286338338789730922)
XLA Ops:
  0.0 0.8 %select_convert_fusion = f32[8,128]{1,0:T(8,128)S(1)} fusion(s32[8,128]{1,0:T(8,128)} %param.6, s32[8,128]{1,0:T(8,128)} %param.5), kind=kLoop, calls=%fused_computation.179 | loop fusion | flops 3072 | bytes 12288 | tf_op jit(solution)/shard_map/convert_element_type | solution.py:102
  0.8 1.5 %fusion.60 = (f32[101,8,4]{2,1,0:T(8,128)S(1)}, f32[101,8,4]{2,1,0:T(8,128)S(1)}) fusion(f32[1,8,128]{2,1,0:T(8,128)S(1)} %bitcast.44, f32[100,8,128]{2,1,0:T(8,128)} %bitcast.35, pred[]{:T(512)S(6)} %eq.25), kind=kLoop, calls=%fused_computation.99 | loop fusion | flops 16160 | bytes 439553 | tf_op jit(solution)/shard_map/jit(_where)/select_n | solution.py:34
  2.5 12.3 %collective-permute-start.1 = (f32[3232]{0:T(1024)S(1)}, f32[3232]{0:T(1024)S(1)}, u32[]{:S(2)}, u32[]{:S(2)}) collective-permute-start(f32[3232]{0:T(1024)S(1)} %reshape.84), channel_id=1, source_target_pairs={{8,16},{24,32},{40,48},{56,64},{72,80},{88,96},{104,112},{120,128}... | collective-permute-start | bytes 38792 | tf_op jit(solution)/shard_map/ppermute | solution.py:22
  15.1 1.9 %collective-permute-start = (f32[3232]{0:T(1024)S(1)}, f32[3232]{0:T(1024)S(1)}, u32[]{:S(2)}, u32[]{:S(2)}) collective-permute-start(f32[3232]{0:T(1024)S(1)} %reshape.83), channel_id=1, source_target_pairs={{0,8},{8,0},{16,24},{24,16},{32,40},{40,32},{48,56},{56,48},{64,72... | collective-permute-start | bytes 38792 | tf_op jit(solution)/shard_map/ppermute | solution.py:22
  17.3 3.3 %collective-permute-done.1 = f32[3232]{0:T(1024)S(1)} collective-permute-done((f32[3232]{0:T(1024)S(1)}, f32[3232]{0:T(1024)S(1)}, u32[]{:S(2)}, u32[]{:S(2)}) %collective-permute-start.1) | collective-permute-done | bytes 12960 | tf_op jit(solution)/shard_map/ppermute | solution.py:22
  20.5 0.4 select_n.106
  21.0 0.4 select_n.108
  22.0 0.5 reshape.87
  22.4 0.5 reshape.85
  22.9 2.0 %collective-permute-start.2 = (f32[54944]{0:T(1024)S(1)}, f32[54944]{0:T(1024)S(1)}, u32[]{:S(2)}, u32[]{:S(2)}) collective-permute-start(f32[54944]{0:T(1024)S(1)} %reshape.85), channel_id=1, source_target_pairs={{0,1},{1,0},{2,3},{3,2},{4,5},{5,4},{6,7},{7,6},{8,9},{9,8},{10,11... | collective-permute-start | bytes 659336 | tf_op jit(solution)/shard_map/ppermute | solution.py:22
  25.0 13.2 %collective-permute-start.3 = (f32[54944]{0:T(1024)S(1)}, f32[54944]{0:T(1024)S(1)}, u32[]{:S(2)}, u32[]{:S(2)}) collective-permute-start(f32[54944]{0:T(1024)S(1)} %reshape.87), channel_id=1, source_target_pairs={{1,2},{3,4},{5,6},{2,1},{4,3},{6,5},{9,10},{11,12},{13,14},{10,9},... | collective-permute-start | bytes 659336 | tf_op jit(solution)/shard_map/ppermute | solution.py:22
  38.3 7.9 %collective-permute-done.3 = f32[54944]{0:T(1024)S(1)} collective-permute-done((f32[54944]{0:T(1024)S(1)}, f32[54944]{0:T(1024)S(1)}, u32[]{:S(2)}, u32[]{:S(2)}) %collective-permute-start.3) | collective-permute-done | bytes 219808 | tf_op jit(solution)/shard_map/ppermute | solution.py:22
  46.3 0.7 %reshape.88 = f32[101,4,136]{2,1,0:T(4,128)S(1)} reshape(f32[54944]{0:T(1024)S(1)} %collective-permute-done.3) | data formatting | bytes 439552 | tf_op jit(solution)/shard_map/reshape | solution.py:23
  46.9 0.9 %reverse = f32[101,4,256]{2,1,0:T(4,128)S(1)} reverse(f32[101,4,256]{2,1,0:T(4,128)S(1)} %bitcast.43), dimensions={1,2} | reverse | bytes 827392
  47.8 0.7 %reshape.86 = f32[101,4,136]{2,1,0:T(4,128)S(1)} reshape(f32[54944]{0:T(1024)S(1)} %collective-permute-done.2) | data formatting | bytes 439552 | tf_op jit(solution)/shard_map/reshape | solution.py:23
  48.5 0.4 select_select_fusion
  49.1 0.8 %pad_maximum_fusion = f32[101,16,136]{2,1,0:T(8,128)S(1)} fusion(f32[101,4,136]{2,1,0:T(4,128)S(1)} %get-tuple-element.9, f32[101,8,4]{2,1,0:T(8,128)S(1)} %select_n.108, f32[1,8,128]{2,1,0:T(8,128)S(1)} %bitcast.47, f32[100,8,128]{2,1,0:T(8,128)S(1)} %bitcast.38, f32[101,8,4]{2,1,0:T(8,128)S(1)} %select_n.106, f32[101,4,136]{2,1,0:T(4,128)S(1)} %get-tuple-element.10), kind=kLoop, calls=%fused_computation | loop fusion | flops 1098880 | bytes 1758208 | tf_op jit(solution)/shard_map/concatenate | solution.py:61
  50.0 1.4 %fusion.1 = f32[1,25,12,132]{3,2,1,0:T(8,128)S(1)} fusion(f32[101,4,136]{2,1,0:T(4,128)S(1)} %get-tuple-element.10, f32[101,8,4]{2,1,0:T(8,128)S(1)} %select_n.108, f32[101,8,4]{2,1,0:T(8,128)S(1)} %select_n.106, f32[1,8,128]{2,1,0:T(8,128)S(1)} %bitcast.48, f32[100,8,128]{2,1,0:T(8,128)S(1)} %bitcast.39, f32[101,4,136]{2,1,0:T(4,128)S(1)} %get-tuple-element.9, ...), kind=kLoop, calls=%fused_computation.13 | loop fusion | flops 1267200 | bytes 2469540 | tf_op jit(solution)/shard_map/stack | solution.py:96
  51.4 1.4 %fusion = f32[1,25,12,132]{3,2,1,0:T(8,128)S(1)} fusion(f32[101,4,136]{2,1,0:T(4,128)S(1)} %get-tuple-element.10, f32[101,8,4]{2,1,0:T(8,128)S(1)} %select_n.108, f32[101,8,4]{2,1,0:T(8,128)S(1)} %select_n.106, f32[1,8,128]{2,1,0:T(8,128)S(1)} %bitcast.49, f32[100,8,128]{2,1,0:T(8,128)S(1)} %bitcast.40, f32[101,4,136]{2,1,0:T(4,128)S(1)} %get-tuple-element.9, ...), kind=kLoop, calls=%fused_computation.12 | loop fusion | flops 1267200 | bytes 2469540 | tf_op jit(solution)/shard_map/stack | solution.py:96
  52.8 1.6 %fusion.2 = f32[1,25,12,132]{3,2,1,0:T(8,128)S(1)} fusion(f32[101,4,136]{2,1,0:T(4,128)S(1)} %get-tuple-element.10, f32[101,8,4]{2,1,0:T(8,128)S(1)} %select_n.108, f32[101,8,4]{2,1,0:T(8,128)S(1)} %select_n.106, f32[1,8,128]{2,1,0:T(8,128)S(1)} %bitcast.50, f32[100,8,128]{2,1,0:T(8,128)S(1)} %bitcast.41, f32[101,4,136]{2,1,0:T(4,128)S(1)} %get-tuple-element.9, ...), kind=kLoop, calls=%fused_computation.14 | loop fusion | flops 1584000 | bytes 2944788 | tf_op jit(solution)/shard_map/stack | solution.py:96
  54.4 1.7 %fusion.3 = f32[1,25,12,132]{3,2,1,0:T(8,128)S(1)} fusion(f32[101,4,136]{2,1,0:T(4,128)S(1)} %get-tuple-element.10, f32[101,8,4]{2,1,0:T(8,128)S(1)} %select_n.108, f32[101,8,4]{2,1,0:T(8,128)S(1)} %select_n.106, f32[1,8,128]{2,1,0:T(8,128)S(1)} %bitcast.51, f32[100,8,128]{2,1,0:T(8,128)S(1)} %bitcast.42, f32[101,4,136]{2,1,0:T(4,128)S(1)} %get-tuple-element.9, ...), kind=kLoop, calls=%fused_computation.15 | loop fusion | flops 1584000 | bytes 2944788 | tf_op jit(solution)/shard_map/stack | solution.py:96
  57.1 0.4 fusion.68
  57.5 0.4 fusion.69
  58.3 0.8 %pad_maximum_fusion.11 = f32[4,25,8,128]{3,2,1,0:T(8,128)} fusion(f32[1,25,8,128]{3,2,1,0:T(8,128)S(1)} %fusion.69, f32[1,25,8,128]{3,2,1,0:T(8,128)S(1)} %fusion.68, f32[1,25,8,128]{3,2,1,0:T(8,128)S(1)} %fusion.67, f32[1,25,8,128]{3,2,1,0:T(8,128)S(1)} %fusion.66), kind=kLoop, calls=%fused_computation.93 | loop fusion | flops 307200 | bytes 819200 | tf_op jit(solution)/shard_map/stack | solution.py:96
  (25 shorter events, 2.9 us)
Async XLA Ops:
  0.0 17.1 %copy-start.1 = (f32[4]{0:T(128)S(1)}, f32[4]{0:T(128)}, u32[]{:S(2)}) copy-start(f32[4]{0:T(128)} %constant.124.clone) | copy-start | bytes 52
  0.0 21.4 %copy-start = (f32[4,25,8,128]{3,2,1,0:T(8,128)S(1)}, f32[4,25,8,128]{3,2,1,0:T(8,128)}, u32[]{:S(2)}) copy-start(f32[4,25,8,128]{3,2,1,0:T(8,128)} %param.4) | copy-start | bytes 1228804
  2.5 18.0 %collective-permute-start.1 = (f32[3232]{0:T(1024)S(1)}, f32[3232]{0:T(1024)S(1)}, u32[]{:S(2)}, u32[]{:S(2)}) collective-permute-start(f32[3232]{0:T(1024)S(1)} %reshape.84), channel_id=1, source_target_pairs={{8,16},{24,32},{40,48},{56,64},{72,80},{88,96},{104,112},{120,128}... | collective-permute-start | bytes 38792 | tf_op jit(solution)/shard_map/ppermute | solution.py:22
  15.1 5.4 %collective-permute-start = (f32[3232]{0:T(1024)S(1)}, f32[3232]{0:T(1024)S(1)}, u32[]{:S(2)}, u32[]{:S(2)}) collective-permute-start(f32[3232]{0:T(1024)S(1)} %reshape.83), channel_id=1, source_target_pairs={{0,8},{8,0},{16,24},{24,16},{32,40},{40,32},{48,56},{56,48},{64,72... | collective-permute-start | bytes 38792 | tf_op jit(solution)/shard_map/ppermute | solution.py:22
  22.9 24.9 %collective-permute-start.2 = (f32[54944]{0:T(1024)S(1)}, f32[54944]{0:T(1024)S(1)}, u32[]{:S(2)}, u32[]{:S(2)}) collective-permute-start(f32[54944]{0:T(1024)S(1)} %reshape.85), channel_id=1, source_target_pairs={{0,1},{1,0},{2,3},{3,2},{4,5},{5,4},{6,7},{7,6},{8,9},{9,8},{10,11... | collective-permute-start | bytes 659336 | tf_op jit(solution)/shard_map/ppermute | solution.py:22
  25.0 21.3 %collective-permute-start.3 = (f32[54944]{0:T(1024)S(1)}, f32[54944]{0:T(1024)S(1)}, u32[]{:S(2)}, u32[]{:S(2)}) collective-permute-start(f32[54944]{0:T(1024)S(1)} %reshape.87), channel_id=1, source_target_pairs={{1,2},{3,4},{5,6},{2,1},{4,3},{6,5},{9,10},{11,12},{13,14},{10,9},... | collective-permute-start | bytes 659336 | tf_op jit(solution)/shard_map/ppermute | solution.py:22

commit v5 on v3

--- a/solution.py
+++ b/solution.py
@@ -18,39 +18,44 @@
     return (1.2 * jnp.sin(-1.3 + 2.8 * (mirrored.astype(jnp.float32) + 0.5) / total))[:, None]
 
 
-def send(block, axes, pairs):
-    moved = lax.ppermute(block.reshape(-1), axes, pairs)
-    return moved.reshape(block.shape)
-
-
 def gather_wide(x, signs):
     n_lon = lax.axis_size("lon")
     n_lat = lax.axis_size("lat")
-    east_ward = [(i, (i + 1) % n_lon) for i in range(n_lon)]
-    west_ward = [(j, i) for i, j in east_ward]
-    west = send(x[..., -WIDE:], "lon", east_ward)
-    east = send(x[..., :WIDE], "lon", west_ward)
-    lon_wide = jnp.concatenate([west, x, east], axis=2)
 
     lat = lax.axis_index("lat")
     odd = lat % 2 == 1
-    top_rows = lon_wide[:, -WIDE:, :]
-    bottom_rows = lon_wide[:, :WIDE, :]
-    to_odd = send(
-        jnp.where(odd, bottom_rows, top_rows),
-        ("lon", "lat"),
-        [(l * n_lat + i, l * n_lat + (i ^ 1)) for l in range(n_lon) for i in range(n_lat)],
-    )
+    top_rows = x[:, -WIDE:, :]
+    bottom_rows = x[:, :WIDE, :]
     inner = [(i, i + 1) for i in range(1, n_lat - 1, 2)]
     inner = inner + [(j, i) for i, j in inner]
     top = n_lat - 1
     pairs = [(l * n_lat + i, l * n_lat + j) for l in range(n_lon) for i, j in inner]
     pairs = pairs + [(l * n_lat + top, (n_lon - 1 - l) * n_lat + top) for l in range(n_lon)]
-    to_even = send(jnp.where(odd, top_rows, bottom_rows), ("lon", "lat"), pairs)
+    to_even = lax.ppermute(jnp.where(odd, top_rows, bottom_rows), ("lon", "lat"), pairs)
+    to_odd = lax.ppermute(
+        jnp.where(odd, bottom_rows, top_rows),
+        ("lon", "lat"),
+        [(l * n_lat + i, l * n_lat + (i ^ 1)) for l in range(n_lon) for i in range(n_lat)],
+    )
     folded = jnp.flip(to_even, axis=(1, 2)) * signs
     north = jnp.where(odd, jnp.where(lat == top, folded, to_even), to_odd)
     south = jnp.where(odd, to_odd, to_even)
-    return jnp.concatenate([south, lon_wide, north], axis=1)
+    lat_wide = jnp.concatenate([south, x, north], axis=1)
+
+    lon = lax.axis_index("lon")
+    lon_odd = lon % 2 == 1
+    edge_shape = lat_wide[..., :WIDE].shape
+    east_cols = lat_wide[..., -WIDE:].reshape(-1)
+    west_cols = lat_wide[..., :WIDE].reshape(-1)
+    on_chip = lax.ppermute(
+        jnp.where(lon_odd, west_cols, east_cols), "lon", [(m, m ^ 1) for m in range(n_lon)]
+    )
+    across = [(m, (m + 1) % n_lon) for m in range(1, n_lon, 2)]
+    across = across + [(j, i) for i, j in across]
+    off_chip = lax.ppermute(jnp.where(lon_odd, east_cols, west_cols), "lon", across)
+    west = jnp.where(lon_odd, on_chip, off_chip).reshape(edge_shape)
+    east = jnp.where(lon_odd, off_chip, on_chip).reshape(edge_shape)
+    return jnp.concatenate([west, lat_wide, east], axis=2)
 
 
 def advance(f, wet, cor):

time: 71.5 us -> 59.2 us (0.83)
  the two profiles are of different devices: /device:TPU:224 before, /device:TPU:192 now
where the time goes in v5:
time: 59.2 us; the launch traced here: 58.9 us
  starting transfers between devices  23.3 us (39%)
  waiting for transfers between devices  18.6 us (31%)
  other arithmetic  12.9 us (22%)
  local copies, waits for them, and re-layouts  3.94 us (7%)
    ppermute x1, starting transfers between devices, gather_wide(): lax.ppermute(jnp.where(odd, bottom_rows, top_rows), ('lon', 'lat'), [(l *...  14.1 us
    ppermute x1, waiting for transfers between devices, gather_wide(): lax.ppermute(jnp.where(lon_odd, east_cols, west_cols), 'lon', across)  10.9 us
    another operation x9, other arithmetic, advance(): return jnp.stack([heat, salt, u, v])  8.04 us
    ppermute x1, waiting for transfers between devices, gather_wide(): lax.ppermute(jnp.where(odd, bottom_rows, top_rows), ('lon', 'lat'), [(l *...  7.6 us
    ppermute x1, starting transfers between devices, gather_wide(): lax.ppermute(jnp.where(lon_odd, east_cols, west_cols), 'lon', across)  5.04 us
    ppermute x1, starting transfers between devices, gather_wide(): lax.ppermute(jnp.where(lon_odd, west_cols, east_cols), 'lon', [(m, m ^ 1)...  2.1 us
    ppermute x1, starting transfers between devices, gather_wide(): lax.ppermute(jnp.where(odd, top_rows, bottom_rows), ('lon', 'lat'), pairs)  2.02 us
    select_n x1, other arithmetic, gather_wide(): jnp.where(odd, top_rows, bottom_rows)  1.45 us
  transfers between devices with their start and end apart: 4, of which 2 were waited for; matrix products, arithmetic and copies ran while one was open for 2% of the time, Pallas kernels for 0%

profile of v5, /device:TPU:192, one launch (start us, length us, event | category | flops | bytes accessed | tf_op | source)
XLA Modules:
  0.0 58.9 jit_solution(252303946362686879)
XLA Ops:
  0.0 0.8 %select_convert_fusion = f32[8,128]{1,0:T(8,128)S(1)} fusion(s32[8,128]{1,0:T(8,128)} %param.6, s32[8,128]{1,0:T(8,128)} %param.5), kind=kLoop, calls=%fused_computation.181 | loop fusion | flops 3072 | bytes 12288 | tf_op jit(solution)/shard_map/convert_element_type | solution.py:99
  0.8 1.5 %broadcast_select_fusion.1 = (f32[101,4,128]{2,1,0:T(4,128)S(1)}, f32[101,4,128]{2,1,0:T(4,128)S(1)}) fusion(pred[]{:T(512)S(6)} %eq.25, f32[1,8,128]{2,1,0:T(8,128)S(1)} %bitcast.42, f32[100,8,128]{2,1,0:T(8,128)} %bitcast.34), kind=kLoop, calls=%fused_computation.110 | loop fusion | flops 258560 | bytes 827393 | tf_op jit(solution)/shard_map/jit(_where)/select_n | solution.py:34
  2.2 2.0 %collective-permute-start.1 = (f32[101,4,128]{2,1,0:T(4,128)S(1)}, f32[101,4,128]{2,1,0:T(4,128)S(1)}, u32[]{:S(2)}, u32[]{:S(2)}) collective-permute-start(f32[101,4,128]{2,1,0:T(4,128)S(1)} %get-tuple-element.13), channel_id=1, source_target_pairs={{1,2},{3,4},{5,6},{2,1},{4,3},{6,5},{9,10},{11,12},{13,14},{10,9},... | collective-permute-start | bytes 620552 | tf_op jit(solution)/shard_map/ppermute | solution.py:34
  4.2 14.1 %collective-permute-start = (f32[101,4,128]{2,1,0:T(4,128)S(1)}, f32[101,4,128]{2,1,0:T(4,128)S(1)}, u32[]{:S(2)}, u32[]{:S(2)}) collective-permute-start(f32[101,4,128]{2,1,0:T(4,128)S(1)} %get-tuple-element.14), channel_id=1, source_target_pairs={{0,1},{1,0},{2,3},{3,2},{4,5},{5,4},{6,7},{7,6},{8,9},{9,8},{10,11... | collective-permute-start | bytes 620552 | tf_op jit(solution)/shard_map/ppermute | solution.py:35
  18.5 0.7 %broadcast_in_dim.34 = f32[4,25]{1,0:T(4,128)S(1)} broadcast(f32[4]{0:T(128)} %constant.124.clone), dimensions={0} | broadcast | bytes 416 | tf_op jit(solution)/shard_map/broadcast_in_dim | solution.py:102
  19.4 0.4 rev.4
  19.8 7.6 %collective-permute-done = f32[101,4,128]{2,1,0:T(4,128)S(1)} collective-permute-done((f32[101,4,128]{2,1,0:T(4,128)S(1)}, f32[101,4,128]{2,1,0:T(4,128)S(1)}, u32[]{:S(2)}, u32[]{:S(2)}) %collective-permute-start) | collective-permute-done | bytes 206880 | tf_op jit(solution)/shard_map/ppermute | solution.py:35
  28.1 0.4 select_n.110
  28.5 0.4 select_n.112
  29.0 5.0 %collective-permute-start.3 = (f32[6464]{0:T(1024)S(1)}, f32[6464]{0:T(1024)S(1)}, u32[]{:S(2)}, u32[]{:S(2)}) collective-permute-start(f32[6464]{0:T(1024)S(1)} %select_n.112), channel_id=1, source_target_pairs={{8,16},{24,32},{40,48},{56,64},{72,80},{88,96},{104,112},{120,128}... | collective-permute-start | bytes 77576 | tf_op jit(solution)/shard_map/ppermute | solution.py:55
  34.0 2.1 %collective-permute-start.2 = (f32[6464]{0:T(1024)S(1)}, f32[6464]{0:T(1024)S(1)}, u32[]{:S(2)}, u32[]{:S(2)}) collective-permute-start(f32[6464]{0:T(1024)S(1)} %select_n.110), channel_id=1, source_target_pairs={{0,8},{8,0},{16,24},{24,16},{32,40},{40,32},{48,56},{56,48},{64,72... | collective-permute-start | bytes 77576 | tf_op jit(solution)/shard_map/ppermute | solution.py:50
  36.1 10.9 %collective-permute-done.3 = f32[6464]{0:T(1024)S(1)} collective-permute-done((f32[6464]{0:T(1024)S(1)}, f32[6464]{0:T(1024)S(1)}, u32[]{:S(2)}, u32[]{:S(2)}) %collective-permute-start.3) | collective-permute-done | bytes 25888 | tf_op jit(solution)/shard_map/ppermute | solution.py:55
  47.1 0.8 %reshape.72 = f32[101,16,4]{2,1,0:T(8,128)S(1)} reshape(f32[6464]{0:T(1024)S(1)} %get-tuple-element.15) | data formatting | bytes 51712 | tf_op jit(solution)/shard_map/reshape | solution.py:56
  47.9 0.9 %reshape.73 = f32[101,16,4]{2,1,0:T(8,128)S(1)} reshape(f32[6464]{0:T(1024)S(1)} %get-tuple-element.16) | data formatting | bytes 51712 | tf_op jit(solution)/shard_map/reshape | solution.py:57
  48.9 1.2 %pad_maximum_fusion = f32[101,16,136]{2,1,0:T(8,128)S(1)} fusion(f32[101,16,4]{2,1,0:T(8,128)S(1)} %reshape.73, f32[101,4,128]{2,1,0:T(4,128)S(1)} %get-tuple-element.12, f32[1,8,128]{2,1,0:T(8,128)S(1)} %bitcast.45, f32[100,8,128]{2,1,0:T(8,128)S(1)} %bitcast.37, f32[101,4,128]{2,1,0:T(4,128)S(1)} %get-tuple-element.11, f32[101,16,4]{2,1,0:T(8,128)S(1)} %reshape.72), kind=kLoop, calls=%fused_computation | loop fusion | flops 1098880 | bytes 1758208 | tf_op jit(solution)/shard_map/concatenate | solution.py:58
  50.3 1.3 %fusion = f32[1,25,12,132]{3,2,1,0:T(8,128)S(1)} fusion(f32[101,16,136]{2,1,0:T(8,128)S(1)} %pad_maximum_fusion, f32[101,16,4]{2,1,0:T(8,128)S(1)} %reshape.72, f32[101,4,128]{2,1,0:T(4,128)S(1)} %get-tuple-element.12, f32[101,4,128]{2,1,0:T(4,128)S(1)} %get-tuple-element.11, f32[1,8,128]{2,1,0:T(8,128)S(1)} %bitcast.46, f32[100,8,128]{2,1,0:T(8,128)S(1)} %bitcast.38, ...), kind=kLoop, calls=%fused_computation.13 | loop fusion | flops 1267200 | bytes 2469540 | tf_op jit(solution)/shard_map/stack | solution.py:93
  51.6 1.3 %fusion.1 = f32[1,25,12,132]{3,2,1,0:T(8,128)S(1)} fusion(f32[101,16,136]{2,1,0:T(8,128)S(1)} %pad_maximum_fusion, f32[101,16,4]{2,1,0:T(8,128)S(1)} %reshape.72, f32[101,4,128]{2,1,0:T(4,128)S(1)} %get-tuple-element.12, f32[101,4,128]{2,1,0:T(4,128)S(1)} %get-tuple-element.11, f32[1,8,128]{2,1,0:T(8,128)S(1)} %bitcast.47, f32[100,8,128]{2,1,0:T(8,128)S(1)} %bitcast.39, ...), kind=kLoop, calls=%fused_computation.14 | loop fusion | flops 1267200 | bytes 2469540 | tf_op jit(solution)/shard_map/stack | solution.py:93
  52.9 1.5 %fusion.2 = f32[1,25,12,132]{3,2,1,0:T(8,128)S(1)} fusion(f32[101,16,136]{2,1,0:T(8,128)S(1)} %pad_maximum_fusion, f32[101,16,4]{2,1,0:T(8,128)S(1)} %reshape.72, f32[101,4,128]{2,1,0:T(4,128)S(1)} %get-tuple-element.12, f32[101,4,128]{2,1,0:T(4,128)S(1)} %get-tuple-element.11, f32[1,8,128]{2,1,0:T(8,128)S(1)} %bitcast.48, f32[100,8,128]{2,1,0:T(8,128)S(1)} %bitcast.40, ...), kind=kLoop, calls=%fused_computation.15 | loop fusion | flops 1584000 | bytes 2944788 | tf_op jit(solution)/shard_map/stack | solution.py:93
  54.4 1.6 %fusion.3 = f32[1,25,12,132]{3,2,1,0:T(8,128)S(1)} fusion(f32[101,16,136]{2,1,0:T(8,128)S(1)} %pad_maximum_fusion, f32[101,16,4]{2,1,0:T(8,128)S(1)} %reshape.72, f32[101,4,128]{2,1,0:T(4,128)S(1)} %get-tuple-element.12, f32[101,4,128]{2,1,0:T(4,128)S(1)} %get-tuple-element.11, f32[1,8,128]{2,1,0:T(8,128)S(1)} %bitcast.49, f32[100,8,128]{2,1,0:T(8,128)S(1)} %bitcast.41, ...), kind=kLoop, calls=%fused_computation.16 | loop fusion | flops 1584000 | bytes 2944788 | tf_op jit(solution)/shard_map/stack | solution.py:93
  56.5 0.4 fusion.65
  56.9 0.4 fusion.67
  57.3 0.4 fusion.68
  57.8 0.4 fusion.66
  58.1 0.8 %pad_maximum_fusion.10 = f32[4,25,8,128]{3,2,1,0:T(8,128)} fusion(f32[1,25,8,128]{3,2,1,0:T(8,128)S(1)} %fusion.68, f32[1,25,8,128]{3,2,1,0:T(8,128)S(1)} %fusion.67, f32[1,25,8,128]{3,2,1,0:T(8,128)S(1)} %fusion.66, f32[1,25,8,128]{3,2,1,0:T(8,128)S(1)} %fusion.65), kind=kLoop, calls=%fused_computation.94 | loop fusion | flops 307200 | bytes 819200 | tf_op jit(solution)/shard_map/stack | solution.py:93
  (19 shorter events, 1.7 us)
Async XLA Ops:
  0.0 27.6 %copy-start = (f32[4,25,8,128]{3,2,1,0:T(8,128)S(1)}, f32[4,25,8,128]{3,2,1,0:T(8,128)}, u32[]{:S(2)}) copy-start(f32[4,25,8,128]{3,2,1,0:T(8,128)} %param.4) | copy-start | bytes 1228804
  2.2 17.2 %collective-permute-start.1 = (f32[101,4,128]{2,1,0:T(4,128)S(1)}, f32[101,4,128]{2,1,0:T(4,128)S(1)}, u32[]{:S(2)}, u32[]{:S(2)}) collective-permute-start(f32[101,4,128]{2,1,0:T(4,128)S(1)} %get-tuple-element.13), channel_id=1, source_target_pairs={{1,2},{3,4},{5,6},{2,1},{4,3},{6,5},{9,10},{11,12},{13,14},{10,9},... | collective-permute-start | bytes 620552 | tf_op jit(solution)/shard_map/ppermute | solution.py:34
  4.2 23.2 %collective-permute-start = (f32[101,4,128]{2,1,0:T(4,128)S(1)}, f32[101,4,128]{2,1,0:T(4,128)S(1)}, u32[]{:S(2)}, u32[]{:S(2)}) collective-permute-start(f32[101,4,128]{2,1,0:T(4,128)S(1)} %get-tuple-element.14), channel_id=1, source_target_pairs={{0,1},{1,0},{2,3},{3,2},{4,5},{5,4},{6,7},{7,6},{8,9},{9,8},{10,11... | collective-permute-start | bytes 620552 | tf_op jit(solution)/shard_map/ppermute | solution.py:35
  29.0 18.1 %collective-permute-start.3 = (f32[6464]{0:T(1024)S(1)}, f32[6464]{0:T(1024)S(1)}, u32[]{:S(2)}, u32[]{:S(2)}) collective-permute-start(f32[6464]{0:T(1024)S(1)} %select_n.112), channel_id=1, source_target_pairs={{8,16},{24,32},{40,48},{56,64},{72,80},{88,96},{104,112},{120,128}... | collective-permute-start | bytes 77576 | tf_op jit(solution)/shard_map/ppermute | solution.py:55
  34.0 13.1 %collective-permute-start.2 = (f32[6464]{0:T(1024)S(1)}, f32[6464]{0:T(1024)S(1)}, u32[]{:S(2)}, u32[]{:S(2)}) collective-permute-start(f32[6464]{0:T(1024)S(1)} %select_n.110), channel_id=1, source_target_pairs={{0,8},{8,0},{16,24},{24,16},{32,40},{40,32},{48,56},{56,48},{64,72... | collective-permute-start | bytes 77576 | tf_op jit(solution)/shard_map/ppermute | solution.py:50

commit v6 on v5

--- a/solution.py
+++ b/solution.py
@@ -55,7 +55,7 @@
     off_chip = lax.ppermute(jnp.where(lon_odd, east_cols, west_cols), "lon", across)
     west = jnp.where(lon_odd, on_chip, off_chip).reshape(edge_shape)
     east = jnp.where(lon_odd, off_chip, on_chip).reshape(edge_shape)
-    return jnp.concatenate([west, lat_wide, east], axis=2)
+    return lat_wide, west, east
 
 
 def advance(f, wet, cor):
@@ -100,18 +100,24 @@
     channels = jnp.concatenate([state.reshape(n_fields * level_count, tile_rows, tile_cols), depth[None]])
     signs = jnp.array([1.0, 1.0, -1.0, -1.0], dtype=jnp.float32)
     signs = jnp.concatenate([jnp.repeat(signs, level_count), jnp.ones((1,), jnp.float32)])
-    wide = gather_wide(channels, signs[:, None, None])
+    lat_wide, west, east = gather_wide(channels, signs[:, None, None])
 
     lat = lax.axis_index("lat")
     total = lax.axis_size("lat") * tile_rows
     first_row = lat * tile_rows
+    grown_rows = first_row - MARGIN + jnp.arange(tile_rows + 2 * MARGIN, dtype=jnp.int32)
+    grown_cor = coriolis(grown_rows, total)
 
-    grown = wide[:, MARGIN:-MARGIN, MARGIN:-MARGIN]
-    grown_depth = grown[-1]
-    grown_wet = (depth_index < grown_depth[None]).astype(jnp.float32)
-    grown_rows = first_row - MARGIN + jnp.arange(tile_rows + 2 * MARGIN, dtype=jnp.int32)
-    fields = wide[:-1].reshape(n_fields, level_count, *wide.shape[1:])
-    once = advance(fields, grown_wet, coriolis(grown_rows, total))
+    def step_once(wide):
+        grown_depth = wide[-1, MARGIN:-MARGIN, MARGIN:-MARGIN]
+        grown_wet = (depth_index < grown_depth[None]).astype(jnp.float32)
+        fields = wide[:-1].reshape(n_fields, level_count, *wide.shape[1:])
+        return advance(fields, grown_wet, grown_cor)
+
+    inner = step_once(lat_wide)
+    edges = step_once(jnp.concatenate([west, lat_wide[..., :WIDE], lat_wide[..., -WIDE:], east], axis=2))
+    span = 2 * MARGIN
+    once = jnp.concatenate([edges[..., :span], inner, edges[..., -span:]], axis=3)
     south_edge = (lat == 0) & (grown_rows < 0)
     once = jnp.where(south_edge[:, None], 0.0, once)
 

time: 59.2 us -> 65.9 us (1.11)
  other arithmetic: 12.9 us -> 17.7 us
  local copies, waits for them, and re-layouts: 3.94 us -> 8.6 us
  waiting for transfers between devices: 18.6 us -> 15.1 us
    another operation x9 -> x14, other arithmetic: 8.04 us -> 10.8 us  [advance(): return jnp.stack([heat, salt, u, v])]
    select_n x1, local copies, waits for them, and re-layouts: 0.44 us -> 2.19 us  [gather_wide(): jnp.where(lon_odd, east_cols, west_cols)]
    select_n x1, local copies, waits for them, and re-layouts: 0.44 us -> 2.19 us  [gather_wide(): jnp.where(lon_odd, west_cols, east_cols)]
    ppermute x1, waiting for transfers between devices: 10.9 us -> 9.22 us  [gather_wide(): lax.ppermute(jnp.where(lon_odd, east_cols, west_cols), 'lon', across)]
    ppermute x1, waiting for transfers between devices: 7.6 us -> 5.89 us  [gather_wide(): lax.ppermute(jnp.where(odd, bottom_rows, top_rows), ('lon', 'lat'), [(l *...]
    slice x0 -> x1, other arithmetic: none -> 1.52 us  [gather_wide(): west_cols = lat_wide[..., :WIDE].reshape(-1)]
    unnamed x2 -> x18, local copies, waits for them, and re-layouts: 0.01 us -> 0.89 us
  transfers between devices with their start and end apart: 4 -> 4, of which waited for: 2 -> 2; matrix products, arithmetic and copies ran while one was open for 2% -> 6% of each run, Pallas kernels for 0% -> 0%
where the time goes in v6:
time: 65.9 us; the launch traced here: 65.6 us
  starting transfers between devices  23.9 us (36%)
  other arithmetic  17.7 us (27%)
  waiting for transfers between devices  15.1 us (23%)
  local copies, waits for them, and re-layouts  8.6 us (13%)
    ppermute x1, starting transfers between devices, gather_wide(): lax.ppermute(jnp.where(odd, bottom_rows, top_rows), ('lon', 'lat'), [(l *...  14.1 us
    another operation x14, other arithmetic, advance(): return jnp.stack([heat, salt, u, v])  10.8 us
    ppermute x1, waiting for transfers between devices, gather_wide(): lax.ppermute(jnp.where(lon_odd, east_cols, west_cols), 'lon', across)  9.22 us
    ppermute x1, waiting for transfers between devices, gather_wide(): lax.ppermute(jnp.where(odd, bottom_rows, top_rows), ('lon', 'lat'), [(l *...  5.89 us
    ppermute x1, starting transfers between devices, gather_wide(): lax.ppermute(jnp.where(lon_odd, east_cols, west_cols), 'lon', across)  5.64 us
    select_n x1, local copies, waits for them, and re-layouts, gather_wide(): jnp.where(lon_odd, east_cols, west_cols)  2.19 us
    select_n x1, local copies, waits for them, and re-layouts, gather_wide(): jnp.where(lon_odd, west_cols, east_cols)  2.19 us
    ppermute x1, starting transfers between devices, gather_wide(): lax.ppermute(jnp.where(lon_odd, west_cols, east_cols), 'lon', [(m, m ^ 1)...  2.1 us
  transfers between devices with their start and end apart: 4, of which 2 were waited for; matrix products, arithmetic and copies ran while one was open for 6% of the time, Pallas kernels for 0%

profile of v6, /device:TPU:192, one launch (start us, length us, event | category | flops | bytes accessed | tf_op | source)
XLA Modules:
  0.0 65.6 jit_solution(11694797745366209861)
XLA Ops:
  0.0 0.8 %select_convert_fusion = f32[8,128]{1,0:T(8,128)S(1)} fusion(s32[8,128]{1,0:T(8,128)} %param.6, s32[8,128]{1,0:T(8,128)} %param.5), kind=kLoop, calls=%fused_computation.259 | loop fusion | flops 3072 | bytes 12288 | tf_op jit(solution)/shard_map/convert_element_type | solution.py:99
  0.8 1.4 %broadcast_select_fusion.3 = (f32[101,4,128]{2,1,0:T(4,128)S(1)}, f32[101,4,128]{2,1,0:T(4,128)S(1)}) fusion(pred[]{:T(512)S(6)} %eq.25, f32[1,8,128]{2,1,0:T(8,128)S(1)} %bitcast.51, f32[100,8,128]{2,1,0:T(8,128)} %bitcast.44), kind=kLoop, calls=%fused_computation.183 | loop fusion | flops 258560 | bytes 827393 | tf_op jit(solution)/shard_map/jit(_where)/select_n | solution.py:34
  2.1 2.0 %collective-permute-start.1 = (f32[101,4,128]{2,1,0:T(4,128)S(1)}, f32[101,4,128]{2,1,0:T(4,128)S(1)}, u32[]{:S(2)}, u32[]{:S(2)}) collective-permute-start(f32[101,4,128]{2,1,0:T(4,128)S(1)} %get-tuple-element.17), channel_id=1, source_target_pairs={{1,2},{3,4},{5,6},{2,1},{4,3},{6,5},{9,10},{11,12},{13,14},{10,9},... | collective-permute-start | bytes 620552 | tf_op jit(solution)/shard_map/ppermute | solution.py:34
  4.1 14.1 %collective-permute-start = (f32[101,4,128]{2,1,0:T(4,128)S(1)}, f32[101,4,128]{2,1,0:T(4,128)S(1)}, u32[]{:S(2)}, u32[]{:S(2)}) collective-permute-start(f32[101,4,128]{2,1,0:T(4,128)S(1)} %get-tuple-element.18), channel_id=1, source_target_pairs={{0,1},{1,0},{2,3},{3,2},{4,5},{5,4},{6,7},{7,6},{8,9},{9,8},{10,11... | collective-permute-start | bytes 620552 | tf_op jit(solution)/shard_map/ppermute | solution.py:35
  18.9 0.7 %broadcast_in_dim.35 = f32[4,25]{1,0:T(4,128)S(1)} broadcast(f32[4]{0:T(128)} %constant.150.clone), dimensions={0} | broadcast | bytes 416 | tf_op jit(solution)/shard_map/broadcast_in_dim | solution.py:102
  20.8 5.9 %collective-permute-done = f32[101,4,128]{2,1,0:T(4,128)S(1)} collective-permute-done((f32[101,4,128]{2,1,0:T(4,128)S(1)}, f32[101,4,128]{2,1,0:T(4,128)S(1)}, u32[]{:S(2)}, u32[]{:S(2)}) %collective-permute-start) | collective-permute-done | bytes 206880 | tf_op jit(solution)/shard_map/ppermute | solution.py:35
  27.2 0.7 %fusion.8 = f32[1,25,12,124]{3,2,1,0:T(8,128)S(1)} fusion(f32[101,4,128]{2,1,0:T(4,128)S(1)} %get-tuple-element.15, f32[1,8,128]{2,1,0:T(8,128)S(1)} %bitcast.54, f32[100,8,128]{2,1,0:T(8,128)S(1)} %bitcast.47, f32[101,4,128]{2,1,0:T(4,128)S(1)} %get-tuple-element.16, f32[101,16,128]{2,1,0:T(8,128)S(1)} %pad_maximum_fusion, ...), kind=kLoop, calls=%fused_computation.34 | loop fusion | flops 1041600 | bytes 2321444 | tf_op jit(solution)/shard_map/stack | solution.py:93
  27.9 1.5 %fusion.10 = f32[1,25,12,124]{3,2,1,0:T(8,128)} fusion(f32[101,4,128]{2,1,0:T(4,128)S(1)} %get-tuple-element.15, f32[1,8,128]{2,1,0:T(8,128)S(1)} %bitcast.55, f32[100,8,128]{2,1,0:T(8,128)S(1)} %bitcast.48, f32[101,4,128]{2,1,0:T(4,128)S(1)} %get-tuple-element.16, f32[101,16,128]{2,1,0:T(8,128)S(1)} %pad_maximum_fusion, ...), kind=kLoop, calls=%fused_computation.36 | loop fusion | flops 1339200 | bytes 2767892 | tf_op jit(solution)/shard_map/stack | solution.py:93
  29.3 1.5 %fusion.11 = f32[1,25,12,124]{3,2,1,0:T(8,128)} fusion(f32[101,4,128]{2,1,0:T(4,128)S(1)} %get-tuple-element.15, f32[1,8,128]{2,1,0:T(8,128)S(1)} %bitcast.56, f32[100,8,128]{2,1,0:T(8,128)S(1)} %bitcast.49, f32[101,4,128]{2,1,0:T(4,128)S(1)} %get-tuple-element.16, f32[101,16,128]{2,1,0:T(8,128)S(1)} %pad_maximum_fusion, ...), kind=kLoop, calls=%fused_computation.37 | loop fusion | flops 1339200 | bytes 2767892 | tf_op jit(solution)/shard_map/stack | solution.py:93
  30.8 1.5 %fusion.198 = (f32[101,16,4]{2,1,0:T(8,128)S(1)}, f32[101,16,4]{2,1,0:T(8,128)}, f32[101,16,4]{2,1,0:T(8,128)}, f32[101,16,4]{2,1,0:T(8,128)S(1)}) fusion(f32[101,16,128]{2,1,0:T(8,128)S(1)} %pad_maximum_fusion, pred[]{:T(512)S(6)} %eq.24), kind=kLoop, calls=%fused_computation.286 | loop fusion | flops 12928 | bytes 155137 | tf_op jit(solution)/shard_map/slice | solution.py:49
  32.4 2.2 %select_n.110 = f32[6464]{0:T(1024)} reshape(f32[101,16,4]{2,1,0:T(8,128)} %get-tuple-element.10) | data formatting | bytes 51712 | tf_op jit(solution)/shard_map/jit(_where)/select_n | solution.py:51
  34.5 2.2 %select_n.112 = f32[6464]{0:T(1024)} reshape(f32[101,16,4]{2,1,0:T(8,128)} %get-tuple-element.11) | data formatting | bytes 51712 | tf_op jit(solution)/shard_map/jit(_where)/select_n | solution.py:55
  36.7 5.6 %collective-permute-start.3 = (f32[6464]{0:T(1024)}, f32[6464]{0:T(1024)S(1)}, u32[]{:S(2)}, u32[]{:S(2)}) collective-permute-start(f32[6464]{0:T(1024)} %select_n.112), channel_id=1, source_target_pairs={{8,16},{24,32},{40,48},{56,64},{72,80},{88,96},{104,112},{120,128}... | collective-permute-start | bytes 77576 | tf_op jit(solution)/shard_map/ppermute | solution.py:55
  42.4 2.1 %collective-permute-start.2 = (f32[6464]{0:T(1024)}, f32[6464]{0:T(1024)S(1)}, u32[]{:S(2)}, u32[]{:S(2)}) collective-permute-start(f32[6464]{0:T(1024)} %select_n.110), channel_id=1, source_target_pairs={{0,8},{8,0},{16,24},{24,16},{32,40},{40,32},{48,56},{56,48},{64,72... | collective-permute-start | bytes 77576 | tf_op jit(solution)/shard_map/ppermute | solution.py:50
  44.5 1.3 %fusion.9 = f32[1,25,12,124]{3,2,1,0:T(8,128)} fusion(f32[101,4,128]{2,1,0:T(4,128)S(1)} %get-tuple-element.15, f32[1,8,128]{2,1,0:T(8,128)S(1)} %bitcast.57, f32[100,8,128]{2,1,0:T(8,128)S(1)} %bitcast.50, f32[101,4,128]{2,1,0:T(4,128)S(1)} %get-tuple-element.16, f32[101,16,128]{2,1,0:T(8,128)S(1)} %pad_maximum_fusion, ...), kind=kLoop, calls=%fused_computation.35 | loop fusion | flops 1041600 | bytes 2321444 | tf_op jit(solution)/shard_map/stack | solution.py:93
  45.8 9.2 %collective-permute-done.3 = f32[6464]{0:T(1024)S(1)} collective-permute-done((f32[6464]{0:T(1024)}, f32[6464]{0:T(1024)S(1)}, u32[]{:S(2)}, u32[]{:S(2)}) %collective-permute-start.3) | collective-permute-done | bytes 25888 | tf_op jit(solution)/shard_map/ppermute | solution.py:55
  55.1 0.8 %reshape.81 = f32[101,16,4]{2,1,0:T(8,128)S(1)} reshape(f32[6464]{0:T(1024)S(1)} %get-tuple-element.19) | data formatting | bytes 51712 | tf_op jit(solution)/shard_map/reshape | solution.py:56
  55.9 0.9 %reshape.82 = f32[101,16,4]{2,1,0:T(8,128)S(1)} reshape(f32[6464]{0:T(1024)S(1)} %get-tuple-element.20) | data formatting | bytes 51712 | tf_op jit(solution)/shard_map/reshape | solution.py:57
  56.9 0.7 %pad_maximum_fusion.1 = f32[101,16,16]{2,1,0:T(8,128)S(1)} fusion(f32[101,16,4]{2,1,0:T(8,128)S(1)} %reshape.82, f32[101,16,4]{2,1,0:T(8,128)S(1)} %get-tuple-element.12, f32[101,16,4]{2,1,0:T(8,128)S(1)} %get-tuple-element.9, f32[101,16,4]{2,1,0:T(8,128)S(1)} %reshape.81), kind=kLoop, calls=%fused_computation.5 | loop fusion | flops 77568 | bytes 206848 | tf_op jit(solution)/shard_map/concatenate | solution.py:118
  57.6 0.9 %fusion.6 = f32[1,25,12,12]{3,2,1,0:T(8,128)S(1)} fusion(f32[101,16,16]{2,1,0:T(8,128)S(1)} %pad_maximum_fusion.1, f32[101,16,4]{2,1,0:T(8,128)S(1)} %get-tuple-element.12, f32[101,16,4]{2,1,0:T(8,128)S(1)} %get-tuple-element.9, f32[101,16,4]{2,1,0:T(8,128)S(1)} %reshape.81, f32[101,16,4]{2,1,0:T(8,128)S(1)} %reshape.82, ...), kind=kLoop, calls=%fused_computation.32 | loop fusion | flops 129600 | bytes 291348 | tf_op jit(solution)/shard_map/stack | solution.py:93
  58.5 1.0 %fusion.7 = f32[1,25,12,12]{3,2,1,0:T(8,128)S(1)} fusion(f32[101,16,16]{2,1,0:T(8,128)S(1)} %pad_maximum_fusion.1, f32[101,16,4]{2,1,0:T(8,128)S(1)} %get-tuple-element.12, f32[101,16,4]{2,1,0:T(8,128)S(1)} %get-tuple-element.9, f32[101,16,4]{2,1,0:T(8,128)S(1)} %reshape.81, f32[101,16,4]{2,1,0:T(8,128)S(1)} %reshape.82, ...), kind=kLoop, calls=%fused_computation.33 | loop fusion | flops 129600 | bytes 291348 | tf_op jit(solution)/shard_map/stack | solution.py:93
  59.5 0.8 %fusion.4 = f32[1,25,12,12]{3,2,1,0:T(8,128)S(1)} fusion(f32[101,16,16]{2,1,0:T(8,128)S(1)} %pad_maximum_fusion.1, f32[101,16,4]{2,1,0:T(8,128)S(1)} %get-tuple-element.12, f32[101,16,4]{2,1,0:T(8,128)S(1)} %get-tuple-element.9, f32[101,16,4]{2,1,0:T(8,128)S(1)} %reshape.81, f32[101,16,4]{2,1,0:T(8,128)S(1)} %reshape.82, ...), kind=kLoop, calls=%fused_computation.30 | loop fusion | flops 100800 | bytes 248100 | tf_op jit(solution)/shard_map/stack | solution.py:93
  60.3 0.8 %fusion.5 = f32[1,25,12,12]{3,2,1,0:T(8,128)S(1)} fusion(f32[101,16,16]{2,1,0:T(8,128)S(1)} %pad_maximum_fusion.1, f32[101,16,4]{2,1,0:T(8,128)S(1)} %get-tuple-element.12, f32[101,16,4]{2,1,0:T(8,128)S(1)} %get-tuple-element.9, f32[101,16,4]{2,1,0:T(8,128)S(1)} %reshape.81, f32[101,16,4]{2,1,0:T(8,128)S(1)} %reshape.82, ...), kind=kLoop, calls=%fused_computation.31 | loop fusion | flops 100800 | bytes 248100 | tf_op jit(solution)/shard_map/stack | solution.py:93
  64.8 0.8 %pad_maximum_fusion.3 = f32[4,25,8,128]{3,2,1,0:T(8,128)} fusion(f32[1,25,8,128]{3,2,1,0:T(8,128)S(1)} %fusion.123, f32[1,25,8,128]{3,2,1,0:T(8,128)S(1)} %fusion.122, f32[1,25,8,128]{3,2,1,0:T(8,128)S(1)} %fusion.121, f32[1,25,8,128]{3,2,1,0:T(8,128)S(1)} %fusion.120), kind=kLoop, calls=%fused_computation.15 | loop fusion | flops 307200 | bytes 819200 | tf_op jit(solution)/shard_map/stack | solution.py:93
  (43 shorter events, 6.0 us)
Async XLA Ops:
  0.0 26.9 %copy-start = (f32[4,25,8,128]{3,2,1,0:T(8,128)S(1)}, f32[4,25,8,128]{3,2,1,0:T(8,128)}, u32[]{:S(2)}) copy-start(f32[4,25,8,128]{3,2,1,0:T(8,128)} %param.4) | copy-start | bytes 1228804
  2.1 18.3 %collective-permute-start.1 = (f32[101,4,128]{2,1,0:T(4,128)S(1)}, f32[101,4,128]{2,1,0:T(4,128)S(1)}, u32[]{:S(2)}, u32[]{:S(2)}) collective-permute-start(f32[101,4,128]{2,1,0:T(4,128)S(1)} %get-tuple-element.17), channel_id=1, source_target_pairs={{1,2},{3,4},{5,6},{2,1},{4,3},{6,5},{9,10},{11,12},{13,14},{10,9},... | collective-permute-start | bytes 620552 | tf_op jit(solution)/shard_map/ppermute | solution.py:34
  4.1 22.6 %collective-permute-start = (f32[101,4,128]{2,1,0:T(4,128)S(1)}, f32[101,4,128]{2,1,0:T(4,128)S(1)}, u32[]{:S(2)}, u32[]{:S(2)}) collective-permute-start(f32[101,4,128]{2,1,0:T(4,128)S(1)} %get-tuple-element.18), channel_id=1, source_target_pairs={{0,1},{1,0},{2,3},{3,2},{4,5},{5,4},{6,7},{7,6},{8,9},{9,8},{10,11... | collective-permute-start | bytes 620552 | tf_op jit(solution)/shard_map/ppermute | solution.py:35
  18.4 9.5 %copy-start.4 = (f32[12]{0:T(128)}, f32[12]{0:T(128)S(1)}, u32[]{:S(2)}) copy-start(f32[12]{0:T(128)S(1)} %get-tuple-element.23) | copy-start | bytes 148
  36.7 18.3 %collective-permute-start.3 = (f32[6464]{0:T(1024)}, f32[6464]{0:T(1024)S(1)}, u32[]{:S(2)}, u32[]{:S(2)}) collective-permute-start(f32[6464]{0:T(1024)} %select_n.112), channel_id=1, source_target_pairs={{8,16},{24,32},{40,48},{56,64},{72,80},{88,96},{104,112},{120,128}... | collective-permute-start | bytes 77576 | tf_op jit(solution)/shard_map/ppermute | solution.py:55
  42.4 12.7 %collective-permute-start.2 = (f32[6464]{0:T(1024)}, f32[6464]{0:T(1024)S(1)}, u32[]{:S(2)}, u32[]{:S(2)}) collective-permute-start(f32[6464]{0:T(1024)} %select_n.110), channel_id=1, source_target_pairs={{0,8},{8,0},{16,24},{24,16},{32,40},{40,32},{48,56},{56,48},{64,72... | collective-permute-start | bytes 77576 | tf_op jit(solution)/shard_map/ppermute | solution.py:50
  56.9 0.8 %copy-start.5 = (f32[12]{0:T(128)S(1)}, f32[12]{0:T(128)}, u32[]{:S(2)}) copy-start(f32[12]{0:T(128)} %copy-done.4) | copy-start | bytes 148
  61.2 0.9 %copy-start.1 = (f32[1,25,12,124]{3,2,1,0:T(8,128)S(1)}, f32[1,25,12,124]{3,2,1,0:T(8,128)}, u32[]{:S(2)}) copy-start(f32[1,25,12,124]{3,2,1,0:T(8,128)} %fusion.10) | copy-start | bytes 446404
  61.2 1.0 %copy-start.2 = (f32[1,25,12,124]{3,2,1,0:T(8,128)S(1)}, f32[1,25,12,124]{3,2,1,0:T(8,128)}, u32[]{:S(2)}) copy-start(f32[1,25,12,124]{3,2,1,0:T(8,128)} %fusion.11) | copy-start | bytes 446404
  61.2 1.1 %copy-start.3 = (f32[1,25,12,124]{3,2,1,0:T(8,128)S(1)}, f32[1,25,12,124]{3,2,1,0:T(8,128)}, u32[]{:S(2)}) copy-start(f32[1,25,12,124]{3,2,1,0:T(8,128)} %fusion.9) | copy-start | bytes 446404
  61.2 1.1 %copy-start.8 = (pred[12]{0:T(512)(128)(4,1)S(1)}, pred[12]{0:T(512)(128)(4,1)}, u32[]{:S(2)}) copy-start(pred[12]{0:T(512)(128)(4,1)} %compare_and_fusion) | copy-start | bytes 40
  63.0 0.6 copy-start.7
  63.1 0.8 %copy-start.6 = (f32[8]{0:T(128)S(1)}, f32[8]{0:T(128)}, u32[]{:S(2)}) copy-start(f32[8]{0:T(128)} %get-tuple-element.22) | copy-start | bytes 100

commit v7 on v6

--- a/solution.py
+++ b/solution.py
@@ -108,13 +108,13 @@
     grown_rows = first_row - MARGIN + jnp.arange(tile_rows + 2 * MARGIN, dtype=jnp.int32)
     grown_cor = coriolis(grown_rows, total)
 
-    def step_once(wide):
-        grown_depth = wide[-1, MARGIN:-MARGIN, MARGIN:-MARGIN]
+    def step_once(wide, tie=0.0):
+        grown_depth = wide[-1, MARGIN:-MARGIN, MARGIN:-MARGIN] + tie
         grown_wet = (depth_index < grown_depth[None]).astype(jnp.float32)
         fields = wide[:-1].reshape(n_fields, level_count, *wide.shape[1:])
         return advance(fields, grown_wet, grown_cor)
 
-    inner = step_once(lat_wide)
+    inner = step_once(lat_wide, 0.0 * (west[-1, :1, :1] + east[-1, :1, :1]))
     edges = step_once(jnp.concatenate([west, lat_wide[..., :WIDE], lat_wide[..., -WIDE:], east], axis=2))
     span = 2 * MARGIN
     once = jnp.concatenate([edges[..., :span], inner, edges[..., -span:]], axis=3)

time: 65.9 us -> 71.1 us (1.079)
  local copies, waits for them, and re-layouts: 8.6 us -> 11.1 us
  between operations: 0.3 us -> 1.53 us
    slice x0 -> x2, local copies, waits for them, and re-layouts: none -> 1.74 us  [shards(): inner = step_once(lat_wide, 0.0 * (west[-1, :1, :1] + east[-1, :1, :1]))]
    ppermute x1, waiting for transfers between devices: 9.22 us -> 10.5 us  [gather_wide(): lax.ppermute(jnp.where(lon_odd, east_cols, west_cols), 'lon', across)]
    select_n x1, local copies, waits for them, and re-layouts: 2.19 us -> 1.05 us  [gather_wide(): jnp.where(lon_odd, east_cols, west_cols)]
    another operation x14, other arithmetic: 10.8 us -> 9.83 us  [advance(): return jnp.stack([heat, salt, u, v])]
    reshape x1, local copies, waits for them, and re-layouts: 0.85 us -> 1.77 us  [gather_wide(): east = jnp.where(lon_odd, off_chip, on_chip).reshape(edge_shape)]
    unnamed x18 -> x22, local copies, waits for them, and re-layouts: 0.89 us -> 1.69 us
    reshape x1, local copies, waits for them, and re-layouts: 0.85 us -> 1.59 us  [gather_wide(): west = jnp.where(lon_odd, on_chip, off_chip).reshape(edge_shape)]
  transfers between devices with their start and end apart: 4 -> 4, of which waited for: 2 -> 2; matrix products, arithmetic and copies ran while one was open for 6% -> 5% of each run, Pallas kernels for 0% -> 0%
where the time goes in v7:
time: 71.1 us; the launch traced here: 70.6 us
  starting transfers between devices  23.9 us (34%)
  other arithmetic  18.3 us (26%)
  waiting for transfers between devices  15.8 us (22%)
  local copies, waits for them, and re-layouts  11.1 us (16%)
  between operations  1.53 us (2%)
    ppermute x1, starting transfers between devices, gather_wide(): lax.ppermute(jnp.where(odd, bottom_rows, top_rows), ('lon', 'lat'), [(l *...  14.1 us
    ppermute x1, waiting for transfers between devices, gather_wide(): lax.ppermute(jnp.where(lon_odd, east_cols, west_cols), 'lon', across)  10.5 us
    another operation x14, other arithmetic, advance(): return jnp.stack([heat, salt, u, v])  9.83 us
    ppermute x1, starting transfers between devices, gather_wide(): lax.ppermute(jnp.where(lon_odd, east_cols, west_cols), 'lon', across)  5.64 us
    ppermute x1, waiting for transfers between devices, gather_wide(): lax.ppermute(jnp.where(odd, bottom_rows, top_rows), ('lon', 'lat'), [(l *...  5.26 us
    ppermute x1, starting transfers between devices, gather_wide(): lax.ppermute(jnp.where(lon_odd, west_cols, east_cols), 'lon', [(m, m ^ 1)...  2.1 us
    ppermute x1, starting transfers between devices, gather_wide(): lax.ppermute(jnp.where(odd, top_rows, bottom_rows), ('lon', 'lat'), pairs)  2.02 us
    reshape x1, local copies, waits for them, and re-layouts, gather_wide(): east = jnp.where(lon_odd, off_chip, on_chip).reshape(edge_shape)  1.77 us
  transfers between devices with their start and end apart: 4, of which 2 were waited for; matrix products, arithmetic and copies ran while one was open for 5% of the time, Pallas kernels for 0%

profile of v7, /device:TPU:192, one launch (start us, length us, event | category | flops | bytes accessed | tf_op | source)
XLA Modules:
  0.0 70.6 jit_solution(13368086480238031271)
XLA Ops:
  0.0 0.8 %select_convert_fusion = f32[8,128]{1,0:T(8,128)S(1)} fusion(s32[8,128]{1,0:T(8,128)} %param.6, s32[8,128]{1,0:T(8,128)} %param.5), kind=kLoop, calls=%fused_computation.260 | loop fusion | flops 3072 | bytes 12288 | tf_op jit(solution)/shard_map/convert_element_type | solution.py:99
  0.8 1.4 %broadcast_select_fusion.3 = (f32[101,4,128]{2,1,0:T(4,128)S(1)}, f32[101,4,128]{2,1,0:T(4,128)S(1)}) fusion(pred[]{:T(512)S(6)} %eq.25, f32[1,8,128]{2,1,0:T(8,128)S(1)} %bitcast.52, f32[100,8,128]{2,1,0:T(8,128)} %bitcast.45), kind=kLoop, calls=%fused_computation.183 | loop fusion | flops 258560 | bytes 827393 | tf_op jit(solution)/shard_map/jit(_where)/select_n | solution.py:34
  2.1 2.0 %collective-permute-start.1 = (f32[101,4,128]{2,1,0:T(4,128)S(1)}, f32[101,4,128]{2,1,0:T(4,128)S(1)}, u32[]{:S(2)}, u32[]{:S(2)}) collective-permute-start(f32[101,4,128]{2,1,0:T(4,128)S(1)} %get-tuple-element.17), channel_id=1, source_target_pairs={{1,2},{3,4},{5,6},{2,1},{4,3},{6,5},{9,10},{11,12},{13,14},{10,9},... | collective-permute-start | bytes 620552 | tf_op jit(solution)/shard_map/ppermute | solution.py:34
  4.1 14.1 %collective-permute-start = (f32[101,4,128]{2,1,0:T(4,128)S(1)}, f32[101,4,128]{2,1,0:T(4,128)S(1)}, u32[]{:S(2)}, u32[]{:S(2)}) collective-permute-start(f32[101,4,128]{2,1,0:T(4,128)S(1)} %get-tuple-element.18), channel_id=1, source_target_pairs={{0,1},{1,0},{2,3},{3,2},{4,5},{5,4},{6,7},{7,6},{8,9},{9,8},{10,11... | collective-permute-start | bytes 620552 | tf_op jit(solution)/shard_map/ppermute | solution.py:35
  19.5 0.7 %broadcast_in_dim.36 = f32[4,25]{1,0:T(4,128)S(1)} broadcast(f32[4]{0:T(128)} %constant.153.clone), dimensions={0} | broadcast | bytes 416 | tf_op jit(solution)/shard_map/broadcast_in_dim | solution.py:102
  21.5 5.3 %collective-permute-done = f32[101,4,128]{2,1,0:T(4,128)S(1)} collective-permute-done((f32[101,4,128]{2,1,0:T(4,128)S(1)}, f32[101,4,128]{2,1,0:T(4,128)S(1)}, u32[]{:S(2)}, u32[]{:S(2)}) %collective-permute-start) | collective-permute-done | bytes 206880 | tf_op jit(solution)/shard_map/ppermute | solution.py:35
  27.8 1.2 %fusion.199 = (f32[101,16,4]{2,1,0:T(8,128)S(1)}, f32[101,16,4]{2,1,0:T(8,128)}, f32[101,16,4]{2,1,0:T(8,128)S(1)}, f32[101,16,4]{2,1,0:T(8,128)S(1)}) fusion(f32[101,16,128]{2,1,0:T(8,128)S(1)} %pad_maximum_fusion, pred[]{:T(512)S(6)} %eq.24), kind=kLoop, calls=%fused_computation.287 | loop fusion | flops 12928 | bytes 155137 | tf_op jit(solution)/shard_map/slice | solution.py:49
  29.1 1.6 %select_n.110 = f32[6464]{0:T(1024)S(1)} reshape(f32[101,16,4]{2,1,0:T(8,128)} %get-tuple-element.10) | data formatting | bytes 51712 | tf_op jit(solution)/shard_map/jit(_where)/select_n | solution.py:51
  30.6 1.1 %select_n.112 = f32[6464]{0:T(1024)} reshape(f32[101,16,4]{2,1,0:T(8,128)S(1)} %get-tuple-element.11) | data formatting | bytes 51712 | tf_op jit(solution)/shard_map/jit(_where)/select_n | solution.py:55
  31.7 5.6 %collective-permute-start.3 = (f32[6464]{0:T(1024)}, f32[6464]{0:T(1024)S(1)}, u32[]{:S(2)}, u32[]{:S(2)}) collective-permute-start(f32[6464]{0:T(1024)} %select_n.112), channel_id=1, source_target_pairs={{8,16},{24,32},{40,48},{56,64},{72,80},{88,96},{104,112},{120,128}... | collective-permute-start | bytes 77576 | tf_op jit(solution)/shard_map/ppermute | solution.py:55
  37.3 2.1 %collective-permute-start.2 = (f32[6464]{0:T(1024)S(1)}, f32[6464]{0:T(1024)S(1)}, u32[]{:S(2)}, u32[]{:S(2)}) collective-permute-start(f32[6464]{0:T(1024)S(1)} %select_n.110), channel_id=1, source_target_pairs={{0,8},{8,0},{16,24},{24,16},{32,40},{40,32},{48,56},{56,48},{64,72... | collective-permute-start | bytes 77576 | tf_op jit(solution)/shard_map/ppermute | solution.py:50
  39.5 10.5 %collective-permute-done.3 = f32[6464]{0:T(1024)S(1)} collective-permute-done((f32[6464]{0:T(1024)}, f32[6464]{0:T(1024)S(1)}, u32[]{:S(2)}, u32[]{:S(2)}) %collective-permute-start.3) | collective-permute-done | bytes 25888 | tf_op jit(solution)/shard_map/ppermute | solution.py:55
  50.6 1.6 %reshape.85 = f32[101,16,4]{2,1,0:T(8,128)S(1)} reshape(f32[6464]{0:T(1024)} %get-tuple-element.19) | data formatting | bytes 51712 | tf_op jit(solution)/shard_map/reshape | solution.py:56
  52.8 1.8 %reshape.86 = f32[101,16,4]{2,1,0:T(8,128)} reshape(f32[6464]{0:T(1024)S(1)} %get-tuple-element.20) | data formatting | bytes 51712 | tf_op jit(solution)/shard_map/reshape | solution.py:57
  54.5 1.2 %slice.846 = f32[1,1,1]{2,1,0:T(1,128)} slice(f32[101,16,4]{2,1,0:T(8,128)} %reshape.86), slice={[100:101], [0:1], [0:1]} | slice | bytes 8 | tf_op jit(solution)/shard_map/slice | solution.py:117
  57.0 0.8 %fusion.178 = f32[12,124]{1,0:T(8,128)S(1)} fusion(f32[101,4,128]{2,1,0:T(4,128)} %copy-done.5, f32[101,4,128]{2,1,0:T(4,128)} %copy-done.3, f32[1,8,128]{2,1,0:T(8,128)S(1)} %bitcast.54, f32[100,8,128]{2,1,0:T(8,128)} %bitcast.46, f32[]{:T(128)} %bitcast.7), kind=kLoop, calls=%fused_computation.258 | loop fusion | flops 5952 | bytes 833348 | tf_op jit(solution)/shard_map/lt | solution.py:113
  57.7 1.7 %fusion.9 = f32[1,25,12,124]{3,2,1,0:T(8,128)S(1)} fusion(f32[101,4,128]{2,1,0:T(4,128)} %copy-done.3, f32[1,8,128]{2,1,0:T(8,128)S(1)} %bitcast.55, f32[100,8,128]{2,1,0:T(8,128)} %bitcast.47, f32[101,4,128]{2,1,0:T(4,128)} %copy-done.5, f32[101,16,128]{2,1,0:T(8,128)S(1)} %pad_maximum_fusion, f32[12,124]{1,0:T(8,128)S(1)} %fusion.178, ...), kind=kLoop, calls=%fused_computation.35 | loop fusion | flops 1041600 | bytes 2321444 | tf_op jit(solution)/shard_map/stack | solution.py:93
  61.4 0.8 %fusion.11 = f32[1,25,12,124]{3,2,1,0:T(8,128)S(1)} fusion(f32[101,4,128]{2,1,0:T(4,128)S(1)} %copy-done.4, f32[1,8,128]{2,1,0:T(8,128)S(1)} %bitcast.57, f32[100,8,128]{2,1,0:T(8,128)S(1)} %bitcast.50, f32[101,4,128]{2,1,0:T(4,128)S(1)} %copy-done.6, f32[101,16,128]{2,1,0:T(8,128)S(1)} %pad_maximum_fusion, ...), kind=kLoop, calls=%fused_computation.37 | loop fusion | flops 1339200 | bytes 2767892 | tf_op jit(solution)/shard_map/stack | solution.py:93
  62.3 0.8 %fusion.10 = f32[1,25,12,124]{3,2,1,0:T(8,128)S(1)} fusion(f32[101,4,128]{2,1,0:T(4,128)S(1)} %copy-done.4, f32[1,8,128]{2,1,0:T(8,128)S(1)} %bitcast.58, f32[100,8,128]{2,1,0:T(8,128)S(1)} %bitcast.51, f32[101,4,128]{2,1,0:T(4,128)S(1)} %copy-done.6, f32[101,16,128]{2,1,0:T(8,128)S(1)} %pad_maximum_fusion, ...), kind=kLoop, calls=%fused_computation.36 | loop fusion | flops 1339200 | bytes 2767892 | tf_op jit(solution)/shard_map/stack | solution.py:93
  63.1 0.9 %fusion.6 = f32[1,25,12,12]{3,2,1,0:T(8,128)S(1)} fusion(f32[101,16,16]{2,1,0:T(8,128)S(1)} %pad_maximum_fusion.1, f32[101,16,4]{2,1,0:T(8,128)S(1)} %get-tuple-element.12, f32[101,16,4]{2,1,0:T(8,128)S(1)} %get-tuple-element.9, f32[101,16,4]{2,1,0:T(8,128)S(1)} %reshape.85, f32[101,16,4]{2,1,0:T(8,128)S(1)} %copy-done, ...), kind=kLoop, calls=%fused_computation.32 | loop fusion | flops 129600 | bytes 291348 | tf_op jit(solution)/shard_map/stack | solution.py:93
  64.0 1.0 %fusion.7 = f32[1,25,12,12]{3,2,1,0:T(8,128)S(1)} fusion(f32[101,16,16]{2,1,0:T(8,128)S(1)} %pad_maximum_fusion.1, f32[101,16,4]{2,1,0:T(8,128)S(1)} %get-tuple-element.12, f32[101,16,4]{2,1,0:T(8,128)S(1)} %get-tuple-element.9, f32[101,16,4]{2,1,0:T(8,128)S(1)} %reshape.85, f32[101,16,4]{2,1,0:T(8,128)S(1)} %copy-done, ...), kind=kLoop, calls=%fused_computation.33 | loop fusion | flops 129600 | bytes 291348 | tf_op jit(solution)/shard_map/stack | solution.py:93
  64.9 0.8 %fusion.4 = f32[1,25,12,12]{3,2,1,0:T(8,128)S(1)} fusion(f32[101,16,16]{2,1,0:T(8,128)S(1)} %pad_maximum_fusion.1, f32[101,16,4]{2,1,0:T(8,128)S(1)} %get-tuple-element.12, f32[101,16,4]{2,1,0:T(8,128)S(1)} %get-tuple-element.9, f32[101,16,4]{2,1,0:T(8,128)S(1)} %reshape.85, f32[101,16,4]{2,1,0:T(8,128)S(1)} %copy-done, ...), kind=kLoop, calls=%fused_computation.30 | loop fusion | flops 100800 | bytes 248100 | tf_op jit(solution)/shard_map/stack | solution.py:93
  65.7 0.8 %fusion.5 = f32[1,25,12,12]{3,2,1,0:T(8,128)S(1)} fusion(f32[101,16,16]{2,1,0:T(8,128)S(1)} %pad_maximum_fusion.1, f32[101,16,4]{2,1,0:T(8,128)S(1)} %get-tuple-element.12, f32[101,16,4]{2,1,0:T(8,128)S(1)} %get-tuple-element.9, f32[101,16,4]{2,1,0:T(8,128)S(1)} %reshape.85, f32[101,16,4]{2,1,0:T(8,128)S(1)} %copy-done, ...), kind=kLoop, calls=%fused_computation.31 | loop fusion | flops 100800 | bytes 248100 | tf_op jit(solution)/shard_map/stack | solution.py:93
  69.8 0.8 %pad_maximum_fusion.3 = f32[4,25,8,128]{3,2,1,0:T(8,128)} fusion(f32[1,25,8,128]{3,2,1,0:T(8,128)S(1)} %fusion.123, f32[1,25,8,128]{3,2,1,0:T(8,128)S(1)} %fusion.122, f32[1,25,8,128]{3,2,1,0:T(8,128)S(1)} %fusion.121, f32[1,25,8,128]{3,2,1,0:T(8,128)S(1)} %fusion.120), kind=kLoop, calls=%fused_computation.15 | loop fusion | flops 307200 | bytes 819200 | tf_op jit(solution)/shard_map/stack | solution.py:93
  (49 shorter events, 9.9 us)
Async XLA Ops:
  0.0 27.7 %copy-start.1 = (f32[4,25,8,128]{3,2,1,0:T(8,128)S(1)}, f32[4,25,8,128]{3,2,1,0:T(8,128)}, u32[]{:S(2)}) copy-start(f32[4,25,8,128]{3,2,1,0:T(8,128)} %param.4) | copy-start | bytes 1228804
  2.1 18.9 %collective-permute-start.1 = (f32[101,4,128]{2,1,0:T(4,128)S(1)}, f32[101,4,128]{2,1,0:T(4,128)S(1)}, u32[]{:S(2)}, u32[]{:S(2)}) collective-permute-start(f32[101,4,128]{2,1,0:T(4,128)S(1)} %get-tuple-element.17), channel_id=1, source_target_pairs={{1,2},{3,4},{5,6},{2,1},{4,3},{6,5},{9,10},{11,12},{13,14},{10,9},... | collective-permute-start | bytes 620552 | tf_op jit(solution)/shard_map/ppermute | solution.py:34
  4.1 22.6 %collective-permute-start = (f32[101,4,128]{2,1,0:T(4,128)S(1)}, f32[101,4,128]{2,1,0:T(4,128)S(1)}, u32[]{:S(2)}, u32[]{:S(2)}) collective-permute-start(f32[101,4,128]{2,1,0:T(4,128)S(1)} %get-tuple-element.18), channel_id=1, source_target_pairs={{0,1},{1,0},{2,3},{3,2},{4,5},{5,4},{6,7},{7,6},{8,9},{9,8},{10,11... | collective-permute-start | bytes 620552 | tf_op jit(solution)/shard_map/ppermute | solution.py:35
  26.9 0.7 copy-start.3
  26.9 0.8 %copy-start.5 = (f32[101,4,128]{2,1,0:T(4,128)}, f32[101,4,128]{2,1,0:T(4,128)S(1)}, u32[]{:S(2)}) copy-start(f32[101,4,128]{2,1,0:T(4,128)S(1)} %get-tuple-element.16) | copy-start | bytes 620548
  31.7 18.3 %collective-permute-start.3 = (f32[6464]{0:T(1024)}, f32[6464]{0:T(1024)S(1)}, u32[]{:S(2)}, u32[]{:S(2)}) collective-permute-start(f32[6464]{0:T(1024)} %select_n.112), channel_id=1, source_target_pairs={{8,16},{24,32},{40,48},{56,64},{72,80},{88,96},{104,112},{120,128}... | collective-permute-start | bytes 77576 | tf_op jit(solution)/shard_map/ppermute | solution.py:55
  37.3 12.7 %collective-permute-start.2 = (f32[6464]{0:T(1024)S(1)}, f32[6464]{0:T(1024)S(1)}, u32[]{:S(2)}, u32[]{:S(2)}) collective-permute-start(f32[6464]{0:T(1024)S(1)} %select_n.110), channel_id=1, source_target_pairs={{0,8},{8,0},{16,24},{24,16},{32,40},{40,32},{48,56},{56,48},{64,72... | collective-permute-start | bytes 77576 | tf_op jit(solution)/shard_map/ppermute | solution.py:50
  57.7 1.7 %copy-start.2 = (f32[4,25,8,128]{3,2,1,0:T(8,128)S(1)}, f32[4,25,8,128]{3,2,1,0:T(8,128)}, u32[]{:S(2)}) copy-start(f32[4,25,8,128]{3,2,1,0:T(8,128)} %param.4) | copy-start | bytes 1228804
  57.7 1.7 %copy-start.4 = (f32[101,4,128]{2,1,0:T(4,128)S(1)}, f32[101,4,128]{2,1,0:T(4,128)}, u32[]{:S(2)}) copy-start(f32[101,4,128]{2,1,0:T(4,128)} %copy-done.3) | copy-start | bytes 620548
  57.7 1.7 %copy-start.6 = (f32[101,4,128]{2,1,0:T(4,128)S(1)}, f32[101,4,128]{2,1,0:T(4,128)}, u32[]{:S(2)}) copy-start(f32[101,4,128]{2,1,0:T(4,128)} %copy-done.5) | copy-start | bytes 620548
  59.5 1.1 %copy-start = (f32[101,16,4]{2,1,0:T(8,128)S(1)}, f32[101,16,4]{2,1,0:T(8,128)}, u32[]{:S(2)}) copy-start(f32[101,16,4]{2,1,0:T(8,128)} %reshape.86) | copy-start | bytes 77572
  61.4 0.8 %copy-start.7 = (f32[12]{0:T(128)S(1)}, f32[12]{0:T(128)}, u32[]{:S(2)}) copy-start(f32[12]{0:T(128)} %get-tuple-element.23) | copy-start | bytes 148
  66.6 0.6 copy-start.10
  68.0 0.6 copy-start.9
  68.1 0.9 %copy-start.8 = (f32[8]{0:T(128)S(1)}, f32[8]{0:T(128)}, u32[]{:S(2)}) copy-start(f32[8]{0:T(128)} %get-tuple-element.22) | copy-start | bytes 100

commit v8 on v5

--- a/solution.py
+++ b/solution.py
@@ -1,6 +1,8 @@
 import jax
 import jax.numpy as jnp
 from jax import lax
+from jax.experimental import pallas as pl
+from jax.experimental.pallas import tpu as pltpu
 from jax.sharding import PartitionSpec as P
 
 TIME_INCREMENT = 0.1
@@ -10,6 +12,7 @@
 HALINE = 0.8
 GRAVITY = 0.1
 MARGIN = 2
+INTERPRET = False
 WIDE = 2 * MARGIN
 
 
@@ -93,6 +96,80 @@
     return jnp.stack([heat, salt, u, v])
 
 
+def two_steps_kernel(wide_ref, cor1_ref, keep1_ref, cor2_ref, out_ref, once_ref, sum1_ref, p1_ref, sum2_ref, p2_ref):
+    n_fields, level_count, rows2, cols2 = out_ref.shape
+    rows1, cols1 = rows2 + 2 * MARGIN, cols2 + 2 * MARGIN
+    depth_ch = n_fields * level_count
+    sum1_ref[...] = jnp.zeros(sum1_ref.shape, jnp.float32)
+    sum2_ref[...] = jnp.zeros(sum2_ref.shape, jnp.float32)
+
+    def stencils(src, dst_p, wet, cor, rows, cols, chans):
+        def at(c, dr, dc):
+            return src(c, MARGIN + dr, rows, MARGIN + dc, cols)
+
+        def at_p(dr, dc):
+            return dst_p[pl.ds(MARGIN + dr, rows), pl.ds(MARGIN + dc, cols)]
+
+        def dx(g):
+            return (8.0 * (g(0, 1) - g(0, -1)) - (g(0, 2) - g(0, -2))) / 12.0
+
+        def dy(g):
+            return (8.0 * (g(1, 0) - g(-1, 0)) - (g(2, 0) - g(-2, 0))) / 12.0
+
+        def field(c):
+            return lambda dr, dc: at(c, dr, dc)
+
+        def lap(g):
+            return g(0, 1) + g(0, -1) + g(1, 0) + g(-1, 0) - 4.0 * g(0, 0)
+
+        heat_c, salt_c, u_c, v_c = chans
+        east_v, north_v = at(u_c, 0, 0), at(v_c, 0, 0)
+
+        def adv(g):
+            return east_v * dx(g) + north_v * dy(g)
+
+        t, sa, u, v = field(heat_c), field(salt_c), field(u_c), field(v_c)
+        heat = wet * (t(0, 0) + TIME_INCREMENT * (SCALAR_MIXING * lap(t) - adv(t)))
+        salt = wet * (sa(0, 0) + TIME_INCREMENT * (SCALAR_MIXING * lap(sa) - adv(sa)))
+        new_u = wet * (
+            east_v + TIME_INCREMENT * (cor * north_v - dx(at_p) - adv(u) + VISCOSITY * lap(u))
+        )
+        new_v = wet * (
+            north_v + TIME_INCREMENT * (-cor * east_v - dy(at_p) - adv(v) + VISCOSITY * lap(v))
+        )
+        return heat, salt, new_u, new_v
+
+    def level(k, carry):
+        kf = k.astype(jnp.float32)
+
+        def wide_at(c, r0, nr, c0, nc):
+            return wide_ref[c, pl.ds(r0, nr), pl.ds(c0, nc)]
+
+        chans = (k, level_count + k, 2 * level_count + k, 3 * level_count + k)
+        sum1_ref[...] += HALINE * wide_ref[chans[1]] - THERMAL * wide_ref[chans[0]]
+        p1_ref[...] = GRAVITY * sum1_ref[...]
+        depth1 = wide_ref[depth_ch, pl.ds(MARGIN, rows1), pl.ds(MARGIN, cols1)]
+        wet1 = jnp.where(kf < depth1, 1.0, 0.0)
+        keep = keep1_ref[...]
+        once = stencils(wide_at, p1_ref, wet1, cor1_ref[...], rows1, cols1, chans)
+        for f in range(n_fields):
+            once_ref[f] = jnp.where(keep > 0.5, once[f], 0.0)
+
+        def once_at(c, r0, nr, c0, nc):
+            return once_ref[c, pl.ds(r0, nr), pl.ds(c0, nc)]
+
+        sum2_ref[...] += HALINE * once_ref[1] - THERMAL * once_ref[0]
+        p2_ref[...] = GRAVITY * sum2_ref[...]
+        depth2 = wide_ref[depth_ch, pl.ds(2 * MARGIN, rows2), pl.ds(2 * MARGIN, cols2)]
+        wet2 = jnp.where(kf < depth2, 1.0, 0.0)
+        twice = stencils(once_at, p2_ref, wet2, cor2_ref[...], rows2, cols2, (0, 1, 2, 3))
+        for f in range(n_fields):
+            out_ref[f, k] = twice[f]
+        return carry
+
+    lax.fori_loop(0, level_count, level, 0)
+
+
 def shards(state, sea_mask, levels):
     n_fields, level_count, tile_rows, tile_cols = state.shape
     depth_index = jnp.arange(level_count, dtype=jnp.int32)[:, None, None]
@@ -105,20 +182,28 @@
     lat = lax.axis_index("lat")
     total = lax.axis_size("lat") * tile_rows
     first_row = lat * tile_rows
-
-    grown = wide[:, MARGIN:-MARGIN, MARGIN:-MARGIN]
-    grown_depth = grown[-1]
-    grown_wet = (depth_index < grown_depth[None]).astype(jnp.float32)
     grown_rows = first_row - MARGIN + jnp.arange(tile_rows + 2 * MARGIN, dtype=jnp.int32)
-    fields = wide[:-1].reshape(n_fields, level_count, *wide.shape[1:])
-    once = advance(fields, grown_wet, coriolis(grown_rows, total))
-    south_edge = (lat == 0) & (grown_rows < 0)
-    once = jnp.where(south_edge[:, None], 0.0, once)
-
-    wet = (depth_index < depth[None]).astype(jnp.float32)
+    grown_cols = tile_cols + 2 * MARGIN
+    cor1 = jnp.broadcast_to(coriolis(grown_rows, total), (tile_rows + 2 * MARGIN, grown_cols))
+    keep1 = jnp.broadcast_to(
+        jnp.where((lat == 0) & (grown_rows < 0), 0.0, 1.0)[:, None], cor1.shape
+    )
     own_rows = first_row + jnp.arange(tile_rows, dtype=jnp.int32)
-    return advance(once, wet, coriolis(own_rows, total))
-
+    cor2 = jnp.broadcast_to(coriolis(own_rows, total), (tile_rows, tile_cols))
+    grown = (n_fields, tile_rows + 2 * MARGIN, grown_cols)
+    wide_shape = (tile_rows + 2 * WIDE, tile_cols + 2 * WIDE)
+    return pl.pallas_call(
+        two_steps_kernel,
+        out_shape=jax.ShapeDtypeStruct(state.shape, jnp.float32),
+        scratch_shapes=[
+            pltpu.VMEM(grown, jnp.float32),
+            pltpu.VMEM(wide_shape, jnp.float32),
+            pltpu.VMEM(wide_shape, jnp.float32),
+            pltpu.VMEM(grown[1:], jnp.float32),
+            pltpu.VMEM(grown[1:], jnp.float32),
+        ],
+        interpret=INTERPRET,
+    )(wide, cor1, keep1, cor2)
 
 def solution(mesh):
     return jax.shard_map(

time: 59.2 us -> 83.2 us (1.41)
  Pallas kernels: 0 us -> 28.3 us
  other arithmetic: 12.9 us -> 5.46 us
  local copies, waits for them, and re-layouts: 3.94 us -> 5.81 us
    pallas_call x0 -> x1, Pallas kernels: none -> 28.3 us  [shards(): pl.pallas_call(two_steps_kernel, out_shape=jax.ShapeDtypeStruct(state.sha...]
    another operation x11 -> x0, other arithmetic: 8.34 us -> none  [the longest x9 8.04 us: advance(): return jnp.stack([heat, salt, u, v])]
    broadcast_in_dim x0 -> x3, local copies, waits for them, and re-layouts: none -> 1.99 us  [the longest x1 0.67 us: shards(): jnp.broadcast_to(coriolis(grown_rows, total), (tile_rows + 2 * MARGIN, gr...]
    concatenate x1, other arithmetic: 1.22 us -> 2.41 us  [gather_wide(): return jnp.concatenate([west, lat_wide, east], axis=2)]
    ppermute x1, waiting for transfers between devices: 10.9 us -> 12.1 us  [gather_wide(): lax.ppermute(jnp.where(lon_odd, east_cols, west_cols), 'lon', across)]
    ppermute x1, starting transfers between devices: 5.04 us -> 5.95 us  [gather_wide(): lax.ppermute(jnp.where(lon_odd, east_cols, west_cols), 'lon', across)]
where the time goes in v8:
time: 83.2 us; the launch traced here: 83 us
  Pallas kernels  28.3 us (34%)
  starting transfers between devices  24.1 us (29%)
  waiting for transfers between devices  19.2 us (23%)
  local copies, waits for them, and re-layouts  5.81 us (7%)
  other arithmetic  5.46 us (7%)
    pallas_call x1, Pallas kernels, shards(): pl.pallas_call(two_steps_kernel, out_shape=jax.ShapeDtypeStruct(state.sha...  28.3 us
    ppermute x1, starting transfers between devices, gather_wide(): lax.ppermute(jnp.where(odd, bottom_rows, top_rows), ('lon', 'lat'), [(l *...  14.1 us
    ppermute x1, waiting for transfers between devices, gather_wide(): lax.ppermute(jnp.where(lon_odd, east_cols, west_cols), 'lon', across)  12.1 us
    ppermute x1, waiting for transfers between devices, gather_wide(): lax.ppermute(jnp.where(odd, bottom_rows, top_rows), ('lon', 'lat'), [(l *...  7.07 us
    ppermute x1, starting transfers between devices, gather_wide(): lax.ppermute(jnp.where(lon_odd, east_cols, west_cols), 'lon', across)  5.95 us
    concatenate x1, other arithmetic, gather_wide(): return jnp.concatenate([west, lat_wide, east], axis=2)  2.41 us
    ppermute x1, starting transfers between devices, gather_wide(): lax.ppermute(jnp.where(odd, top_rows, bottom_rows), ('lon', 'lat'), pairs)  2.02 us
    ppermute x1, starting transfers between devices, gather_wide(): lax.ppermute(jnp.where(lon_odd, west_cols, east_cols), 'lon', [(m, m ^ 1)...  2 us
  transfers between devices with their start and end apart: 4, of which 2 were waited for; matrix products, arithmetic and copies ran while one was open for 2% of the time, Pallas kernels for 0%

profile of v8, /device:TPU:192, one launch (start us, length us, event | category | flops | bytes accessed | tf_op | source)
XLA Modules:
  0.0 83.0 jit_solution(16488882474783832762)
XLA Ops:
  0.0 0.8 convert_bitcast_fusion
  0.8 1.5 %broadcast_select_fusion.1 = (f32[101,4,128]{2,1,0:T(4,128)S(1)}, f32[101,4,128]{2,1,0:T(4,128)S(1)}) fusion(pred[]{:T(512)S(6)} %eq.22, f32[1,8,128]{2,1,0:T(8,128)S(1)} %convert_bitcast_fusion, f32[100,8,128]{2,1,0:T(8,128)} %bitcast.3), kind=kLoop, calls=%fused_computation.10 | loop fusion | flops 258560 | bytes 827393 | tf_op jit(solution)/shard_map/jit(_where)/select_n | solution.py:37
  2.2 2.0 %collective-permute-start.1 = (f32[101,4,128]{2,1,0:T(4,128)S(1)}, f32[101,4,128]{2,1,0:T(4,128)S(1)}, u32[]{:S(2)}, u32[]{:S(2)}) collective-permute-start(f32[101,4,128]{2,1,0:T(4,128)S(1)} %get-tuple-element.9), channel_id=1, source_target_pairs={{1,2},{3,4},{5,6},{2,1},{4,3},{6,5},{9,10},{11,12},{13,14},{10,9},... | collective-permute-start | bytes 620552 | tf_op jit(solution)/shard_map/ppermute | solution.py:37
  4.3 14.1 %collective-permute-start = (f32[101,4,128]{2,1,0:T(4,128)S(1)}, f32[101,4,128]{2,1,0:T(4,128)S(1)}, u32[]{:S(2)}, u32[]{:S(2)}) collective-permute-start(f32[101,4,128]{2,1,0:T(4,128)S(1)} %get-tuple-element.10), channel_id=1, source_target_pairs={{0,1},{1,0},{2,3},{3,2},{4,5},{5,4},{6,7},{7,6},{8,9},{9,8},{10,11... | collective-permute-start | bytes 620552 | tf_op jit(solution)/shard_map/ppermute | solution.py:38
  18.4 0.7 broadcast_in_dim.39
  19.1 0.1 reshape.51
  19.2 0.1 pad_maximum_fusion.3
  19.3 0.4 rev.4
  19.8 7.1 %collective-permute-done = f32[101,4,128]{2,1,0:T(4,128)S(1)} collective-permute-done((f32[101,4,128]{2,1,0:T(4,128)S(1)}, f32[101,4,128]{2,1,0:T(4,128)S(1)}, u32[]{:S(2)}, u32[]{:S(2)}) %collective-permute-start) | collective-permute-done | bytes 206880 | tf_op jit(solution)/shard_map/ppermute | solution.py:38
  26.8 0.2 broadcast_select_fusion
  27.1 0.2 pad_maximum_fusion.1
  27.2 0.3 slice_select_fusion.1
  27.5 0.4 select_n.106
  27.9 2.0 %collective-permute-start.2 = (f32[6464]{0:T(1024)S(1)}, f32[6464]{0:T(1024)S(1)}, u32[]{:S(2)}, u32[]{:S(2)}) collective-permute-start(f32[6464]{0:T(1024)S(1)} %select_n.106), channel_id=1, source_target_pairs={{0,8},{8,0},{16,24},{24,16},{32,40},{40,32},{48,56},{56,48},{64,72... | collective-permute-start | bytes 77576 | tf_op jit(solution)/shard_map/ppermute | solution.py:53
  30.0 0.4 select_n.108
  30.4 6.0 %collective-permute-start.3 = (f32[6464]{0:T(1024)S(1)}, f32[6464]{0:T(1024)S(1)}, u32[]{:S(2)}, u32[]{:S(2)}) collective-permute-start(f32[6464]{0:T(1024)S(1)} %select_n.108), channel_id=1, source_target_pairs={{8,16},{24,32},{40,48},{56,64},{72,80},{88,96},{104,112},{120,128}... | collective-permute-start | bytes 77576 | tf_op jit(solution)/shard_map/ppermute | solution.py:58
  36.4 12.1 %collective-permute-done.3 = f32[6464]{0:T(1024)S(1)} collective-permute-done((f32[6464]{0:T(1024)S(1)}, f32[6464]{0:T(1024)S(1)}, u32[]{:S(2)}, u32[]{:S(2)}) %collective-permute-start.3) | collective-permute-done | bytes 25888 | tf_op jit(solution)/shard_map/ppermute | solution.py:58
  48.5 0.8 %reshape.52 = f32[101,16,4]{2,1,0:T(8,128)S(1)} reshape(f32[6464]{0:T(1024)S(1)} %get-tuple-element.11) | data formatting | bytes 51712 | tf_op jit(solution)/shard_map/reshape | solution.py:59
  49.4 0.9 %reshape.53 = f32[101,16,4]{2,1,0:T(8,128)S(1)} reshape(f32[6464]{0:T(1024)S(1)} %get-tuple-element.12) | data formatting | bytes 51712 | tf_op jit(solution)/shard_map/reshape | solution.py:60
  50.2 2.4 %pad_maximum_fusion.wide_ref = f32[101,16,136]{2,1,0:T(8,128)} fusion(f32[101,16,4]{2,1,0:T(8,128)S(1)} %reshape.53, f32[101,4,128]{2,1,0:T(4,128)S(1)} %get-tuple-element.8, f32[1,8,128]{2,1,0:T(8,128)S(1)} %convert_bitcast_fusion, f32[100,8,128]{2,1,0:T(8,128)S(1)} %bitcast.5, f32[101,4,128]{2,1,0:T(4,128)S(1)} %get-tuple-element.7, f32[101,16,4]{2,1,0:T(8,128)S(1)} %reshape.52), kind=kLoop, calls=%fused_computation | loop fusion | flops 1098880 | bytes 1758208 | tf_op jit(solution)/shard_map/concatenate | solution.py:61
  52.6 0.7 broadcast_in_dim.40.cor1_ref
  53.3 0.7 broadcast_in_dim.43.keep1_ref
  54.0 0.7 broadcast_in_dim.44.cor2_ref
  54.6 28.3 %shard_map.46 = f32[4,25,8,128]{3,2,1,0:T(8,128)} custom-call(f32[101,16,136]{2,1,0:T(8,128)} %pad_maximum_fusion.wide_ref, f32[12,132]{1,0:T(8,128)} %broadcast_in_dim.40.cor1_ref, f32[12,132]{1,0:T(8,128)} %broadcast_in_dim.43.keep1_ref, f32[8,128]{1,0:T(8,128)} %broadcast_in_dim.44.cor2_ref), custom_call_target="tpu_custom_call" | custom-call | tf_op jit(solution)/shard_map/pallas_call | solution.py:195
  (7 shorter events, 0.1 us)
Async XLA Ops:
  0.0 27.0 %copy-start = (f32[4,25,8,128]{3,2,1,0:T(8,128)S(1)}, f32[4,25,8,128]{3,2,1,0:T(8,128)}, u32[]{:S(2)}) copy-start(f32[4,25,8,128]{3,2,1,0:T(8,128)} %param.4) | copy-start | bytes 1228804
  2.2 17.1 %collective-permute-start.1 = (f32[101,4,128]{2,1,0:T(4,128)S(1)}, f32[101,4,128]{2,1,0:T(4,128)S(1)}, u32[]{:S(2)}, u32[]{:S(2)}) collective-permute-start(f32[101,4,128]{2,1,0:T(4,128)S(1)} %get-tuple-element.9), channel_id=1, source_target_pairs={{1,2},{3,4},{5,6},{2,1},{4,3},{6,5},{9,10},{11,12},{13,14},{10,9},... | collective-permute-start | bytes 620552 | tf_op jit(solution)/shard_map/ppermute | solution.py:37
  4.3 22.6 %collective-permute-start = (f32[101,4,128]{2,1,0:T(4,128)S(1)}, f32[101,4,128]{2,1,0:T(4,128)S(1)}, u32[]{:S(2)}, u32[]{:S(2)}) collective-permute-start(f32[101,4,128]{2,1,0:T(4,128)S(1)} %get-tuple-element.10), channel_id=1, source_target_pairs={{0,1},{1,0},{2,3},{3,2},{4,5},{5,4},{6,7},{7,6},{8,9},{9,8},{10,11... | collective-permute-start | bytes 620552 | tf_op jit(solution)/shard_map/ppermute | solution.py:38
  27.9 8.5 %collective-permute-start.2 = (f32[6464]{0:T(1024)S(1)}, f32[6464]{0:T(1024)S(1)}, u32[]{:S(2)}, u32[]{:S(2)}) collective-permute-start(f32[6464]{0:T(1024)S(1)} %select_n.106), channel_id=1, source_target_pairs={{0,8},{8,0},{16,24},{24,16},{32,40},{40,32},{48,56},{56,48},{64,72... | collective-permute-start | bytes 77576 | tf_op jit(solution)/shard_map/ppermute | solution.py:53
  30.4 18.1 %collective-permute-start.3 = (f32[6464]{0:T(1024)S(1)}, f32[6464]{0:T(1024)S(1)}, u32[]{:S(2)}, u32[]{:S(2)}) collective-permute-start(f32[6464]{0:T(1024)S(1)} %select_n.108), channel_id=1, source_target_pairs={{8,16},{24,32},{40,48},{56,64},{72,80},{88,96},{104,112},{120,128}... | collective-permute-start | bytes 77576 | tf_op jit(solution)/shard_map/ppermute | solution.py:58

commit v9 on v5

--- a/solution.py
+++ b/solution.py
@@ -24,22 +24,22 @@
 
     lat = lax.axis_index("lat")
     odd = lat % 2 == 1
-    top_rows = x[:, -WIDE:, :]
-    bottom_rows = x[:, :WIDE, :]
     inner = [(i, i + 1) for i in range(1, n_lat - 1, 2)]
     inner = inner + [(j, i) for i, j in inner]
     top = n_lat - 1
     pairs = [(l * n_lat + i, l * n_lat + j) for l in range(n_lon) for i, j in inner]
     pairs = pairs + [(l * n_lat + top, (n_lon - 1 - l) * n_lat + top) for l in range(n_lon)]
-    to_even = lax.ppermute(jnp.where(odd, top_rows, bottom_rows), ("lon", "lat"), pairs)
+    to_even = lax.ppermute(x, ("lon", "lat"), pairs)
     to_odd = lax.ppermute(
-        jnp.where(odd, bottom_rows, top_rows),
+        x,
         ("lon", "lat"),
         [(l * n_lat + i, l * n_lat + (i ^ 1)) for l in range(n_lon) for i in range(n_lat)],
     )
-    folded = jnp.flip(to_even, axis=(1, 2)) * signs
-    north = jnp.where(odd, jnp.where(lat == top, folded, to_even), to_odd)
-    south = jnp.where(odd, to_odd, to_even)
+    folded = jnp.flip(to_even[:, -WIDE:, :], axis=(1, 2)) * signs
+    north = jnp.where(
+        odd, jnp.where(lat == top, folded, to_even[:, :WIDE, :]), to_odd[:, :WIDE, :]
+    )
+    south = jnp.where(odd, to_odd[:, -WIDE:, :], to_even[:, -WIDE:, :])
     lat_wide = jnp.concatenate([south, x, north], axis=1)
 
     lon = lax.axis_index("lon")

time: 59.2 us -> 67.4 us (1.14)
  waiting for transfers between devices: 18.6 us -> 26.8 us
    ppermute x2, waiting for transfers between devices: 7.6 us -> 16.1 us  [the longest x1 16.1 us: gather_wide(): lax.ppermute(x, ('lon', 'lat'), [(l * n_lat + i, l * n_lat + (i ^ 1)) for...]
    select_n x2 -> x1, other arithmetic: 1.64 us -> 0.25 us  [gather_wide(): south = jnp.where(odd, to_odd[:, -WIDE:, :], to_even[:, -WIDE:, :])]
    concatenate x0 -> x1, other arithmetic: none -> 1.03 us  [shards(): jnp.concatenate([state.reshape(n_fields * level_count, tile_rows, tile_co...]
where the time goes in v9:
time: 67.4 us; the launch traced here: 67.1 us
  waiting for transfers between devices  26.8 us (40%)
  starting transfers between devices  23.6 us (35%)
  other arithmetic  12.6 us (19%)
  local copies, waits for them, and re-layouts  3.99 us (6%)
    ppermute x1, waiting for transfers between devices, gather_wide(): lax.ppermute(x, ('lon', 'lat'), [(l * n_lat + i, l * n_lat + (i ^ 1)) for...  16.1 us
    ppermute x1, starting transfers between devices, gather_wide(): lax.ppermute(x, ('lon', 'lat'), [(l * n_lat + i, l * n_lat + (i ^ 1)) for...  14.1 us
    ppermute x1, waiting for transfers between devices, gather_wide(): lax.ppermute(jnp.where(lon_odd, east_cols, west_cols), 'lon', across)  10.6 us
    another operation x9, other arithmetic, advance(): return jnp.stack([heat, salt, u, v])  8.04 us
    ppermute x1, starting transfers between devices, gather_wide(): lax.ppermute(jnp.where(lon_odd, east_cols, west_cols), 'lon', across)  5.34 us
    ppermute x1, starting transfers between devices, gather_wide(): lax.ppermute(jnp.where(lon_odd, west_cols, east_cols), 'lon', [(m, m ^ 1)...  2.1 us
    ppermute x1, starting transfers between devices, gather_wide(): to_even = lax.ppermute(x, ('lon', 'lat'), pairs)  2.02 us
  transfers between devices with their start and end apart: 4, of which 2 were waited for; matrix products, arithmetic and copies ran while one was open for 2% of the time, Pallas kernels for 0%

profile of v9, /device:TPU:192, one launch (start us, length us, event | category | flops | bytes accessed | tf_op | source)
XLA Modules:
  0.0 67.1 jit_solution(672223063924364673)
XLA Ops:
  0.0 0.8 %select_convert_fusion = f32[8,128]{1,0:T(8,128)S(1)} fusion(s32[8,128]{1,0:T(8,128)} %param.6, s32[8,128]{1,0:T(8,128)} %param.5), kind=kLoop, calls=%fused_computation.177 | loop fusion | flops 3072 | bytes 12288 | tf_op jit(solution)/shard_map/convert_element_type | solution.py:99
  0.8 1.0 %pad_maximum_fusion.2 = f32[101,8,128]{2,1,0:T(8,128)S(1)} fusion(f32[1,8,128]{2,1,0:T(8,128)S(1)} %bitcast.42, f32[100,8,128]{2,1,0:T(8,128)} %bitcast.34), kind=kLoop, calls=%fused_computation.11 | loop fusion | flops 103424 | bytes 827392 | tf_op jit(solution)/shard_map/concatenate | solution.py:100
  1.8 2.0 %collective-permute-start.1 = (f32[101,8,128]{2,1,0:T(8,128)S(1)}, f32[101,8,128]{2,1,0:T(8,128)S(1)}, u32[]{:S(2)}, u32[]{:S(2)}) collective-permute-start(f32[101,8,128]{2,1,0:T(8,128)S(1)} %pad_maximum_fusion.2), channel_id=1, source_target_pairs={{1,2},{3,4},{5,6},{2,1},{4,3},{6,5},{9,10},{11,12},{13,14},{10,9},... | collective-permute-start | bytes 1241096 | tf_op jit(solution)/shard_map/ppermute | solution.py:32
  3.8 14.1 %collective-permute-start = (f32[101,8,128]{2,1,0:T(8,128)S(1)}, f32[101,8,128]{2,1,0:T(8,128)S(1)}, u32[]{:S(2)}, u32[]{:S(2)}) collective-permute-start(f32[101,8,128]{2,1,0:T(8,128)S(1)} %pad_maximum_fusion.2), channel_id=1, source_target_pairs={{0,1},{1,0},{2,3},{3,2},{4,5},{5,4},{6,7},{7,6},{8,9},{9,8},{10,11... | collective-permute-start | bytes 1241096 | tf_op jit(solution)/shard_map/ppermute | solution.py:33
  18.0 0.7 %broadcast_in_dim.34 = f32[4,25]{1,0:T(4,128)S(1)} broadcast(f32[4]{0:T(128)} %constant.124.clone), dimensions={0} | broadcast | bytes 416 | tf_op jit(solution)/shard_map/broadcast_in_dim | solution.py:102
  19.0 0.4 rev.4
  19.5 16.1 %collective-permute-done = f32[101,8,128]{2,1,0:T(8,128)S(1)} collective-permute-done((f32[101,8,128]{2,1,0:T(8,128)S(1)}, f32[101,8,128]{2,1,0:T(8,128)S(1)}, u32[]{:S(2)}, u32[]{:S(2)}) %collective-permute-start) | collective-permute-done | bytes 413728 | tf_op jit(solution)/shard_map/ppermute | solution.py:33
  36.3 0.4 select_n.100
  36.7 0.4 select_n.102
  37.2 5.3 %collective-permute-start.3 = (f32[6464]{0:T(1024)S(1)}, f32[6464]{0:T(1024)S(1)}, u32[]{:S(2)}, u32[]{:S(2)}) collective-permute-start(f32[6464]{0:T(1024)S(1)} %select_n.102), channel_id=1, source_target_pairs={{8,16},{24,32},{40,48},{56,64},{72,80},{88,96},{104,112},{120,128}... | collective-permute-start | bytes 77576 | tf_op jit(solution)/shard_map/ppermute | solution.py:55
  42.5 2.1 %collective-permute-start.2 = (f32[6464]{0:T(1024)S(1)}, f32[6464]{0:T(1024)S(1)}, u32[]{:S(2)}, u32[]{:S(2)}) collective-permute-start(f32[6464]{0:T(1024)S(1)} %select_n.100), channel_id=1, source_target_pairs={{0,8},{8,0},{16,24},{24,16},{32,40},{40,32},{48,56},{56,48},{64,72... | collective-permute-start | bytes 77576 | tf_op jit(solution)/shard_map/ppermute | solution.py:50
  44.6 10.6 %collective-permute-done.3 = f32[6464]{0:T(1024)S(1)} collective-permute-done((f32[6464]{0:T(1024)S(1)}, f32[6464]{0:T(1024)S(1)}, u32[]{:S(2)}, u32[]{:S(2)}) %collective-permute-start.3) | collective-permute-done | bytes 25888 | tf_op jit(solution)/shard_map/ppermute | solution.py:55
  55.3 0.8 %reshape.72 = f32[101,16,4]{2,1,0:T(8,128)S(1)} reshape(f32[6464]{0:T(1024)S(1)} %get-tuple-element.13) | data formatting | bytes 51712 | tf_op jit(solution)/shard_map/reshape | solution.py:56
  56.1 0.9 %reshape.73 = f32[101,16,4]{2,1,0:T(8,128)S(1)} reshape(f32[6464]{0:T(1024)S(1)} %get-tuple-element.14) | data formatting | bytes 51712 | tf_op jit(solution)/shard_map/reshape | solution.py:57
  57.1 1.2 %pad_maximum_fusion = f32[101,16,136]{2,1,0:T(8,128)S(1)} fusion(f32[101,16,4]{2,1,0:T(8,128)S(1)} %reshape.73, f32[101,4,128]{2,1,0:T(4,128)S(1)} %get-tuple-element.12, f32[1,8,128]{2,1,0:T(8,128)S(1)} %bitcast.45, f32[100,8,128]{2,1,0:T(8,128)S(1)} %bitcast.37, f32[101,4,128]{2,1,0:T(4,128)S(1)} %get-tuple-element.11, f32[101,16,4]{2,1,0:T(8,128)S(1)} %reshape.72), kind=kLoop, calls=%fused_computation | loop fusion | flops 1098880 | bytes 1758208 | tf_op jit(solution)/shard_map/concatenate | solution.py:58
  58.5 1.3 %fusion = f32[1,25,12,132]{3,2,1,0:T(8,128)S(1)} fusion(f32[101,16,136]{2,1,0:T(8,128)S(1)} %pad_maximum_fusion, f32[101,16,4]{2,1,0:T(8,128)S(1)} %reshape.72, f32[101,4,128]{2,1,0:T(4,128)S(1)} %get-tuple-element.12, f32[101,4,128]{2,1,0:T(4,128)S(1)} %get-tuple-element.11, f32[1,8,128]{2,1,0:T(8,128)S(1)} %bitcast.46, f32[100,8,128]{2,1,0:T(8,128)S(1)} %bitcast.38, ...), kind=kLoop, calls=%fused_computation.12 | loop fusion | flops 1267200 | bytes 2469540 | tf_op jit(solution)/shard_map/stack | solution.py:93
  59.8 1.3 %fusion.1 = f32[1,25,12,132]{3,2,1,0:T(8,128)S(1)} fusion(f32[101,16,136]{2,1,0:T(8,128)S(1)} %pad_maximum_fusion, f32[101,16,4]{2,1,0:T(8,128)S(1)} %reshape.72, f32[101,4,128]{2,1,0:T(4,128)S(1)} %get-tuple-element.12, f32[101,4,128]{2,1,0:T(4,128)S(1)} %get-tuple-element.11, f32[1,8,128]{2,1,0:T(8,128)S(1)} %bitcast.47, f32[100,8,128]{2,1,0:T(8,128)S(1)} %bitcast.39, ...), kind=kLoop, calls=%fused_computation.13 | loop fusion | flops 1267200 | bytes 2469540 | tf_op jit(solution)/shard_map/stack | solution.py:93
  61.1 1.5 %fusion.2 = f32[1,25,12,132]{3,2,1,0:T(8,128)S(1)} fusion(f32[101,16,136]{2,1,0:T(8,128)S(1)} %pad_maximum_fusion, f32[101,16,4]{2,1,0:T(8,128)S(1)} %reshape.72, f32[101,4,128]{2,1,0:T(4,128)S(1)} %get-tuple-element.12, f32[101,4,128]{2,1,0:T(4,128)S(1)} %get-tuple-element.11, f32[1,8,128]{2,1,0:T(8,128)S(1)} %bitcast.48, f32[100,8,128]{2,1,0:T(8,128)S(1)} %bitcast.40, ...), kind=kLoop, calls=%fused_computation.14 | loop fusion | flops 1584000 | bytes 2944788 | tf_op jit(solution)/shard_map/stack | solution.py:93
  62.6 1.6 %fusion.3 = f32[1,25,12,132]{3,2,1,0:T(8,128)S(1)} fusion(f32[101,16,136]{2,1,0:T(8,128)S(1)} %pad_maximum_fusion, f32[101,16,4]{2,1,0:T(8,128)S(1)} %reshape.72, f32[101,4,128]{2,1,0:T(4,128)S(1)} %get-tuple-element.12, f32[101,4,128]{2,1,0:T(4,128)S(1)} %get-tuple-element.11, f32[1,8,128]{2,1,0:T(8,128)S(1)} %bitcast.49, f32[100,8,128]{2,1,0:T(8,128)S(1)} %bitcast.41, ...), kind=kLoop, calls=%fused_computation.15 | loop fusion | flops 1584000 | bytes 2944788 | tf_op jit(solution)/shard_map/stack | solution.py:93
  64.7 0.4 fusion.64
  65.1 0.4 fusion.66
  65.5 0.4 fusion.67
  66.0 0.4 fusion.65
  66.3 0.8 %pad_maximum_fusion.11 = f32[4,25,8,128]{3,2,1,0:T(8,128)} fusion(f32[1,25,8,128]{3,2,1,0:T(8,128)S(1)} %fusion.67, f32[1,25,8,128]{3,2,1,0:T(8,128)S(1)} %fusion.66, f32[1,25,8,128]{3,2,1,0:T(8,128)S(1)} %fusion.65, f32[1,25,8,128]{3,2,1,0:T(8,128)S(1)} %fusion.64), kind=kLoop, calls=%fused_computation.93 | loop fusion | flops 307200 | bytes 819200 | tf_op jit(solution)/shard_map/stack | solution.py:93
  (20 shorter events, 1.8 us)
Async XLA Ops:
  0.0 35.8 %copy-start = (f32[4,25,8,128]{3,2,1,0:T(8,128)S(1)}, f32[4,25,8,128]{3,2,1,0:T(8,128)}, u32[]{:S(2)}) copy-start(f32[4,25,8,128]{3,2,1,0:T(8,128)} %param.4) | copy-start | bytes 1228804
  1.8 17.2 %collective-permute-start.1 = (f32[101,8,128]{2,1,0:T(8,128)S(1)}, f32[101,8,128]{2,1,0:T(8,128)S(1)}, u32[]{:S(2)}, u32[]{:S(2)}) collective-permute-start(f32[101,8,128]{2,1,0:T(8,128)S(1)} %pad_maximum_fusion.2), channel_id=1, source_target_pairs={{1,2},{3,4},{5,6},{2,1},{4,3},{6,5},{9,10},{11,12},{13,14},{10,9},... | collective-permute-start | bytes 1241096 | tf_op jit(solution)/shard_map/ppermute | solution.py:32
  3.8 31.7 %collective-permute-start = (f32[101,8,128]{2,1,0:T(8,128)S(1)}, f32[101,8,128]{2,1,0:T(8,128)S(1)}, u32[]{:S(2)}, u32[]{:S(2)}) collective-permute-start(f32[101,8,128]{2,1,0:T(8,128)S(1)} %pad_maximum_fusion.2), channel_id=1, source_target_pairs={{0,1},{1,0},{2,3},{3,2},{4,5},{5,4},{6,7},{7,6},{8,9},{9,8},{10,11... | collective-permute-start | bytes 1241096 | tf_op jit(solution)/shard_map/ppermute | solution.py:33
  37.2 18.1 %collective-permute-start.3 = (f32[6464]{0:T(1024)S(1)}, f32[6464]{0:T(1024)S(1)}, u32[]{:S(2)}, u32[]{:S(2)}) collective-permute-start(f32[6464]{0:T(1024)S(1)} %select_n.102), channel_id=1, source_target_pairs={{8,16},{24,32},{40,48},{56,64},{72,80},{88,96},{104,112},{120,128}... | collective-permute-start | bytes 77576 | tf_op jit(solution)/shard_map/ppermute | solution.py:55
  42.5 12.8 %collective-permute-start.2 = (f32[6464]{0:T(1024)S(1)}, f32[6464]{0:T(1024)S(1)}, u32[]{:S(2)}, u32[]{:S(2)}) collective-permute-start(f32[6464]{0:T(1024)S(1)} %select_n.100), channel_id=1, source_target_pairs={{0,8},{8,0},{16,24},{24,16},{32,40},{40,32},{48,56},{56,48},{64,72... | collective-permute-start | bytes 77576 | tf_op jit(solution)/shard_map/ppermute | solution.py:50

commit v10 on v5

--- a/solution.py
+++ b/solution.py
@@ -18,14 +18,15 @@
     return (1.2 * jnp.sin(-1.3 + 2.8 * (mirrored.astype(jnp.float32) + 0.5) / total))[:, None]
 
 
-def gather_wide(x, signs):
+def lat_exchange(x, signs, far):
     n_lon = lax.axis_size("lon")
     n_lat = lax.axis_size("lat")
-
     lat = lax.axis_index("lat")
     odd = lat % 2 == 1
-    top_rows = x[:, -WIDE:, :]
-    bottom_rows = x[:, :WIDE, :]
+    rows = x.shape[1]
+    skip = MARGIN if far else 0
+    top_rows = x[:, rows - MARGIN - skip : rows - skip, :]
+    bottom_rows = x[:, skip : skip + MARGIN, :]
     inner = [(i, i + 1) for i in range(1, n_lat - 1, 2)]
     inner = inner + [(j, i) for i, j in inner]
     top = n_lat - 1
@@ -40,13 +41,16 @@
     folded = jnp.flip(to_even, axis=(1, 2)) * signs
     north = jnp.where(odd, jnp.where(lat == top, folded, to_even), to_odd)
     south = jnp.where(odd, to_odd, to_even)
-    lat_wide = jnp.concatenate([south, x, north], axis=1)
+    return south, north
 
+
+def lon_exchange(x):
+    n_lon = lax.axis_size("lon")
     lon = lax.axis_index("lon")
     lon_odd = lon % 2 == 1
-    edge_shape = lat_wide[..., :WIDE].shape
-    east_cols = lat_wide[..., -WIDE:].reshape(-1)
-    west_cols = lat_wide[..., :WIDE].reshape(-1)
+    edge_shape = x[..., :WIDE].shape
+    east_cols = x[..., -WIDE:].reshape(-1)
+    west_cols = x[..., :WIDE].reshape(-1)
     on_chip = lax.ppermute(
         jnp.where(lon_odd, west_cols, east_cols), "lon", [(m, m ^ 1) for m in range(n_lon)]
     )
@@ -55,7 +59,18 @@
     off_chip = lax.ppermute(jnp.where(lon_odd, east_cols, west_cols), "lon", across)
     west = jnp.where(lon_odd, on_chip, off_chip).reshape(edge_shape)
     east = jnp.where(lon_odd, off_chip, on_chip).reshape(edge_shape)
-    return jnp.concatenate([west, lat_wide, east], axis=2)
+    return west, east
+
+
+def gather_wide(x, signs):
+    south, north = lat_exchange(x, signs, False)
+    lat_wide = jnp.concatenate([south, x, north], axis=1)
+    west, east = lon_exchange(lat_wide)
+    tie = 0.0 * (south[:-1, :1, :1] + north[:-1, :1, :1])
+    far_south, far_north = lat_exchange(x[:-1] + tie, signs[:-1], True)
+    middle = jnp.concatenate([west, lat_wide, east], axis=2)
+    fill = ((0, 1), (0, 0), (WIDE, WIDE))
+    return jnp.concatenate([jnp.pad(far_south, fill), middle, jnp.pad(far_north, fill)], axis=1)
 
 
 def advance(f, wet, cor):

time: 59.2 us -> 77.7 us (1.31)
  the two profiles are of different devices: /device:TPU:192 before, /device:TPU:225 now
where the time goes in v10:
time: 77.7 us; the launch traced here: 77.4 us
  starting transfers between devices  38.9 us (50%)
  other arithmetic  20.6 us (27%)
  waiting for transfers between devices  14.1 us (18%)
  local copies, waits for them, and re-layouts  3.41 us (4%)
    ppermute x2, starting transfers between devices, lat_exchange(): lax.ppermute(jnp.where(odd, top_rows, bottom_rows), ('lon', 'lat'), pairs)  19.6 us
    ppermute x2, waiting for transfers between devices, lat_exchange(): lax.ppermute(jnp.where(odd, top_rows, bottom_rows), ('lon', 'lat'), pairs)  14.1 us
    ppermute x1, starting transfers between devices, lon_exchange(): lax.ppermute(jnp.where(lon_odd, west_cols, east_cols), 'lon', [(m, m ^ 1)...  13.1 us
    another operation x9, other arithmetic, advance(): return jnp.stack([heat, salt, u, v])  8.02 us
    concatenate x2, other arithmetic, gather_wide(): jnp.concatenate([jnp.pad(far_south, fill), middle, jnp.pad(far_north, fil...  5.52 us
    ppermute x2, starting transfers between devices, lat_exchange(): lax.ppermute(jnp.where(odd, bottom_rows, top_rows), ('lon', 'lat'), [(l *...  3.84 us
    ppermute x1, starting transfers between devices, lon_exchange(): lax.ppermute(jnp.where(lon_odd, east_cols, west_cols), 'lon', across)  2.36 us
    concatenate x1, other arithmetic, gather_wide(): middle = jnp.concatenate([west, lat_wide, east], axis=2)  2.35 us
  transfers between devices with their start and end apart: 6, of which 2 were waited for; matrix products, arithmetic and copies ran while one was open for 6% of the time, Pallas kernels for 0%

profile of v10, /device:TPU:225, one launch (start us, length us, event | category | flops | bytes accessed | tf_op | source)
XLA Modules:
  0.0 77.4 jit_solution(11526707855819339814)
XLA Ops:
  0.0 0.8 select_convert_fusion
  0.8 1.2 %broadcast_select_fusion.1 = (f32[101,2,128]{2,1,0:T(2,128)S(1)}, f32[101,2,128]{2,1,0:T(2,128)S(1)}, f32[101,2,128]{2,1,0:T(2,128)S(1)}) fusion(pred[]{:T(512)S(6)} %eq.28, f32[1,8,128]{2,1,0:T(8,128)S(1)} %bitcast.45, f32[100,8,128]{2,1,0:T(8,128)} %bitcast.35), kind=kLoop, calls=%fused_computation.112 | loop fusion | flops 77568 | bytes 723969 | tf_op jit(solution)/shard_map/jit(_where)/select_n | solution.py:35
  2.0 1.9 %collective-permute-start = (f32[101,2,128]{2,1,0:T(2,128)S(1)}, f32[101,2,128]{2,1,0:T(2,128)S(1)}, u32[]{:S(2)}, u32[]{:S(2)}) collective-permute-start(f32[101,2,128]{2,1,0:T(2,128)S(1)} %broadcast_select_fusion.2), channel_id=1, source_target_pairs={{0,1},{1,0},{2,3},{3,2},{4,5},{5,4},{6,7},{7,6},{8,9},{9,8},{10,11... | collective-permute-start | bytes 310280 | tf_op jit(solution)/shard_map/ppermute | solution.py:36
  4.0 14.1 %collective-permute-start.1 = (f32[101,2,128]{2,1,0:T(2,128)S(1)}, f32[101,2,128]{2,1,0:T(2,128)S(1)}, u32[]{:S(2)}, u32[]{:S(2)}) collective-permute-start(f32[101,2,128]{2,1,0:T(2,128)S(1)} %get-tuple-element.5), channel_id=1, source_target_pairs={{1,2},{3,4},{5,6},{2,1},{4,3},{6,5},{9,10},{11,12},{13,14},{10,9},... | collective-permute-start | bytes 310280 | tf_op jit(solution)/shard_map/ppermute | solution.py:35
  18.3 0.7 broadcast_in_dim.34
  19.2 5.0 %collective-permute-done.1 = f32[101,2,128]{2,1,0:T(2,128)S(1)} collective-permute-done((f32[101,2,128]{2,1,0:T(2,128)S(1)}, f32[101,2,128]{2,1,0:T(2,128)S(1)}, u32[]{:S(2)}, u32[]{:S(2)}) %collective-permute-start.1) | collective-permute-done | bytes 103456 | tf_op jit(solution)/shard_map/ppermute | solution.py:35
  24.2 0.4 rev.8
  24.8 0.8 %fusion.119 = f32[100]{0:T(128)S(1)} fusion(f32[101,2,128]{2,1,0:T(2,128)S(1)} %get-tuple-element.19, f32[101,2,128]{2,1,0:T(2,128)S(1)} %get-tuple-element.18), kind=kLoop, calls=%fused_computation.186 | loop fusion | flops 200 | bytes 1200 | tf_op jit(solution)/shard_map/mul | solution.py:69
  26.8 2.4 %collective-permute-start.3 = (f32[4848]{0:T(1024)S(1)}, f32[4848]{0:T(1024)S(1)}, u32[]{:S(2)}, u32[]{:S(2)}) collective-permute-start(f32[4848]{0:T(1024)S(1)} %select_n.140), channel_id=1, source_target_pairs={{8,16},{24,32},{40,48},{56,64},{72,80},{88,96},{104,112},{120,128}... | collective-permute-start | bytes 58184 | tf_op jit(solution)/shard_map/ppermute | solution.py:59
  29.1 13.1 %collective-permute-start.2 = (f32[4848]{0:T(1024)S(1)}, f32[4848]{0:T(1024)S(1)}, u32[]{:S(2)}, u32[]{:S(2)}) collective-permute-start(f32[4848]{0:T(1024)S(1)} %select_n.138), channel_id=1, source_target_pairs={{0,8},{8,0},{16,24},{24,16},{32,40},{40,32},{48,56},{56,48},{64,72... | collective-permute-start | bytes 58184 | tf_op jit(solution)/shard_map/ppermute | solution.py:54
  42.3 5.5 %collective-permute-start.4 = (f32[100,2,128]{2,1,0:T(2,128)S(1)}, f32[100,2,128]{2,1,0:T(2,128)S(1)}, u32[]{:S(2)}, u32[]{:S(2)}) collective-permute-start(f32[100,2,128]{2,1,0:T(2,128)S(1)} %get-tuple-element.16), channel_id=1, source_target_pairs={{1,2},{3,4},{5,6},{2,1},{4,3},{6,5},{9,10},{11,12},{13,14},{10,9},... | collective-permute-start | bytes 307208 | tf_op jit(solution)/shard_map/ppermute | solution.py:35
  47.8 1.9 %collective-permute-start.5 = (f32[100,2,128]{2,1,0:T(2,128)S(1)}, f32[100,2,128]{2,1,0:T(2,128)S(1)}, u32[]{:S(2)}, u32[]{:S(2)}) collective-permute-start(f32[100,2,128]{2,1,0:T(2,128)S(1)} %get-tuple-element.17), channel_id=1, source_target_pairs={{0,1},{1,0},{2,3},{3,2},{4,5},{5,4},{6,7},{7,6},{8,9},{9,8},{10,11... | collective-permute-start | bytes 307208 | tf_op jit(solution)/shard_map/ppermute | solution.py:36
  50.4 2.3 %pad_maximum_fusion = f32[101,12,136]{2,1,0:T(8,128)} fusion(f32[101,12,4]{2,1,0:T(8,128)S(1)} %reshape.76, f32[101,2,128]{2,1,0:T(2,128)S(1)} %get-tuple-element.19, f32[1,8,128]{2,1,0:T(8,128)S(1)} %bitcast.47, f32[100,8,128]{2,1,0:T(8,128)S(1)} %bitcast.37, f32[101,2,128]{2,1,0:T(2,128)S(1)} %get-tuple-element.18, f32[101,12,4]{2,1,0:T(8,128)S(1)} %reshape.75), kind=kLoop, calls=%fused_computation | loop fusion | flops 824160 | bytes 1318656 | tf_op jit(solution)/shard_map/concatenate | solution.py:71
  52.8 9.1 %collective-permute-done.4 = f32[100,2,128]{2,1,0:T(2,128)S(1)} collective-permute-done((f32[100,2,128]{2,1,0:T(2,128)S(1)}, f32[100,2,128]{2,1,0:T(2,128)S(1)}, u32[]{:S(2)}, u32[]{:S(2)}) %collective-permute-start.4) | collective-permute-done | bytes 102432 | tf_op jit(solution)/shard_map/ppermute | solution.py:35
  61.9 0.4 rev.9
  63.0 1.4 %pad_maximum_fusion.2 = f32[101,16,136]{2,1,0:T(8,128)S(1)} fusion(f32[101,2,136]{2,1,0:T(2,128)S(1)} %pad.7, f32[101,12,4]{2,1,0:T(8,128)S(1)} %reshape.76, f32[101,2,128]{2,1,0:T(2,128)S(1)} %get-tuple-element.19, f32[1,8,128]{2,1,0:T(8,128)S(1)} %bitcast.49, f32[100,8,128]{2,1,0:T(8,128)S(1)} %bitcast.39, f32[101,2,128]{2,1,0:T(2,128)S(1)} %get-tuple-element.18, ...), kind=kLoop, calls=%fused_computation.3 | loop fusion | flops 1538432 | bytes 1758208 | tf_op jit(solution)/shard_map/concatenate | solution.py:73
  64.5 4.1 %pad_maximum_fusion.1 = (f32[101,14,136]{2,1,0:T(8,128)S(1)}, f32[101,14,136]{2,1,0:T(8,128)S(1)}) fusion(f32[101,2,136]{2,1,0:T(2,128)S(1)} %pad.7, f32[101,12,4]{2,1,0:T(8,128)S(1)} %reshape.76, f32[101,2,128]{2,1,0:T(2,128)S(1)} %get-tuple-element.19, f32[1,8,128]{2,1,0:T(8,128)S(1)} %bitcast.50, f32[100,8,128]{2,1,0:T(8,128)S(1)} %bitcast.40, ...), kind=kLoop, calls=%fused_computation.1 | loop fusion | flops 2307648 | bytes 2417536 | tf_op jit(solution)/shard_map/concatenate | solution.py:73
  68.6 1.3 %fusion.1 = f32[1,25,12,132]{3,2,1,0:T(8,128)S(1)} fusion(f32[101,14,136]{2,1,0:T(8,128)S(1)} %get-tuple-element.9, f32[101,14,136]{2,1,0:T(8,128)S(1)} %get-tuple-element.8, f32[101,12,4]{2,1,0:T(8,128)S(1)} %reshape.75, f32[101,2,128]{2,1,0:T(2,128)S(1)} %get-tuple-element.19, f32[101,2,128]{2,1,0:T(2,128)S(1)} %get-tuple-element.18, ...), kind=kLoop, calls=%fused_computation.15 | loop fusion | flops 1267200 | bytes 2249764 | tf_op jit(solution)/shard_map/stack | solution.py:108
  69.9 1.3 %fusion = f32[1,25,12,132]{3,2,1,0:T(8,128)S(1)} fusion(f32[101,14,136]{2,1,0:T(8,128)S(1)} %get-tuple-element.9, f32[101,14,136]{2,1,0:T(8,128)S(1)} %get-tuple-element.8, f32[101,12,4]{2,1,0:T(8,128)S(1)} %reshape.75, f32[101,2,128]{2,1,0:T(2,128)S(1)} %get-tuple-element.19, f32[101,2,128]{2,1,0:T(2,128)S(1)} %get-tuple-element.18, ...), kind=kLoop, calls=%fused_computation.14 | loop fusion | flops 1267200 | bytes 2249764 | tf_op jit(solution)/shard_map/stack | solution.py:108
  71.3 1.5 %fusion.2 = f32[1,25,12,132]{3,2,1,0:T(8,128)S(1)} fusion(f32[101,14,136]{2,1,0:T(8,128)S(1)} %get-tuple-element.9, f32[101,14,136]{2,1,0:T(8,128)S(1)} %get-tuple-element.8, f32[101,12,4]{2,1,0:T(8,128)S(1)} %reshape.75, f32[101,2,128]{2,1,0:T(2,128)S(1)} %get-tuple-element.19, f32[101,2,128]{2,1,0:T(2,128)S(1)} %get-tuple-element.18, ...), kind=kLoop, calls=%fused_computation.16 | loop fusion | flops 1584000 | bytes 2725012 | tf_op jit(solution)/shard_map/stack | solution.py:108
  72.8 1.6 %fusion.3 = f32[1,25,12,132]{3,2,1,0:T(8,128)S(1)} fusion(f32[101,14,136]{2,1,0:T(8,128)S(1)} %get-tuple-element.9, f32[101,14,136]{2,1,0:T(8,128)S(1)} %get-tuple-element.8, f32[101,12,4]{2,1,0:T(8,128)S(1)} %reshape.75, f32[101,2,128]{2,1,0:T(2,128)S(1)} %get-tuple-element.19, f32[101,2,128]{2,1,0:T(2,128)S(1)} %get-tuple-element.18, ...), kind=kLoop, calls=%fused_computation.17 | loop fusion | flops 1584000 | bytes 2725012 | tf_op jit(solution)/shard_map/stack | solution.py:108
  75.4 0.4 fusion.66
  75.8 0.4 fusion.67
  76.6 0.8 %pad_maximum_fusion.12 = f32[4,25,8,128]{3,2,1,0:T(8,128)} fusion(f32[1,25,8,128]{3,2,1,0:T(8,128)S(1)} %fusion.67, f32[1,25,8,128]{3,2,1,0:T(8,128)S(1)} %fusion.66, f32[1,25,8,128]{3,2,1,0:T(8,128)S(1)} %fusion.65, f32[1,25,8,128]{3,2,1,0:T(8,128)S(1)} %fusion.64), kind=kLoop, calls=%fused_computation.95 | loop fusion | flops 307200 | bytes 819200 | tf_op jit(solution)/shard_map/stack | solution.py:108
  (35 shorter events, 4.5 us)
Async XLA Ops:
  0.0 25.7 %copy-start = (f32[4,25,8,128]{3,2,1,0:T(8,128)S(1)}, f32[4,25,8,128]{3,2,1,0:T(8,128)}, u32[]{:S(2)}) copy-start(f32[4,25,8,128]{3,2,1,0:T(8,128)} %param.4) | copy-start | bytes 1228804
  2.0 22.6 %collective-permute-start = (f32[101,2,128]{2,1,0:T(2,128)S(1)}, f32[101,2,128]{2,1,0:T(2,128)S(1)}, u32[]{:S(2)}, u32[]{:S(2)}) collective-permute-start(f32[101,2,128]{2,1,0:T(2,128)S(1)} %broadcast_select_fusion.2), channel_id=1, source_target_pairs={{0,1},{1,0},{2,3},{3,2},{4,5},{5,4},{6,7},{7,6},{8,9},{9,8},{10,11... | collective-permute-start | bytes 310280 | tf_op jit(solution)/shard_map/ppermute | solution.py:36
  4.0 20.2 %collective-permute-start.1 = (f32[101,2,128]{2,1,0:T(2,128)S(1)}, f32[101,2,128]{2,1,0:T(2,128)S(1)}, u32[]{:S(2)}, u32[]{:S(2)}) collective-permute-start(f32[101,2,128]{2,1,0:T(2,128)S(1)} %get-tuple-element.5), channel_id=1, source_target_pairs={{1,2},{3,4},{5,6},{2,1},{4,3},{6,5},{9,10},{11,12},{13,14},{10,9},... | collective-permute-start | bytes 310280 | tf_op jit(solution)/shard_map/ppermute | solution.py:35
  26.8 22.9 %collective-permute-start.3 = (f32[4848]{0:T(1024)S(1)}, f32[4848]{0:T(1024)S(1)}, u32[]{:S(2)}, u32[]{:S(2)}) collective-permute-start(f32[4848]{0:T(1024)S(1)} %select_n.140), channel_id=1, source_target_pairs={{8,16},{24,32},{40,48},{56,64},{72,80},{88,96},{104,112},{120,128}... | collective-permute-start | bytes 58184 | tf_op jit(solution)/shard_map/ppermute | solution.py:59
  29.1 20.6 %collective-permute-start.2 = (f32[4848]{0:T(1024)S(1)}, f32[4848]{0:T(1024)S(1)}, u32[]{:S(2)}, u32[]{:S(2)}) collective-permute-start(f32[4848]{0:T(1024)S(1)} %select_n.138), channel_id=1, source_target_pairs={{0,8},{8,0},{16,24},{24,16},{32,40},{40,32},{48,56},{56,48},{64,72... | collective-permute-start | bytes 58184 | tf_op jit(solution)/shard_map/ppermute | solution.py:54
  42.3 19.6 %collective-permute-start.4 = (f32[100,2,128]{2,1,0:T(2,128)S(1)}, f32[100,2,128]{2,1,0:T(2,128)S(1)}, u32[]{:S(2)}, u32[]{:S(2)}) collective-permute-start(f32[100,2,128]{2,1,0:T(2,128)S(1)} %get-tuple-element.16), channel_id=1, source_target_pairs={{1,2},{3,4},{5,6},{2,1},{4,3},{6,5},{9,10},{11,12},{13,14},{10,9},... | collective-permute-start | bytes 307208 | tf_op jit(solution)/shard_map/ppermute | solution.py:35
  47.8 14.5 %collective-permute-start.5 = (f32[100,2,128]{2,1,0:T(2,128)S(1)}, f32[100,2,128]{2,1,0:T(2,128)S(1)}, u32[]{:S(2)}, u32[]{:S(2)}) collective-permute-start(f32[100,2,128]{2,1,0:T(2,128)S(1)} %get-tuple-element.17), channel_id=1, source_target_pairs={{0,1},{1,0},{2,3},{3,2},{4,5},{5,4},{6,7},{7,6},{8,9},{9,8},{10,11... | collective-permute-start | bytes 307208 | tf_op jit(solution)/shard_map/ppermute | solution.py:36
  64.4 4.1 %copy-start.1 = (f32[101,12,136]{2,1,0:T(8,128)S(1)}, f32[101,12,136]{2,1,0:T(8,128)}, u32[]{:S(2)}) copy-start(f32[101,12,136]{2,1,0:T(8,128)} %pad_maximum_fusion) | copy-start | bytes 1977988

commit v11 on v5

--- a/solution.py
+++ b/solution.py
@@ -55,7 +55,9 @@
     off_chip = lax.ppermute(jnp.where(lon_odd, east_cols, west_cols), "lon", across)
     west = jnp.where(lon_odd, on_chip, off_chip).reshape(edge_shape)
     east = jnp.where(lon_odd, off_chip, on_chip).reshape(edge_shape)
-    return jnp.concatenate([west, lat_wide, east], axis=2)
+    wide_state = jnp.concatenate([west[:-1], lat_wide[:-1], east[:-1]], axis=2)
+    wide_depth = jnp.concatenate([west[-1], lat_wide[-1], east[-1]], axis=1)
+    return wide_state, wide_depth
 
 
 def advance(f, wet, cor):
@@ -75,23 +77,16 @@
         return at(g, 0, 1) + at(g, 0, -1) + at(g, 1, 0) + at(g, -1, 0) - 4.0 * at(g, 0, 0)
 
     pressure = GRAVITY * jnp.cumsum(HALINE * f[1] - THERMAL * f[0], axis=0)
-    east_v, north_v = at(f[2], 0, 0), at(f[3], 0, 0)
-
-    def adv(g):
-        return east_v * dx(g) + north_v * dy(g)
-
-    heat = wet * (at(f[0], 0, 0) + TIME_INCREMENT * (SCALAR_MIXING * lap(f[0]) - adv(f[0])))
-    salt = wet * (at(f[1], 0, 0) + TIME_INCREMENT * (SCALAR_MIXING * lap(f[1]) - adv(f[1])))
-    u = wet * (
-        east_v
-        + TIME_INCREMENT * (cor * north_v - dx(pressure) - adv(f[2]) + VISCOSITY * lap(f[2]))
+    centre = at(f, 0, 0)
+    east_v, north_v = centre[2], centre[3]
+    advection = east_v * dx(f) + north_v * dy(f)
+    mixing = jnp.array([SCALAR_MIXING, SCALAR_MIXING, VISCOSITY, VISCOSITY], jnp.float32)
+    tendency = mixing.reshape(4, 1, 1, 1) * lap(f) - advection
+    still = jnp.zeros_like(east_v)
+    forcing = jnp.stack(
+        [still, still, cor * north_v - dx(pressure), -cor * east_v - dy(pressure)]
     )
-    v = wet * (
-        north_v
-        + TIME_INCREMENT * (-cor * east_v - dy(pressure) - adv(f[3]) + VISCOSITY * lap(f[3]))
-    )
-    return jnp.stack([heat, salt, u, v])
-
+    return wet * (centre + TIME_INCREMENT * (tendency + forcing))
 
 def shards(state, sea_mask, levels):
     n_fields, level_count, tile_rows, tile_cols = state.shape
@@ -100,17 +95,16 @@
     channels = jnp.concatenate([state.reshape(n_fields * level_count, tile_rows, tile_cols), depth[None]])
     signs = jnp.array([1.0, 1.0, -1.0, -1.0], dtype=jnp.float32)
     signs = jnp.concatenate([jnp.repeat(signs, level_count), jnp.ones((1,), jnp.float32)])
-    wide = gather_wide(channels, signs[:, None, None])
+    wide_state, wide_depth = gather_wide(channels, signs[:, None, None])
 
     lat = lax.axis_index("lat")
     total = lax.axis_size("lat") * tile_rows
     first_row = lat * tile_rows
 
-    grown = wide[:, MARGIN:-MARGIN, MARGIN:-MARGIN]
-    grown_depth = grown[-1]
+    grown_depth = wide_depth[MARGIN:-MARGIN, MARGIN:-MARGIN]
     grown_wet = (depth_index < grown_depth[None]).astype(jnp.float32)
     grown_rows = first_row - MARGIN + jnp.arange(tile_rows + 2 * MARGIN, dtype=jnp.int32)
-    fields = wide[:-1].reshape(n_fields, level_count, *wide.shape[1:])
+    fields = wide_state.reshape(n_fields, level_count, *wide_state.shape[1:])
     once = advance(fields, grown_wet, coriolis(grown_rows, total))
     south_edge = (lat == 0) & (grown_rows < 0)
     once = jnp.where(south_edge[:, None], 0.0, once)

time: 59.2 us -> 58.6 us (0.990)
  other arithmetic: 12.9 us -> 11.1 us
  starting transfers between devices: 23.3 us -> 24.1 us
    another operation x9 -> x2, other arithmetic: 8.04 us -> 1.34 us  [advance(): jnp.stack([still, still, cor * north_v - dx(pressure), -cor * east_v - dy...]
    select_n x1, other arithmetic: 0.28 us -> 3.74 us  [shards(): once = jnp.where(south_edge[:, None], 0.0, once)]
    slice x0 -> x8, local copies, waits for them, and re-layouts: none -> 1.85 us  [the longest x4 1.67 us: gather_wide(): wide_state = jnp.concatenate([west[:-1], lat_wide[:-1], east[:-1]], axis=2)]
    reshape x2 -> x0, local copies, waits for them, and re-layouts: 1.7 us -> none  [the longest x1 0.85 us: gather_wide(): east = jnp.where(lon_odd, off_chip, on_chip).reshape(edge_shape)]
    mul x0 -> x1, other arithmetic: none -> 1.68 us  [advance(): return wet * (centre + TIME_INCREMENT * (tendency + forcing))]
    ppermute x1, waiting for transfers between devices: 10.9 us -> 12.1 us  [gather_wide(): lax.ppermute(jnp.where(lon_odd, east_cols, west_cols), 'lon', across)]
    ppermute x1, starting transfers between devices: 5.04 us -> 5.95 us  [gather_wide(): lax.ppermute(jnp.where(lon_odd, east_cols, west_cols), 'lon', across)]
    ppermute x1, waiting for transfers between devices: 7.6 us -> 6.89 us  [gather_wide(): lax.ppermute(jnp.where(odd, bottom_rows, top_rows), ('lon', 'lat'), [(l *...]
  transfers between devices with their start and end apart: 4 -> 4, of which waited for: 2 -> 2; matrix products, arithmetic and copies ran while one was open for 2% -> 3% of each run, Pallas kernels for 0% -> 0%
where the time goes in v11:
time: 58.6 us; the launch traced here: 58.4 us
  starting transfers between devices  24.1 us (41%)
  waiting for transfers between devices  19 us (32%)
  other arithmetic  11.1 us (19%)
  local copies, waits for them, and re-layouts  3.97 us (7%)
    ppermute x1, starting transfers between devices, gather_wide(): lax.ppermute(jnp.where(odd, bottom_rows, top_rows), ('lon', 'lat'), [(l *...  14.1 us
    ppermute x1, waiting for transfers between devices, gather_wide(): lax.ppermute(jnp.where(lon_odd, east_cols, west_cols), 'lon', across)  12.1 us
    ppermute x1, waiting for transfers between devices, gather_wide(): lax.ppermute(jnp.where(odd, bottom_rows, top_rows), ('lon', 'lat'), [(l *...  6.89 us
    ppermute x1, starting transfers between devices, gather_wide(): lax.ppermute(jnp.where(lon_odd, east_cols, west_cols), 'lon', across)  5.95 us
    select_n x1, other arithmetic, shards(): once = jnp.where(south_edge[:, None], 0.0, once)  3.74 us
    ppermute x1, starting transfers between devices, gather_wide(): lax.ppermute(jnp.where(odd, top_rows, bottom_rows), ('lon', 'lat'), pairs)  2.02 us
    ppermute x1, starting transfers between devices, gather_wide(): lax.ppermute(jnp.where(lon_odd, west_cols, east_cols), 'lon', [(m, m ^ 1)...  2 us
    mul x1, other arithmetic, advance(): return wet * (centre + TIME_INCREMENT * (tendency + forcing))  1.68 us
  transfers between devices with their start and end apart: 4, of which 2 were waited for; matrix products, arithmetic and copies ran while one was open for 3% of the time, Pallas kernels for 0%

profile of v11, /device:TPU:192, one launch (start us, length us, event | category | flops | bytes accessed | tf_op | source)
XLA Modules:
  0.0 58.4 jit_solution(1874596384994463943)
XLA Ops:
  0.0 0.8 %select_convert_fusion = f32[8,128]{1,0:T(8,128)S(1)} fusion(s32[8,128]{1,0:T(8,128)} %param.8, s32[8,128]{1,0:T(8,128)} %param.7), kind=kLoop, calls=%fused_computation.93 | loop fusion | flops 3072 | bytes 12288 | tf_op jit(solution)/shard_map/convert_element_type | solution.py:94
  0.8 1.5 %broadcast_select_fusion.1 = (f32[101,4,128]{2,1,0:T(4,128)S(1)}, f32[101,4,128]{2,1,0:T(4,128)S(1)}) fusion(pred[]{:T(512)S(6)} %eq.25, f32[1,8,128]{2,1,0:T(8,128)S(1)} %bitcast.49, f32[100,8,128]{2,1,0:T(8,128)} %bitcast.44), kind=kLoop, calls=%fused_computation.67 | loop fusion | flops 258560 | bytes 827393 | tf_op jit(solution)/shard_map/jit(_where)/select_n | solution.py:34
  2.2 2.0 %collective-permute-start.1 = (f32[101,4,128]{2,1,0:T(4,128)S(1)}, f32[101,4,128]{2,1,0:T(4,128)S(1)}, u32[]{:S(2)}, u32[]{:S(2)}) collective-permute-start(f32[101,4,128]{2,1,0:T(4,128)S(1)} %get-tuple-element.17), channel_id=1, source_target_pairs={{1,2},{3,4},{5,6},{2,1},{4,3},{6,5},{9,10},{11,12},{13,14},{10,9},... | collective-permute-start | bytes 620552 | tf_op jit(solution)/shard_map/ppermute | solution.py:34
  4.3 14.1 %collective-permute-start = (f32[101,4,128]{2,1,0:T(4,128)S(1)}, f32[101,4,128]{2,1,0:T(4,128)S(1)}, u32[]{:S(2)}, u32[]{:S(2)}) collective-permute-start(f32[101,4,128]{2,1,0:T(4,128)S(1)} %get-tuple-element.18), channel_id=1, source_target_pairs={{0,1},{1,0},{2,3},{3,2},{4,5},{5,4},{6,7},{7,6},{8,9},{9,8},{10,11... | collective-permute-start | bytes 620552 | tf_op jit(solution)/shard_map/ppermute | solution.py:35
  18.4 0.7 %broadcast_in_dim.37 = f32[4,25]{1,0:T(4,128)S(1)} broadcast(f32[4]{0:T(128)} %constant.110.clone), dimensions={0} | broadcast | bytes 416 | tf_op jit(solution)/shard_map/broadcast_in_dim | solution.py:97
  19.5 0.4 rev.4
  20.0 6.9 %collective-permute-done = f32[101,4,128]{2,1,0:T(4,128)S(1)} collective-permute-done((f32[101,4,128]{2,1,0:T(4,128)S(1)}, f32[101,4,128]{2,1,0:T(4,128)S(1)}, u32[]{:S(2)}, u32[]{:S(2)}) %collective-permute-start) | collective-permute-done | bytes 206880 | tf_op jit(solution)/shard_map/ppermute | solution.py:35
  26.8 0.2 broadcast_select_fusion
  27.0 0.2 pad_maximum_fusion.1
  27.2 0.3 slice_select_fusion.1
  27.5 0.4 select_n.110
  27.9 2.0 %collective-permute-start.2 = (f32[6464]{0:T(1024)S(1)}, f32[6464]{0:T(1024)S(1)}, u32[]{:S(2)}, u32[]{:S(2)}) collective-permute-start(f32[6464]{0:T(1024)S(1)} %select_n.110), channel_id=1, source_target_pairs={{0,8},{8,0},{16,24},{24,16},{32,40},{40,32},{48,56},{56,48},{64,72... | collective-permute-start | bytes 77576 | tf_op jit(solution)/shard_map/ppermute | solution.py:50
  29.9 0.4 select_n.112
  30.4 6.0 %collective-permute-start.3 = (f32[6464]{0:T(1024)S(1)}, f32[6464]{0:T(1024)S(1)}, u32[]{:S(2)}, u32[]{:S(2)}) collective-permute-start(f32[6464]{0:T(1024)S(1)} %select_n.112), channel_id=1, source_target_pairs={{8,16},{24,32},{40,48},{56,64},{72,80},{88,96},{104,112},{120,128}... | collective-permute-start | bytes 77576 | tf_op jit(solution)/shard_map/ppermute | solution.py:55
  36.4 12.1 %collective-permute-done.3 = f32[6464]{0:T(1024)S(1)} collective-permute-done((f32[6464]{0:T(1024)S(1)}, f32[6464]{0:T(1024)S(1)}, u32[]{:S(2)}, u32[]{:S(2)}) %collective-permute-start.3) | collective-permute-done | bytes 25888 | tf_op jit(solution)/shard_map/ppermute | solution.py:55
  48.9 0.8 %slice.230 = f32[100,16,4]{2,1,0:T(8,128)S(1)} reshape(f32[6400]{0:T(1024)S(1)} %bitcast.48) | data formatting | bytes 51200 | tf_op jit(solution)/shard_map/slice | solution.py:58
  49.7 0.8 %slice.233 = f32[100,16,4]{2,1,0:T(8,128)S(1)} reshape(f32[6400]{0:T(1024)S(1)} %bitcast.47) | data formatting | bytes 51200 | tf_op jit(solution)/shard_map/slice | solution.py:58
  50.6 0.7 %pad_maximum_fusion = f32[100,16,136]{2,1,0:T(8,128)S(1)} fusion(f32[100,16,4]{2,1,0:T(8,128)S(1)} %slice.233, f32[100,16,128]{2,1,0:T(8,128)S(1)} %slice-done, f32[100,16,4]{2,1,0:T(8,128)S(1)} %slice.230), kind=kLoop, calls=%fused_computation.13 | loop fusion | flops 435200 | bytes 1740800 | tf_op jit(solution)/shard_map/concatenate | solution.py:58
  51.3 0.1 reduce-window_multiply_fusion.1
  51.4 1.0 %fusion.32 = (f32[1,25,12,132]{3,2,1,0:T(8,128)S(1)}, f32[1,25,12,132]{3,2,1,0:T(8,128)S(1)}, f32[25,12,132]{2,1,0:T(8,128)S(1)}, f32[25,12,132]{2,1,0:T(8,128)S(1)}) fusion(f32[25,16,136]{2,1,0:T(8,128)S(1)} %reduce-window_multiply_fusion.1, f32[4,25,16,136]{3,2,1,0:T(8,128)S(1)} %bitcast.42, f32[12]{0:T(128)S(1)} %get-tuple-element.23, ...), kind=kLoop, calls=%fused_computation.48 | loop fusion | flops 633600 | bytes 2217696 | tf_op jit(solution)/shard_map/stack | solution.py:86
  52.5 3.7 %fusion.8 = f32[4,25,12,132]{3,2,1,0:T(8,128)S(1)} fusion(f32[4,25,16,136]{3,2,1,0:T(8,128)S(1)} %bitcast.43, f32[1,25,12,132]{3,2,1,0:T(8,128)S(1)} %get-tuple-element.8, f32[1,25,12,132]{3,2,1,0:T(8,128)S(1)} %get-tuple-element.7, f32[4]{0:T(128)S(1)} %pad.3.clone, f32[25,12,132]{2,1,0:T(8,128)S(1)} %get-tuple-element.12, ...), kind=kLoop, calls=%fused_computation.9 | loop fusion | flops 3960000 | bytes 7128028 | tf_op jit(solution)/shard_map/jit(_where)/select_n | solution.py:110
  56.2 0.1 reduce-window_multiply_fusion
  56.4 0.3 fusion.51
  56.7 1.7 %fusion.21 = f32[4,25,8,128]{3,2,1,0:T(8,128)} fusion(f32[4,25,12,132]{3,2,1,0:T(8,128)S(1)} %fusion.8, f32[1,25,8,128]{3,2,1,0:T(8,128)S(1)} %get-tuple-element.6, f32[1,25,8,128]{3,2,1,0:T(8,128)S(1)} %get-tuple-element.5, f32[4]{0:T(128)S(1)} %pad.3.clone, f32[25,8,128]{2,1,0:T(8,128)S(1)} %get-tuple-element.10, f32[25,8,128]{2,1,0:T(8,128)S(1)} %get-tuple-element.9, ...), kind=kLoop, calls=%fused_computation.33 | loop fusion | flops 2457600 | bytes 4608016 | tf_op jit(solution)/shard_map/mul | solution.py:89
  (25 shorter events, 0.8 us)
Async XLA Ops:
  0.0 27.0 %copy-start.1 = (f32[4,25,8,128]{3,2,1,0:T(8,128)S(1)}, f32[4,25,8,128]{3,2,1,0:T(8,128)}, u32[]{:S(2)}) copy-start(f32[4,25,8,128]{3,2,1,0:T(8,128)} %param.6) | copy-start | bytes 1228804
  2.2 17.3 %collective-permute-start.1 = (f32[101,4,128]{2,1,0:T(4,128)S(1)}, f32[101,4,128]{2,1,0:T(4,128)S(1)}, u32[]{:S(2)}, u32[]{:S(2)}) collective-permute-start(f32[101,4,128]{2,1,0:T(4,128)S(1)} %get-tuple-element.17), channel_id=1, source_target_pairs={{1,2},{3,4},{5,6},{2,1},{4,3},{6,5},{9,10},{11,12},{13,14},{10,9},... | collective-permute-start | bytes 620552 | tf_op jit(solution)/shard_map/ppermute | solution.py:34
  4.3 22.6 %collective-permute-start = (f32[101,4,128]{2,1,0:T(4,128)S(1)}, f32[101,4,128]{2,1,0:T(4,128)S(1)}, u32[]{:S(2)}, u32[]{:S(2)}) collective-permute-start(f32[101,4,128]{2,1,0:T(4,128)S(1)} %get-tuple-element.18), channel_id=1, source_target_pairs={{0,1},{1,0},{2,3},{3,2},{4,5},{5,4},{6,7},{7,6},{8,9},{9,8},{10,11... | collective-permute-start | bytes 620552 | tf_op jit(solution)/shard_map/ppermute | solution.py:35
  27.2 9.2 %copy-start = (f32[101,16,128]{2,1,0:T(8,128)}, f32[101,16,128]{2,1,0:T(8,128)S(1)}, u32[]{:S(2)}) copy-start(f32[101,16,128]{2,1,0:T(8,128)S(1)} %pad_maximum_fusion.1) | copy-start | bytes 2482180
  27.9 8.4 %collective-permute-start.2 = (f32[6464]{0:T(1024)S(1)}, f32[6464]{0:T(1024)S(1)}, u32[]{:S(2)}, u32[]{:S(2)}) collective-permute-start(f32[6464]{0:T(1024)S(1)} %select_n.110), channel_id=1, source_target_pairs={{0,8},{8,0},{16,24},{24,16},{32,40},{40,32},{48,56},{56,48},{64,72... | collective-permute-start | bytes 77576 | tf_op jit(solution)/shard_map/ppermute | solution.py:50
  30.4 18.1 %collective-permute-start.3 = (f32[6464]{0:T(1024)S(1)}, f32[6464]{0:T(1024)S(1)}, u32[]{:S(2)}, u32[]{:S(2)}) collective-permute-start(f32[6464]{0:T(1024)S(1)} %select_n.112), channel_id=1, source_target_pairs={{8,16},{24,32},{40,48},{56,64},{72,80},{88,96},{104,112},{120,128}... | collective-permute-start | bytes 77576 | tf_op jit(solution)/shard_map/ppermute | solution.py:55
  36.4 14.2 %slice-start = ((f32[101,16,128]{2,1,0:T(8,128)}), f32[100,16,128]{2,1,0:T(8,128)S(1)}, s32[]{:S(2)}) async-start(f32[101,16,128]{2,1,0:T(8,128)} %copy-done), calls=%async_computation | async-start | bytes 1638400 | tf_op jit(solution)/shard_map/slice | solution.py:58

commit v12 on v11

--- a/solution.py
+++ b/solution.py
@@ -47,12 +47,12 @@
     edge_shape = lat_wide[..., :WIDE].shape
     east_cols = lat_wide[..., -WIDE:].reshape(-1)
     west_cols = lat_wide[..., :WIDE].reshape(-1)
-    on_chip = lax.ppermute(
-        jnp.where(lon_odd, west_cols, east_cols), "lon", [(m, m ^ 1) for m in range(n_lon)]
-    )
     across = [(m, (m + 1) % n_lon) for m in range(1, n_lon, 2)]
     across = across + [(j, i) for i, j in across]
-    off_chip = lax.ppermute(jnp.where(lon_odd, east_cols, west_cols), "lon", across)
+    off_send = jnp.where(lon_odd, east_cols, west_cols)
+    off_chip = lax.ppermute(off_send, "lon", across)
+    on_send = jnp.where(lon_odd, west_cols, east_cols) + 0.0 * off_send[:1]
+    on_chip = lax.ppermute(on_send, "lon", [(m, m ^ 1) for m in range(n_lon)])
     west = jnp.where(lon_odd, on_chip, off_chip).reshape(edge_shape)
     east = jnp.where(lon_odd, off_chip, on_chip).reshape(edge_shape)
     wide_state = jnp.concatenate([west[:-1], lat_wide[:-1], east[:-1]], axis=2)

time: 58.6 us -> 57.3 us (0.978)
  waiting for transfers between devices: 19 us -> 17.2 us
  starting transfers between devices: 24.1 us -> 23.1 us
  between operations: 0.25 us -> 0.89 us
    ppermute x2, waiting for transfers between devices: 12.1 us -> 9.74 us  [the longest x1 8.61 us: gather_wide(): off_chip = lax.ppermute(off_send, 'lon', across)]
    ppermute x2, starting transfers between devices: 7.95 us -> 6.94 us  [the longest x1 5.03 us: gather_wide(): off_chip = lax.ppermute(off_send, 'lon', across)]
    ppermute x1, waiting for transfers between devices: 6.89 us -> 7.49 us  [gather_wide(): lax.ppermute(jnp.where(odd, bottom_rows, top_rows), ('lon', 'lat'), [(l *...]
  transfers between devices with their start and end apart: 4 -> 4, of which waited for: 2 -> 3; matrix products, arithmetic and copies ran while one was open for 3% -> 4% of each run, Pallas kernels for 0% -> 0%
where the time goes in v12:
time: 57.3 us; the launch traced here: 57.1 us
  starting transfers between devices  23.1 us (40%)
  waiting for transfers between devices  17.2 us (30%)
  other arithmetic  11.4 us (20%)
  local copies, waits for them, and re-layouts  4.49 us (8%)
  between operations  0.89 us (2%)
    ppermute x1, starting transfers between devices, gather_wide(): lax.ppermute(jnp.where(odd, bottom_rows, top_rows), ('lon', 'lat'), [(l *...  14.1 us
    ppermute x1, waiting for transfers between devices, gather_wide(): off_chip = lax.ppermute(off_send, 'lon', across)  8.61 us
    ppermute x1, waiting for transfers between devices, gather_wide(): lax.ppermute(jnp.where(odd, bottom_rows, top_rows), ('lon', 'lat'), [(l *...  7.49 us
    ppermute x1, starting transfers between devices, gather_wide(): off_chip = lax.ppermute(off_send, 'lon', across)  5.03 us
    select_n x1, other arithmetic, shards(): once = jnp.where(south_edge[:, None], 0.0, once)  3.74 us
    ppermute x1, starting transfers between devices, gather_wide(): lax.ppermute(jnp.where(odd, top_rows, bottom_rows), ('lon', 'lat'), pairs)  2.02 us
    ppermute x1, starting transfers between devices, gather_wide(): on_chip = lax.ppermute(on_send, 'lon', [(m, m ^ 1) for m in range(n_lon)])  1.91 us
    mul x1, other arithmetic, advance(): return wet * (centre + TIME_INCREMENT * (tendency + forcing))  1.68 us
  transfers between devices with their start and end apart: 4, of which 3 were waited for; matrix products, arithmetic and copies ran while one was open for 4% of the time, Pallas kernels for 0%

profile of v12, /device:TPU:192, one launch (start us, length us, event | category | flops | bytes accessed | tf_op | source)
XLA Modules:
  0.0 57.1 jit_solution(6987028097596436317)
XLA Ops:
  0.0 0.8 %select_convert_fusion = f32[8,128]{1,0:T(8,128)S(1)} fusion(s32[8,128]{1,0:T(8,128)} %param.8, s32[8,128]{1,0:T(8,128)} %param.7), kind=kLoop, calls=%fused_computation.93 | loop fusion | flops 3072 | bytes 12288 | tf_op jit(solution)/shard_map/convert_element_type | solution.py:94
  0.8 1.5 %broadcast_select_fusion.1 = (f32[101,4,128]{2,1,0:T(4,128)S(1)}, f32[101,4,128]{2,1,0:T(4,128)S(1)}) fusion(pred[]{:T(512)S(6)} %eq.25, f32[1,8,128]{2,1,0:T(8,128)S(1)} %bitcast.50, f32[100,8,128]{2,1,0:T(8,128)} %bitcast.45), kind=kLoop, calls=%fused_computation.67 | loop fusion | flops 258560 | bytes 827393 | tf_op jit(solution)/shard_map/jit(_where)/select_n | solution.py:34
  2.2 2.0 %collective-permute-start.1 = (f32[101,4,128]{2,1,0:T(4,128)S(1)}, f32[101,4,128]{2,1,0:T(4,128)S(1)}, u32[]{:S(2)}, u32[]{:S(2)}) collective-permute-start(f32[101,4,128]{2,1,0:T(4,128)S(1)} %get-tuple-element.15), channel_id=1, source_target_pairs={{1,2},{3,4},{5,6},{2,1},{4,3},{6,5},{9,10},{11,12},{13,14},{10,9},... | collective-permute-start | bytes 620552 | tf_op jit(solution)/shard_map/ppermute | solution.py:34
  4.3 14.1 %collective-permute-start = (f32[101,4,128]{2,1,0:T(4,128)S(1)}, f32[101,4,128]{2,1,0:T(4,128)S(1)}, u32[]{:S(2)}, u32[]{:S(2)}) collective-permute-start(f32[101,4,128]{2,1,0:T(4,128)S(1)} %get-tuple-element.16), channel_id=1, source_target_pairs={{0,1},{1,0},{2,3},{3,2},{4,5},{5,4},{6,7},{7,6},{8,9},{9,8},{10,11... | collective-permute-start | bytes 620552 | tf_op jit(solution)/shard_map/ppermute | solution.py:35
  18.4 0.7 %broadcast_in_dim.37 = f32[4,25]{1,0:T(4,128)S(1)} broadcast(f32[4]{0:T(128)} %constant.112.clone), dimensions={0} | broadcast | bytes 416 | tf_op jit(solution)/shard_map/broadcast_in_dim | solution.py:97
  19.5 0.4 rev.4
  20.0 7.5 %collective-permute-done = f32[101,4,128]{2,1,0:T(4,128)S(1)} collective-permute-done((f32[101,4,128]{2,1,0:T(4,128)S(1)}, f32[101,4,128]{2,1,0:T(4,128)S(1)}, u32[]{:S(2)}, u32[]{:S(2)}) %collective-permute-start) | collective-permute-done | bytes 206880 | tf_op jit(solution)/shard_map/ppermute | solution.py:35
  27.4 0.2 broadcast_select_fusion
  27.8 0.3 slice_select_fusion
  28.1 0.4 select_n.109
  28.5 0.5 slice.284
  29.1 5.0 %collective-permute-start.3 = (f32[6464]{0:T(1024)S(1)}, f32[6464]{0:T(1024)S(1)}, u32[]{:S(2)}, u32[]{:S(2)}) collective-permute-start(f32[6464]{0:T(1024)S(1)} %select_n.109), channel_id=1, source_target_pairs={{8,16},{24,32},{40,48},{56,64},{72,80},{88,96},{104,112},{120,128}... | collective-permute-start | bytes 77576 | tf_op jit(solution)/shard_map/ppermute | solution.py:53
  34.7 0.3 select_add_fusion
  35.0 0.4 add.136
  35.5 1.9 %collective-permute-start.2 = (f32[6464]{0:T(1024)S(1)}, f32[6464]{0:T(1024)S(1)}, u32[]{:S(2)}, u32[]{:S(2)}) collective-permute-start(f32[6464]{0:T(1024)S(1)} %add.136), channel_id=1, source_target_pairs={{0,8},{8,0},{16,24},{24,16},{32,40},{40,32},{48,56},{56,48},{64,72... | collective-permute-start | bytes 77576 | tf_op jit(solution)/shard_map/ppermute | solution.py:55
  37.4 1.1 %collective-permute-done.2 = f32[6464]{0:T(1024)S(1)} collective-permute-done((f32[6464]{0:T(1024)S(1)}, f32[6464]{0:T(1024)S(1)}, u32[]{:S(2)}, u32[]{:S(2)}) %collective-permute-start.2) | collective-permute-done | bytes 25888 | tf_op jit(solution)/shard_map/ppermute | solution.py:55
  38.6 8.6 %collective-permute-done.3 = f32[6464]{0:T(1024)S(1)} collective-permute-done((f32[6464]{0:T(1024)S(1)}, f32[6464]{0:T(1024)S(1)}, u32[]{:S(2)}, u32[]{:S(2)}) %collective-permute-start.3) | collective-permute-done | bytes 25888 | tf_op jit(solution)/shard_map/ppermute | solution.py:53
  47.6 0.8 %slice.234 = f32[100,16,4]{2,1,0:T(8,128)S(1)} reshape(f32[6400]{0:T(1024)S(1)} %bitcast.49) | data formatting | bytes 51200 | tf_op jit(solution)/shard_map/slice | solution.py:58
  48.4 0.8 %slice.237 = f32[100,16,4]{2,1,0:T(8,128)S(1)} reshape(f32[6400]{0:T(1024)S(1)} %bitcast.48) | data formatting | bytes 51200 | tf_op jit(solution)/shard_map/slice | solution.py:58
  49.3 0.7 %pad_maximum_fusion = f32[100,16,136]{2,1,0:T(8,128)S(1)} fusion(f32[100,16,4]{2,1,0:T(8,128)S(1)} %slice.237, f32[100,16,128]{2,1,0:T(8,128)S(1)} %slice-done, f32[100,16,4]{2,1,0:T(8,128)S(1)} %slice.234), kind=kLoop, calls=%fused_computation.13 | loop fusion | flops 435200 | bytes 1740800 | tf_op jit(solution)/shard_map/concatenate | solution.py:58
  50.1 1.0 %fusion.32 = (f32[1,25,12,132]{3,2,1,0:T(8,128)S(1)}, f32[1,25,12,132]{3,2,1,0:T(8,128)S(1)}, f32[25,12,132]{2,1,0:T(8,128)S(1)}, f32[25,12,132]{2,1,0:T(8,128)S(1)}) fusion(f32[25,16,136]{2,1,0:T(8,128)S(1)} %reduce-window_multiply_fusion.1, f32[4,25,16,136]{3,2,1,0:T(8,128)S(1)} %bitcast.43, f32[12]{0:T(128)S(1)} %get-tuple-element.21, ...), kind=kLoop, calls=%fused_computation.48 | loop fusion | flops 633600 | bytes 2217696 | tf_op jit(solution)/shard_map/stack | solution.py:86
  51.2 3.7 %fusion.8 = f32[4,25,12,132]{3,2,1,0:T(8,128)S(1)} fusion(f32[4,25,16,136]{3,2,1,0:T(8,128)S(1)} %bitcast.44, f32[1,25,12,132]{3,2,1,0:T(8,128)S(1)} %get-tuple-element.8, f32[1,25,12,132]{3,2,1,0:T(8,128)S(1)} %get-tuple-element.7, f32[4]{0:T(128)S(1)} %pad.3.clone, f32[25,12,132]{2,1,0:T(8,128)S(1)} %get-tuple-element.12, ...), kind=kLoop, calls=%fused_computation.9 | loop fusion | flops 3960000 | bytes 7128028 | tf_op jit(solution)/shard_map/jit(_where)/select_n | solution.py:110
  55.1 0.3 fusion.51
  55.4 1.7 %fusion.21 = f32[4,25,8,128]{3,2,1,0:T(8,128)} fusion(f32[4,25,12,132]{3,2,1,0:T(8,128)S(1)} %fusion.8, f32[1,25,8,128]{3,2,1,0:T(8,128)S(1)} %get-tuple-element.6, f32[1,25,8,128]{3,2,1,0:T(8,128)S(1)} %get-tuple-element.5, f32[4]{0:T(128)S(1)} %pad.3.clone, f32[25,8,128]{2,1,0:T(8,128)S(1)} %get-tuple-element.10, f32[25,8,128]{2,1,0:T(8,128)S(1)} %get-tuple-element.9, ...), kind=kLoop, calls=%fused_computation.33 | loop fusion | flops 2457600 | bytes 4608016 | tf_op jit(solution)/shard_map/mul | solution.py:89
  (27 shorter events, 1.2 us)
Async XLA Ops:
  0.0 27.6 %copy-start.1 = (f32[4,25,8,128]{3,2,1,0:T(8,128)S(1)}, f32[4,25,8,128]{3,2,1,0:T(8,128)}, u32[]{:S(2)}) copy-start(f32[4,25,8,128]{3,2,1,0:T(8,128)} %param.6) | copy-start | bytes 1228804
  2.2 17.3 %collective-permute-start.1 = (f32[101,4,128]{2,1,0:T(4,128)S(1)}, f32[101,4,128]{2,1,0:T(4,128)S(1)}, u32[]{:S(2)}, u32[]{:S(2)}) collective-permute-start(f32[101,4,128]{2,1,0:T(4,128)S(1)} %get-tuple-element.15), channel_id=1, source_target_pairs={{1,2},{3,4},{5,6},{2,1},{4,3},{6,5},{9,10},{11,12},{13,14},{10,9},... | collective-permute-start | bytes 620552 | tf_op jit(solution)/shard_map/ppermute | solution.py:34
  4.3 23.2 %collective-permute-start = (f32[101,4,128]{2,1,0:T(4,128)S(1)}, f32[101,4,128]{2,1,0:T(4,128)S(1)}, u32[]{:S(2)}, u32[]{:S(2)}) collective-permute-start(f32[101,4,128]{2,1,0:T(4,128)S(1)} %get-tuple-element.16), channel_id=1, source_target_pairs={{0,1},{1,0},{2,3},{3,2},{4,5},{5,4},{6,7},{7,6},{8,9},{9,8},{10,11... | collective-permute-start | bytes 620552 | tf_op jit(solution)/shard_map/ppermute | solution.py:35
  27.8 9.6 %copy-start = (f32[101,16,128]{2,1,0:T(8,128)}, f32[101,16,128]{2,1,0:T(8,128)S(1)}, u32[]{:S(2)}) copy-start(f32[101,16,128]{2,1,0:T(8,128)S(1)} %pad_maximum_fusion.1) | copy-start | bytes 2482180
  29.1 18.1 %collective-permute-start.3 = (f32[6464]{0:T(1024)S(1)}, f32[6464]{0:T(1024)S(1)}, u32[]{:S(2)}, u32[]{:S(2)}) collective-permute-start(f32[6464]{0:T(1024)S(1)} %select_n.109), channel_id=1, source_target_pairs={{8,16},{24,32},{40,48},{56,64},{72,80},{88,96},{104,112},{120,128}... | collective-permute-start | bytes 77576 | tf_op jit(solution)/shard_map/ppermute | solution.py:53
  35.5 3.1 %collective-permute-start.2 = (f32[6464]{0:T(1024)S(1)}, f32[6464]{0:T(1024)S(1)}, u32[]{:S(2)}, u32[]{:S(2)}) collective-permute-start(f32[6464]{0:T(1024)S(1)} %add.136), channel_id=1, source_target_pairs={{0,8},{8,0},{16,24},{24,16},{32,40},{40,32},{48,56},{56,48},{64,72... | collective-permute-start | bytes 77576 | tf_op jit(solution)/shard_map/ppermute | solution.py:55
  37.4 11.8 %slice-start = ((f32[101,16,128]{2,1,0:T(8,128)}), f32[100,16,128]{2,1,0:T(8,128)S(1)}, s32[]{:S(2)}) async-start(f32[101,16,128]{2,1,0:T(8,128)} %copy-done), calls=%async_computation | async-start | bytes 1638400 | tf_op jit(solution)/shard_map/slice | solution.py:58

commit v13 on v12

--- a/solution.py
+++ b/solution.py
@@ -51,7 +51,8 @@
     across = across + [(j, i) for i, j in across]
     off_send = jnp.where(lon_odd, east_cols, west_cols)
     off_chip = lax.ppermute(off_send, "lon", across)
-    on_send = jnp.where(lon_odd, west_cols, east_cols) + 0.0 * off_send[:1]
+    off_send, later = lax.optimization_barrier((off_send, lat_wide))
+    on_send = jnp.where(lon_odd, later[..., :WIDE].reshape(-1), later[..., -WIDE:].reshape(-1))
     on_chip = lax.ppermute(on_send, "lon", [(m, m ^ 1) for m in range(n_lon)])
     west = jnp.where(lon_odd, on_chip, off_chip).reshape(edge_shape)
     east = jnp.where(lon_odd, off_chip, on_chip).reshape(edge_shape)

time: 57.3 us -> 56.8 us (level)
  waiting for transfers between devices: 17.2 us -> 17.9 us
  between operations: 0.89 us -> 0.24 us
    ppermute x1, waiting for transfers between devices: 8.61 us -> 9.26 us  [gather_wide(): off_chip = lax.ppermute(off_send, 'lon', across)]
where the time goes in v13:
time: 56.8 us; the launch traced here: 56.6 us
  starting transfers between devices  23.1 us (41%)
  waiting for transfers between devices  17.9 us (32%)
  other arithmetic  11.4 us (20%)
  local copies, waits for them, and re-layouts  3.98 us (7%)
    ppermute x1, starting transfers between devices, gather_wide(): lax.ppermute(jnp.where(odd, bottom_rows, top_rows), ('lon', 'lat'), [(l *...  14.1 us
    ppermute x1, waiting for transfers between devices, gather_wide(): off_chip = lax.ppermute(off_send, 'lon', across)  9.26 us
    ppermute x1, waiting for transfers between devices, gather_wide(): lax.ppermute(jnp.where(odd, bottom_rows, top_rows), ('lon', 'lat'), [(l *...  7.49 us
    ppermute x1, starting transfers between devices, gather_wide(): off_chip = lax.ppermute(off_send, 'lon', across)  5.04 us
    select_n x1, other arithmetic, shards(): once = jnp.where(south_edge[:, None], 0.0, once)  3.74 us
    ppermute x1, starting transfers between devices, gather_wide(): lax.ppermute(jnp.where(odd, top_rows, bottom_rows), ('lon', 'lat'), pairs)  2.02 us
    ppermute x1, starting transfers between devices, gather_wide(): on_chip = lax.ppermute(on_send, 'lon', [(m, m ^ 1) for m in range(n_lon)])  1.91 us
    mul x1, other arithmetic, advance(): return wet * (centre + TIME_INCREMENT * (tendency + forcing))  1.68 us
  transfers between devices with their start and end apart: 4, of which 3 were waited for; matrix products, arithmetic and copies ran while one was open for 4% of the time, Pallas kernels for 0%

profile of v13, /device:TPU:192, one launch (start us, length us, event | category | flops | bytes accessed | tf_op | source)
XLA Modules:
  0.0 56.6 jit_solution(13642512916803569199)
XLA Ops:
  0.0 0.8 %select_convert_fusion = f32[8,128]{1,0:T(8,128)S(1)} fusion(s32[8,128]{1,0:T(8,128)} %param.8, s32[8,128]{1,0:T(8,128)} %param.7), kind=kLoop, calls=%fused_computation.93 | loop fusion | flops 3072 | bytes 12288 | tf_op jit(solution)/shard_map/convert_element_type | solution.py:95
  0.8 1.5 %broadcast_select_fusion.1 = (f32[101,4,128]{2,1,0:T(4,128)S(1)}, f32[101,4,128]{2,1,0:T(4,128)S(1)}) fusion(pred[]{:T(512)S(6)} %eq.25, f32[1,8,128]{2,1,0:T(8,128)S(1)} %bitcast.48, f32[100,8,128]{2,1,0:T(8,128)} %bitcast.44), kind=kLoop, calls=%fused_computation.67 | loop fusion | flops 258560 | bytes 827393 | tf_op jit(solution)/shard_map/jit(_where)/select_n | solution.py:34
  2.2 2.0 %collective-permute-start.1 = (f32[101,4,128]{2,1,0:T(4,128)S(1)}, f32[101,4,128]{2,1,0:T(4,128)S(1)}, u32[]{:S(2)}, u32[]{:S(2)}) collective-permute-start(f32[101,4,128]{2,1,0:T(4,128)S(1)} %get-tuple-element.17), channel_id=1, source_target_pairs={{1,2},{3,4},{5,6},{2,1},{4,3},{6,5},{9,10},{11,12},{13,14},{10,9},... | collective-permute-start | bytes 620552 | tf_op jit(solution)/shard_map/ppermute | solution.py:34
  4.3 14.1 %collective-permute-start = (f32[101,4,128]{2,1,0:T(4,128)S(1)}, f32[101,4,128]{2,1,0:T(4,128)S(1)}, u32[]{:S(2)}, u32[]{:S(2)}) collective-permute-start(f32[101,4,128]{2,1,0:T(4,128)S(1)} %get-tuple-element.18), channel_id=1, source_target_pairs={{0,1},{1,0},{2,3},{3,2},{4,5},{5,4},{6,7},{7,6},{8,9},{9,8},{10,11... | collective-permute-start | bytes 620552 | tf_op jit(solution)/shard_map/ppermute | solution.py:35
  18.4 0.7 %broadcast_in_dim.37 = f32[4,25]{1,0:T(4,128)S(1)} broadcast(f32[4]{0:T(128)} %constant.110.clone), dimensions={0} | broadcast | bytes 416 | tf_op jit(solution)/shard_map/broadcast_in_dim | solution.py:98
  19.5 0.4 rev.4
  20.0 7.5 %collective-permute-done = f32[101,4,128]{2,1,0:T(4,128)S(1)} collective-permute-done((f32[101,4,128]{2,1,0:T(4,128)S(1)}, f32[101,4,128]{2,1,0:T(4,128)S(1)}, u32[]{:S(2)}, u32[]{:S(2)}) %collective-permute-start) | collective-permute-done | bytes 206880 | tf_op jit(solution)/shard_map/ppermute | solution.py:35
  27.4 0.2 broadcast_select_fusion
  27.6 0.2 pad_maximum_fusion.1
  27.8 0.3 slice_select_fusion
  28.1 0.4 select_n.110
  28.5 5.0 %collective-permute-start.3 = (f32[6464]{0:T(1024)S(1)}, f32[6464]{0:T(1024)S(1)}, u32[]{:S(2)}, u32[]{:S(2)}) collective-permute-start(f32[6464]{0:T(1024)S(1)} %select_n.110), channel_id=1, source_target_pairs={{8,16},{24,32},{40,48},{56,64},{72,80},{88,96},{104,112},{120,128}... | collective-permute-start | bytes 77576 | tf_op jit(solution)/shard_map/ppermute | solution.py:53
  33.6 0.3 slice_select_fusion.1
  33.9 0.4 select_n.112
  34.3 1.9 %collective-permute-start.2 = (f32[6464]{0:T(1024)S(1)}, f32[6464]{0:T(1024)S(1)}, u32[]{:S(2)}, u32[]{:S(2)}) collective-permute-start(f32[6464]{0:T(1024)S(1)} %select_n.112), channel_id=1, source_target_pairs={{0,8},{8,0},{16,24},{24,16},{32,40},{40,32},{48,56},{56,48},{64,72... | collective-permute-start | bytes 77576 | tf_op jit(solution)/shard_map/ppermute | solution.py:56
  36.3 1.1 %collective-permute-done.2 = f32[6464]{0:T(1024)S(1)} collective-permute-done((f32[6464]{0:T(1024)S(1)}, f32[6464]{0:T(1024)S(1)}, u32[]{:S(2)}, u32[]{:S(2)}) %collective-permute-start.2) | collective-permute-done | bytes 25888 | tf_op jit(solution)/shard_map/ppermute | solution.py:56
  37.4 9.3 %collective-permute-done.3 = f32[6464]{0:T(1024)S(1)} collective-permute-done((f32[6464]{0:T(1024)S(1)}, f32[6464]{0:T(1024)S(1)}, u32[]{:S(2)}, u32[]{:S(2)}) %collective-permute-start.3) | collective-permute-done | bytes 25888 | tf_op jit(solution)/shard_map/ppermute | solution.py:53
  47.1 0.8 %slice.238 = f32[100,16,4]{2,1,0:T(8,128)S(1)} reshape(f32[6400]{0:T(1024)S(1)} %bitcast.47) | data formatting | bytes 51200 | tf_op jit(solution)/shard_map/slice | solution.py:59
  47.9 0.8 %slice.241 = f32[100,16,4]{2,1,0:T(8,128)S(1)} reshape(f32[6400]{0:T(1024)S(1)} %bitcast.46) | data formatting | bytes 51200 | tf_op jit(solution)/shard_map/slice | solution.py:59
  48.8 0.7 %pad_maximum_fusion = f32[100,16,136]{2,1,0:T(8,128)S(1)} fusion(f32[100,16,4]{2,1,0:T(8,128)S(1)} %slice.241, f32[100,16,128]{2,1,0:T(8,128)S(1)} %slice-done, f32[100,16,4]{2,1,0:T(8,128)S(1)} %slice.238), kind=kLoop, calls=%fused_computation.13 | loop fusion | flops 435200 | bytes 1740800 | tf_op jit(solution)/shard_map/concatenate | solution.py:59
  49.6 1.0 %fusion.32 = (f32[1,25,12,132]{3,2,1,0:T(8,128)S(1)}, f32[1,25,12,132]{3,2,1,0:T(8,128)S(1)}, f32[25,12,132]{2,1,0:T(8,128)S(1)}, f32[25,12,132]{2,1,0:T(8,128)S(1)}) fusion(f32[25,16,136]{2,1,0:T(8,128)S(1)} %reduce-window_multiply_fusion.1, f32[4,25,16,136]{3,2,1,0:T(8,128)S(1)} %bitcast.42, f32[12]{0:T(128)S(1)} %get-tuple-element.23, ...), kind=kLoop, calls=%fused_computation.48 | loop fusion | flops 633600 | bytes 2217696 | tf_op jit(solution)/shard_map/stack | solution.py:87
  50.6 3.7 %fusion.8 = f32[4,25,12,132]{3,2,1,0:T(8,128)S(1)} fusion(f32[4,25,16,136]{3,2,1,0:T(8,128)S(1)} %bitcast.43, f32[1,25,12,132]{3,2,1,0:T(8,128)S(1)} %get-tuple-element.10, f32[1,25,12,132]{3,2,1,0:T(8,128)S(1)} %get-tuple-element.9, f32[4]{0:T(128)S(1)} %pad.3.clone, f32[25,12,132]{2,1,0:T(8,128)S(1)} %get-tuple-element.14, ...), kind=kLoop, calls=%fused_computation.9 | loop fusion | flops 3960000 | bytes 7128028 | tf_op jit(solution)/shard_map/jit(_where)/select_n | solution.py:111
  54.5 0.3 fusion.51
  54.9 1.7 %fusion.21 = f32[4,25,8,128]{3,2,1,0:T(8,128)} fusion(f32[4,25,12,132]{3,2,1,0:T(8,128)S(1)} %fusion.8, f32[1,25,8,128]{3,2,1,0:T(8,128)S(1)} %get-tuple-element.8, f32[1,25,8,128]{3,2,1,0:T(8,128)S(1)} %get-tuple-element.7, f32[4]{0:T(128)S(1)} %pad.3.clone, f32[25,8,128]{2,1,0:T(8,128)S(1)} %get-tuple-element.12, f32[25,8,128]{2,1,0:T(8,128)S(1)} %get-tuple-element.11, ...), kind=kLoop, calls=%fused_computation.33 | loop fusion | flops 2457600 | bytes 4608016 | tf_op jit(solution)/shard_map/mul | solution.py:90
  (26 shorter events, 1.1 us)
Async XLA Ops:
  0.0 27.6 %copy-start.1 = (f32[4,25,8,128]{3,2,1,0:T(8,128)S(1)}, f32[4,25,8,128]{3,2,1,0:T(8,128)}, u32[]{:S(2)}) copy-start(f32[4,25,8,128]{3,2,1,0:T(8,128)} %param.6) | copy-start | bytes 1228804
  2.2 17.3 %collective-permute-start.1 = (f32[101,4,128]{2,1,0:T(4,128)S(1)}, f32[101,4,128]{2,1,0:T(4,128)S(1)}, u32[]{:S(2)}, u32[]{:S(2)}) collective-permute-start(f32[101,4,128]{2,1,0:T(4,128)S(1)} %get-tuple-element.17), channel_id=1, source_target_pairs={{1,2},{3,4},{5,6},{2,1},{4,3},{6,5},{9,10},{11,12},{13,14},{10,9},... | collective-permute-start | bytes 620552 | tf_op jit(solution)/shard_map/ppermute | solution.py:34
  4.3 23.2 %collective-permute-start = (f32[101,4,128]{2,1,0:T(4,128)S(1)}, f32[101,4,128]{2,1,0:T(4,128)S(1)}, u32[]{:S(2)}, u32[]{:S(2)}) collective-permute-start(f32[101,4,128]{2,1,0:T(4,128)S(1)} %get-tuple-element.18), channel_id=1, source_target_pairs={{0,1},{1,0},{2,3},{3,2},{4,5},{5,4},{6,7},{7,6},{8,9},{9,8},{10,11... | collective-permute-start | bytes 620552 | tf_op jit(solution)/shard_map/ppermute | solution.py:35
  27.8 8.4 %copy-start = (f32[101,16,128]{2,1,0:T(8,128)}, f32[101,16,128]{2,1,0:T(8,128)S(1)}, u32[]{:S(2)}) copy-start(f32[101,16,128]{2,1,0:T(8,128)S(1)} %pad_maximum_fusion.1) | copy-start | bytes 2482180
  28.5 18.1 %collective-permute-start.3 = (f32[6464]{0:T(1024)S(1)}, f32[6464]{0:T(1024)S(1)}, u32[]{:S(2)}, u32[]{:S(2)}) collective-permute-start(f32[6464]{0:T(1024)S(1)} %select_n.110), channel_id=1, source_target_pairs={{8,16},{24,32},{40,48},{56,64},{72,80},{88,96},{104,112},{120,128}... | collective-permute-start | bytes 77576 | tf_op jit(solution)/shard_map/ppermute | solution.py:53
  34.3 3.1 %collective-permute-start.2 = (f32[6464]{0:T(1024)S(1)}, f32[6464]{0:T(1024)S(1)}, u32[]{:S(2)}, u32[]{:S(2)}) collective-permute-start(f32[6464]{0:T(1024)S(1)} %select_n.112), channel_id=1, source_target_pairs={{0,8},{8,0},{16,24},{24,16},{32,40},{40,32},{48,56},{56,48},{64,72... | collective-permute-start | bytes 77576 | tf_op jit(solution)/shard_map/ppermute | solution.py:56
  36.3 12.5 %slice-start = ((f32[101,16,128]{2,1,0:T(8,128)}), f32[100,16,128]{2,1,0:T(8,128)S(1)}, s32[]{:S(2)}) async-start(f32[101,16,128]{2,1,0:T(8,128)} %copy-done), calls=%async_computation | async-start | bytes 1638400 | tf_op jit(solution)/shard_map/slice | solution.py:59

commit v14 on v13

--- a/solution.py
+++ b/solution.py
@@ -18,25 +18,43 @@
     return (1.2 * jnp.sin(-1.3 + 2.8 * (mirrored.astype(jnp.float32) + 0.5) / total))[:, None]
 
 
-def gather_wide(x, signs):
+def gather_wide(state, sea_mask, levels, signs):
     n_lon = lax.axis_size("lon")
     n_lat = lax.axis_size("lat")
+    n_fields, level_count, tile_rows, tile_cols = state.shape
+
+    def rows_of(st, mask, lev, first):
+        st = st.reshape(n_fields * level_count, tile_rows, tile_cols)[:, first : first + WIDE]
+        depth = jnp.where(mask[first : first + WIDE] == 1, lev[first : first + WIDE], 0)
+        return jnp.concatenate([st, depth.astype(jnp.float32)[None]])
 
     lat = lax.axis_index("lat")
     odd = lat % 2 == 1
-    top_rows = x[:, -WIDE:, :]
-    bottom_rows = x[:, :WIDE, :]
+    top_first, bottom_first = tile_rows - WIDE, 0
     inner = [(i, i + 1) for i in range(1, n_lat - 1, 2)]
     inner = inner + [(j, i) for i, j in inner]
     top = n_lat - 1
     pairs = [(l * n_lat + i, l * n_lat + j) for l in range(n_lon) for i, j in inner]
     pairs = pairs + [(l * n_lat + top, (n_lon - 1 - l) * n_lat + top) for l in range(n_lon)]
-    to_even = lax.ppermute(jnp.where(odd, top_rows, bottom_rows), ("lon", "lat"), pairs)
+    even_send = jnp.where(
+        odd,
+        rows_of(state, sea_mask, levels, top_first),
+        rows_of(state, sea_mask, levels, bottom_first),
+    )
+    to_even = lax.ppermute(even_send, ("lon", "lat"), pairs)
+    even_send, state, sea_mask, levels = lax.optimization_barrier((even_send, state, sea_mask, levels))
+    odd_send = jnp.where(
+        odd,
+        rows_of(state, sea_mask, levels, bottom_first),
+        rows_of(state, sea_mask, levels, top_first),
+    )
     to_odd = lax.ppermute(
-        jnp.where(odd, bottom_rows, top_rows),
+        odd_send,
         ("lon", "lat"),
         [(l * n_lat + i, l * n_lat + (i ^ 1)) for l in range(n_lon) for i in range(n_lat)],
     )
+    depth = jnp.where(sea_mask == 1, levels, 0).astype(jnp.float32)
+    x = jnp.concatenate([state.reshape(n_fields * level_count, tile_rows, tile_cols), depth[None]])
     folded = jnp.flip(to_even, axis=(1, 2)) * signs
     north = jnp.where(odd, jnp.where(lat == top, folded, to_even), to_odd)
     south = jnp.where(odd, to_odd, to_even)
@@ -93,10 +111,9 @@
     n_fields, level_count, tile_rows, tile_cols = state.shape
     depth_index = jnp.arange(level_count, dtype=jnp.int32)[:, None, None]
     depth = jnp.where(sea_mask == 1, levels, 0).astype(jnp.float32)
-    channels = jnp.concatenate([state.reshape(n_fields * level_count, tile_rows, tile_cols), depth[None]])
     signs = jnp.array([1.0, 1.0, -1.0, -1.0], dtype=jnp.float32)
     signs = jnp.concatenate([jnp.repeat(signs, level_count), jnp.ones((1,), jnp.float32)])
-    wide_state, wide_depth = gather_wide(channels, signs[:, None, None])
+    wide_state, wide_depth = gather_wide(state, sea_mask, levels, signs[:, None, None])
 
     lat = lax.axis_index("lat")
     total = lax.axis_size("lat") * tile_rows

time: 56.8 us -> 56.7 us (level)
  other arithmetic: 11.4 us -> 10.1 us
  local copies, waits for them, and re-layouts: 3.98 us -> 4.64 us
    slice x0 -> x2, local copies, waits for them, and re-layouts: none -> 1.31 us  [rows_of(): st.reshape(n_fields * level_count, tile_rows, tile_cols)]
    select_n x1 -> x2, other arithmetic: 1.47 us -> 0.16 us  [the longest x1 0.08 us: gather_wide(): jnp.where(odd, rows_of(state, sea_mask, levels, bottom_first), rows_of(st...]
    broadcast_in_dim x0 -> x3, other arithmetic: none -> 0.78 us  [the longest x2 0.78 us: rows_of(): return jnp.concatenate([st, depth.astype(jnp.float32)[None]])]
    convert_element_type x1, other arithmetic: 0.76 us -> 0.01 us  [shards(): depth = jnp.where(sea_mask == 1, levels, 0).astype(jnp.float32)]
    broadcast_in_dim x1, local copies, waits for them, and re-layouts: 0.73 us -> 0.07 us  [shards(): jnp.repeat(signs, level_count)]
  transfers between devices with their start and end apart: 4 -> 4, of which waited for: 3 -> 3; matrix products, arithmetic and copies ran while one was open for 4% -> 3% of each run, Pallas kernels for 0% -> 0%
where the time goes in v14:
time: 56.7 us; the launch traced here: 56.5 us
  starting transfers between devices  23.1 us (41%)
  waiting for transfers between devices  18.3 us (32%)
  other arithmetic  10.1 us (18%)
  local copies, waits for them, and re-layouts  4.64 us (8%)
    ppermute x1, starting transfers between devices, gather_wide(): lax.ppermute(odd_send, ('lon', 'lat'), [(l * n_lat + i, l * n_lat + (i ^...  14.1 us
    ppermute x1, waiting for transfers between devices, gather_wide(): off_chip = lax.ppermute(off_send, 'lon', across)  9.26 us
    ppermute x1, waiting for transfers between devices, gather_wide(): lax.ppermute(odd_send, ('lon', 'lat'), [(l * n_lat + i, l * n_lat + (i ^...  7.9 us
    ppermute x1, starting transfers between devices, gather_wide(): off_chip = lax.ppermute(off_send, 'lon', across)  5.04 us
    select_n x1, other arithmetic, shards(): once = jnp.where(south_edge[:, None], 0.0, once)  3.74 us
    ppermute x1, starting transfers between devices, gather_wide(): to_even = lax.ppermute(even_send, ('lon', 'lat'), pairs)  2.02 us
    ppermute x1, starting transfers between devices, gather_wide(): on_chip = lax.ppermute(on_send, 'lon', [(m, m ^ 1) for m in range(n_lon)])  1.91 us
    mul x1, other arithmetic, advance(): return wet * (centre + TIME_INCREMENT * (tendency + forcing))  1.68 us
  transfers between devices with their start and end apart: 4, of which 3 were waited for; matrix products, arithmetic and copies ran while one was open for 3% of the time, Pallas kernels for 0%

profile of v14, /device:TPU:192, one launch (start us, length us, event | category | flops | bytes accessed | tf_op | source)
XLA Modules:
  0.0 56.5 jit_solution(14148126581195369333)
XLA Ops:
  0.0 1.2 %fusion.73 = (f32[100,4,128]{2,1,0:T(4,128)S(1)}, f32[100,4,128]{2,1,0:T(4,128)S(1)}) fusion(f32[100,8,128]{2,1,0:T(8,128)} %bitcast.54), kind=kLoop, calls=%fused_computation.124 | loop fusion | bytes 819200 | tf_op jit(solution)/shard_map/slice | solution.py:27
  1.3 0.8 %convert_bitcast_fusion.3 = (f32[1,4,128]{2,1,0:T(4,128)S(1)}, f32[1,4,128]{2,1,0:T(4,128)S(1)}) fusion(s32[8,128]{1,0:T(8,128)} %param.8, s32[8,128]{1,0:T(8,128)} %param.7), kind=kLoop, calls=%fused_computation.97 | loop fusion | flops 3072 | bytes 12288 | tf_op jit(solution)/shard_map/broadcast_in_dim | solution.py:29
  2.1 2.0 %collective-permute-start.1 = (f32[101,4,128]{2,1,0:T(4,128)S(1)}, f32[101,4,128]{2,1,0:T(4,128)S(1)}, u32[]{:S(2)}, u32[]{:S(2)}) collective-permute-start(f32[101,4,128]{2,1,0:T(4,128)S(1)} %maximum_select_fusion), channel_id=1, source_target_pairs={{1,2},{3,4},{5,6},{2,1},{4,3},{6,5},{9,10},{11,12},{13,14},{10,9},... | collective-permute-start | bytes 620552 | tf_op jit(solution)/shard_map/ppermute | solution.py:44
  4.4 14.1 %collective-permute-start = (f32[101,4,128]{2,1,0:T(4,128)S(1)}, f32[101,4,128]{2,1,0:T(4,128)S(1)}, u32[]{:S(2)}, u32[]{:S(2)}) collective-permute-start(f32[101,4,128]{2,1,0:T(4,128)S(1)} %maximum_select_fusion.1), channel_id=1, source_target_pairs={{0,1},{1,0},{2,3},{3,2},{4,5},{5,4},{6,7},{7,6},{8,9},{9,8},{10,11... | collective-permute-start | bytes 620552 | tf_op jit(solution)/shard_map/ppermute | solution.py:51
  19.0 0.4 rev.4
  19.4 7.9 %collective-permute-done = f32[101,4,128]{2,1,0:T(4,128)S(1)} collective-permute-done((f32[101,4,128]{2,1,0:T(4,128)S(1)}, f32[101,4,128]{2,1,0:T(4,128)S(1)}, u32[]{:S(2)}, u32[]{:S(2)}) %collective-permute-start) | collective-permute-done | bytes 206880 | tf_op jit(solution)/shard_map/ppermute | solution.py:51
  27.4 0.2 broadcast_select_fusion
  27.5 0.2 pad_maximum_fusion.1
  27.7 0.3 slice_select_fusion
  28.0 0.4 select_n.131
  28.4 5.0 %collective-permute-start.3 = (f32[6464]{0:T(1024)S(1)}, f32[6464]{0:T(1024)S(1)}, u32[]{:S(2)}, u32[]{:S(2)}) collective-permute-start(f32[6464]{0:T(1024)S(1)} %select_n.131), channel_id=1, source_target_pairs={{8,16},{24,32},{40,48},{56,64},{72,80},{88,96},{104,112},{120,128}... | collective-permute-start | bytes 77576 | tf_op jit(solution)/shard_map/ppermute | solution.py:71
  33.5 0.3 slice_select_fusion.1
  33.8 0.4 select_n.133
  34.2 1.9 %collective-permute-start.2 = (f32[6464]{0:T(1024)S(1)}, f32[6464]{0:T(1024)S(1)}, u32[]{:S(2)}, u32[]{:S(2)}) collective-permute-start(f32[6464]{0:T(1024)S(1)} %select_n.133), channel_id=1, source_target_pairs={{0,8},{8,0},{16,24},{24,16},{32,40},{40,32},{48,56},{56,48},{64,72... | collective-permute-start | bytes 77576 | tf_op jit(solution)/shard_map/ppermute | solution.py:74
  36.2 1.1 %collective-permute-done.2 = f32[6464]{0:T(1024)S(1)} collective-permute-done((f32[6464]{0:T(1024)S(1)}, f32[6464]{0:T(1024)S(1)}, u32[]{:S(2)}, u32[]{:S(2)}) %collective-permute-start.2) | collective-permute-done | bytes 25888 | tf_op jit(solution)/shard_map/ppermute | solution.py:74
  37.3 9.3 %collective-permute-done.3 = f32[6464]{0:T(1024)S(1)} collective-permute-done((f32[6464]{0:T(1024)S(1)}, f32[6464]{0:T(1024)S(1)}, u32[]{:S(2)}, u32[]{:S(2)}) %collective-permute-start.3) | collective-permute-done | bytes 25888 | tf_op jit(solution)/shard_map/ppermute | solution.py:71
  47.0 0.8 %slice.278 = f32[100,16,4]{2,1,0:T(8,128)S(1)} reshape(f32[6400]{0:T(1024)S(1)} %bitcast.58) | data formatting | bytes 51200 | tf_op jit(solution)/shard_map/slice | solution.py:77
  47.8 0.8 %slice.281 = f32[100,16,4]{2,1,0:T(8,128)S(1)} reshape(f32[6400]{0:T(1024)S(1)} %bitcast.57) | data formatting | bytes 51200 | tf_op jit(solution)/shard_map/slice | solution.py:77
  48.7 0.7 %pad_maximum_fusion = f32[100,16,136]{2,1,0:T(8,128)S(1)} fusion(f32[100,16,4]{2,1,0:T(8,128)S(1)} %slice.281, f32[100,16,128]{2,1,0:T(8,128)S(1)} %slice-done, f32[100,16,4]{2,1,0:T(8,128)S(1)} %slice.278), kind=kLoop, calls=%fused_computation.13 | loop fusion | flops 435200 | bytes 1740800 | tf_op jit(solution)/shard_map/concatenate | solution.py:77
  49.4 0.1 reduce-window_multiply_fusion.1
  49.5 1.0 %fusion.32 = (f32[1,25,12,132]{3,2,1,0:T(8,128)S(1)}, f32[1,25,12,132]{3,2,1,0:T(8,128)S(1)}, f32[25,12,132]{2,1,0:T(8,128)S(1)}, f32[25,12,132]{2,1,0:T(8,128)S(1)}) fusion(f32[25,16,136]{2,1,0:T(8,128)S(1)} %reduce-window_multiply_fusion.1, f32[4,25,16,136]{3,2,1,0:T(8,128)S(1)} %bitcast.52, f32[12]{0:T(128)S(1)} %get-tuple-element.35, ...), kind=kLoop, calls=%fused_computation.46 | loop fusion | flops 633600 | bytes 2217696 | tf_op jit(solution)/shard_map/stack | solution.py:105
  50.5 3.7 %fusion.8 = f32[4,25,12,132]{3,2,1,0:T(8,128)S(1)} fusion(f32[4,25,16,136]{3,2,1,0:T(8,128)S(1)} %bitcast.53, f32[1,25,12,132]{3,2,1,0:T(8,128)S(1)} %get-tuple-element.16, f32[1,25,12,132]{3,2,1,0:T(8,128)S(1)} %get-tuple-element.15, f32[4]{0:T(128)S(1)} %pad.3.clone, f32[25,12,132]{2,1,0:T(8,128)S(1)} %get-tuple-element.20, ...), kind=kLoop, calls=%fused_computation.9 | loop fusion | flops 3960000 | bytes 7128028 | tf_op jit(solution)/shard_map/jit(_where)/select_n | solution.py:128
  54.4 0.3 fusion.50
  54.8 1.7 %fusion.21 = f32[4,25,8,128]{3,2,1,0:T(8,128)} fusion(f32[4,25,12,132]{3,2,1,0:T(8,128)S(1)} %fusion.8, f32[1,25,8,128]{3,2,1,0:T(8,128)S(1)} %get-tuple-element.14, f32[1,25,8,128]{3,2,1,0:T(8,128)S(1)} %get-tuple-element.13, f32[4]{0:T(128)S(1)} %pad.3.clone, f32[25,8,128]{2,1,0:T(8,128)S(1)} %get-tuple-element.18, ...), kind=kLoop, calls=%fused_computation.31 | loop fusion | flops 2457600 | bytes 4608016 | tf_op jit(solution)/shard_map/mul | solution.py:108
  (38 shorter events, 1.2 us)
Async XLA Ops:
  0.0 18.5 %copy-start.4 = (f32[4]{0:T(128)S(1)}, f32[4]{0:T(128)}, u32[]{:S(2)}) copy-start(f32[4]{0:T(128)} %constant.111.clone) | copy-start | bytes 52
  0.0 4.2 %copy-start.1 = (f32[4,25,8,128]{3,2,1,0:T(8,128)S(1)}, f32[4,25,8,128]{3,2,1,0:T(8,128)}, u32[]{:S(2)}) copy-start(f32[4,25,8,128]{3,2,1,0:T(8,128)} %param.6) | copy-start | bytes 1228804
  0.0 4.2 %copy-start.3 = (s32[8,128]{1,0:T(8,128)S(1)}, s32[8,128]{1,0:T(8,128)}, u32[]{:S(2)}) copy-start(s32[8,128]{1,0:T(8,128)} %param.7) | copy-start | bytes 12292
  0.0 4.3 %copy-start.2 = (s32[8,128]{1,0:T(8,128)S(1)}, s32[8,128]{1,0:T(8,128)}, u32[]{:S(2)}) copy-start(s32[8,128]{1,0:T(8,128)} %param.8) | copy-start | bytes 12292
  2.1 16.9 %collective-permute-start.1 = (f32[101,4,128]{2,1,0:T(4,128)S(1)}, f32[101,4,128]{2,1,0:T(4,128)S(1)}, u32[]{:S(2)}, u32[]{:S(2)}) collective-permute-start(f32[101,4,128]{2,1,0:T(4,128)S(1)} %maximum_select_fusion), channel_id=1, source_target_pairs={{1,2},{3,4},{5,6},{2,1},{4,3},{6,5},{9,10},{11,12},{13,14},{10,9},... | collective-permute-start | bytes 620552 | tf_op jit(solution)/shard_map/ppermute | solution.py:44
  4.4 23.0 %collective-permute-start = (f32[101,4,128]{2,1,0:T(4,128)S(1)}, f32[101,4,128]{2,1,0:T(4,128)S(1)}, u32[]{:S(2)}, u32[]{:S(2)}) collective-permute-start(f32[101,4,128]{2,1,0:T(4,128)S(1)} %maximum_select_fusion.1), channel_id=1, source_target_pairs={{0,1},{1,0},{2,3},{3,2},{4,5},{5,4},{6,7},{7,6},{8,9},{9,8},{10,11... | collective-permute-start | bytes 620552 | tf_op jit(solution)/shard_map/ppermute | solution.py:51
  27.7 8.4 %copy-start = (f32[101,16,128]{2,1,0:T(8,128)}, f32[101,16,128]{2,1,0:T(8,128)S(1)}, u32[]{:S(2)}) copy-start(f32[101,16,128]{2,1,0:T(8,128)S(1)} %pad_maximum_fusion.1) | copy-start | bytes 2482180
  28.4 18.1 %collective-permute-start.3 = (f32[6464]{0:T(1024)S(1)}, f32[6464]{0:T(1024)S(1)}, u32[]{:S(2)}, u32[]{:S(2)}) collective-permute-start(f32[6464]{0:T(1024)S(1)} %select_n.131), channel_id=1, source_target_pairs={{8,16},{24,32},{40,48},{56,64},{72,80},{88,96},{104,112},{120,128}... | collective-permute-start | bytes 77576 | tf_op jit(solution)/shard_map/ppermute | solution.py:71
  34.2 3.1 %collective-permute-start.2 = (f32[6464]{0:T(1024)S(1)}, f32[6464]{0:T(1024)S(1)}, u32[]{:S(2)}, u32[]{:S(2)}) collective-permute-start(f32[6464]{0:T(1024)S(1)} %select_n.133), channel_id=1, source_target_pairs={{0,8},{8,0},{16,24},{24,16},{32,40},{40,32},{48,56},{56,48},{64,72... | collective-permute-start | bytes 77576 | tf_op jit(solution)/shard_map/ppermute | solution.py:74
  36.2 12.5 %slice-start = ((f32[101,16,128]{2,1,0:T(8,128)}), f32[100,16,128]{2,1,0:T(8,128)S(1)}, s32[]{:S(2)}) async-start(f32[101,16,128]{2,1,0:T(8,128)} %copy-done), calls=%async_computation | async-start | bytes 1638400 | tf_op jit(solution)/shard_map/slice | solution.py:77

commit v15 on v14

--- a/solution.py
+++ b/solution.py
@@ -36,13 +36,6 @@
     top = n_lat - 1
     pairs = [(l * n_lat + i, l * n_lat + j) for l in range(n_lon) for i, j in inner]
     pairs = pairs + [(l * n_lat + top, (n_lon - 1 - l) * n_lat + top) for l in range(n_lon)]
-    even_send = jnp.where(
-        odd,
-        rows_of(state, sea_mask, levels, top_first),
-        rows_of(state, sea_mask, levels, bottom_first),
-    )
-    to_even = lax.ppermute(even_send, ("lon", "lat"), pairs)
-    even_send, state, sea_mask, levels = lax.optimization_barrier((even_send, state, sea_mask, levels))
     odd_send = jnp.where(
         odd,
         rows_of(state, sea_mask, levels, bottom_first),
@@ -53,6 +46,13 @@
         ("lon", "lat"),
         [(l * n_lat + i, l * n_lat + (i ^ 1)) for l in range(n_lon) for i in range(n_lat)],
     )
+    odd_send, state, sea_mask, levels = lax.optimization_barrier((odd_send, state, sea_mask, levels))
+    even_send = jnp.where(
+        odd,
+        rows_of(state, sea_mask, levels, top_first),
+        rows_of(state, sea_mask, levels, bottom_first),
+    )
+    to_even = lax.ppermute(even_send, ("lon", "lat"), pairs)
     depth = jnp.where(sea_mask == 1, levels, 0).astype(jnp.float32)
     x = jnp.concatenate([state.reshape(n_fields * level_count, tile_rows, tile_cols), depth[None]])
     folded = jnp.flip(to_even, axis=(1, 2)) * signs

time: 56.7 us -> 57.4 us (1.012)
  the two profiles are of different devices: /device:TPU:192 before, /device:TPU:511 now
where the time goes in v15:
time: 57.4 us; the launch traced here: 57.1 us
  waiting for transfers between devices  26.6 us (46%)
  starting transfers between devices  15.4 us (27%)
  other arithmetic  10.1 us (18%)
  local copies, waits for them, and re-layouts  4.64 us (8%)
    ppermute x1, waiting for transfers between devices, gather_wide(): to_even = lax.ppermute(even_send, ('lon', 'lat'), pairs)  16.5 us
    ppermute x1, waiting for transfers between devices, gather_wide(): off_chip = lax.ppermute(off_send, 'lon', across)  8.98 us
    ppermute x1, starting transfers between devices, gather_wide(): to_even = lax.ppermute(even_send, ('lon', 'lat'), pairs)  5.57 us
    ppermute x1, starting transfers between devices, gather_wide(): off_chip = lax.ppermute(off_send, 'lon', across)  5.31 us
    select_n x1, other arithmetic, shards(): once = jnp.where(south_edge[:, None], 0.0, once)  3.74 us
    ppermute x1, starting transfers between devices, gather_wide(): lax.ppermute(odd_send, ('lon', 'lat'), [(l * n_lat + i, l * n_lat + (i ^...  2.64 us
    ppermute x1, starting transfers between devices, gather_wide(): on_chip = lax.ppermute(on_send, 'lon', [(m, m ^ 1) for m in range(n_lon)])  1.91 us
    mul x1, other arithmetic, advance(): return wet * (centre + TIME_INCREMENT * (tendency + forcing))  1.68 us
  transfers between devices with their start and end apart: 4, of which 3 were waited for; matrix products, arithmetic and copies ran while one was open for 3% of the time, Pallas kernels for 0%

profile of v15, /device:TPU:511, one launch (start us, length us, event | category | flops | bytes accessed | tf_op | source)
XLA Modules:
  0.0 57.1 jit_solution(8867845533733832223)
XLA Ops:
  0.0 1.2 %fusion.73 = (f32[100,4,128]{2,1,0:T(4,128)S(1)}, f32[100,4,128]{2,1,0:T(4,128)S(1)}) fusion(f32[100,8,128]{2,1,0:T(8,128)} %bitcast.54), kind=kLoop, calls=%fused_computation.124 | loop fusion | bytes 819200 | tf_op jit(solution)/shard_map/slice | solution.py:27
  1.3 0.8 %convert_bitcast_fusion.3 = (f32[1,4,128]{2,1,0:T(4,128)S(1)}, f32[1,4,128]{2,1,0:T(4,128)S(1)}) fusion(s32[8,128]{1,0:T(8,128)} %param.8, s32[8,128]{1,0:T(8,128)} %param.7), kind=kLoop, calls=%fused_computation.97 | loop fusion | flops 3072 | bytes 12288 | tf_op jit(solution)/shard_map/broadcast_in_dim | solution.py:29
  2.1 2.6 %collective-permute-start = (f32[101,4,128]{2,1,0:T(4,128)S(1)}, f32[101,4,128]{2,1,0:T(4,128)S(1)}, u32[]{:S(2)}, u32[]{:S(2)}) collective-permute-start(f32[101,4,128]{2,1,0:T(4,128)S(1)} %maximum_select_fusion), channel_id=1, source_target_pairs={{0,1},{1,0},{2,3},{3,2},{4,5},{5,4},{6,7},{7,6},{8,9},{9,8},{10,11... | collective-permute-start | bytes 620552 | tf_op jit(solution)/shard_map/ppermute | solution.py:44
  5.0 5.6 %collective-permute-start.1 = (f32[101,4,128]{2,1,0:T(4,128)S(1)}, f32[101,4,128]{2,1,0:T(4,128)S(1)}, u32[]{:S(2)}, u32[]{:S(2)}) collective-permute-start(f32[101,4,128]{2,1,0:T(4,128)S(1)} %maximum_select_fusion.1), channel_id=1, source_target_pairs={{1,2},{3,4},{5,6},{2,1},{4,3},{6,5},{9,10},{11,12},{13,14},{10,9},... | collective-permute-start | bytes 620552 | tf_op jit(solution)/shard_map/ppermute | solution.py:55
  11.1 16.5 %collective-permute-done.1 = f32[101,4,128]{2,1,0:T(4,128)S(1)} collective-permute-done((f32[101,4,128]{2,1,0:T(4,128)S(1)}, f32[101,4,128]{2,1,0:T(4,128)S(1)}, u32[]{:S(2)}, u32[]{:S(2)}) %collective-permute-start.1) | collective-permute-done | bytes 206880 | tf_op jit(solution)/shard_map/ppermute | solution.py:55
  27.6 0.4 rev.4
  28.0 0.2 broadcast_select_fusion
  28.2 0.2 pad_maximum_fusion.1
  28.4 0.3 slice_select_fusion
  28.7 0.4 select_n.131
  29.1 5.3 %collective-permute-start.3 = (f32[6464]{0:T(1024)S(1)}, f32[6464]{0:T(1024)S(1)}, u32[]{:S(2)}, u32[]{:S(2)}) collective-permute-start(f32[6464]{0:T(1024)S(1)} %select_n.131), channel_id=1, source_target_pairs={{8,16},{24,32},{40,48},{56,64},{72,80},{88,96},{104,112},{120,128}... | collective-permute-start | bytes 77576 | tf_op jit(solution)/shard_map/ppermute | solution.py:71
  34.4 0.3 slice_select_fusion.1
  34.7 0.4 select_n.133
  35.1 1.9 %collective-permute-start.2 = (f32[6464]{0:T(1024)S(1)}, f32[6464]{0:T(1024)S(1)}, u32[]{:S(2)}, u32[]{:S(2)}) collective-permute-start(f32[6464]{0:T(1024)S(1)} %select_n.133), channel_id=1, source_target_pairs={{0,8},{8,0},{16,24},{24,16},{32,40},{40,32},{48,56},{56,48},{64,72... | collective-permute-start | bytes 77576 | tf_op jit(solution)/shard_map/ppermute | solution.py:74
  37.1 1.1 %collective-permute-done.2 = f32[6464]{0:T(1024)S(1)} collective-permute-done((f32[6464]{0:T(1024)S(1)}, f32[6464]{0:T(1024)S(1)}, u32[]{:S(2)}, u32[]{:S(2)}) %collective-permute-start.2) | collective-permute-done | bytes 25888 | tf_op jit(solution)/shard_map/ppermute | solution.py:74
  38.2 9.0 %collective-permute-done.3 = f32[6464]{0:T(1024)S(1)} collective-permute-done((f32[6464]{0:T(1024)S(1)}, f32[6464]{0:T(1024)S(1)}, u32[]{:S(2)}, u32[]{:S(2)}) %collective-permute-start.3) | collective-permute-done | bytes 25888 | tf_op jit(solution)/shard_map/ppermute | solution.py:71
  47.6 0.8 %slice.278 = f32[100,16,4]{2,1,0:T(8,128)S(1)} reshape(f32[6400]{0:T(1024)S(1)} %bitcast.58) | data formatting | bytes 51200 | tf_op jit(solution)/shard_map/slice | solution.py:77
  48.4 0.8 %slice.281 = f32[100,16,4]{2,1,0:T(8,128)S(1)} reshape(f32[6400]{0:T(1024)S(1)} %bitcast.57) | data formatting | bytes 51200 | tf_op jit(solution)/shard_map/slice | solution.py:77
  49.3 0.7 %pad_maximum_fusion = f32[100,16,136]{2,1,0:T(8,128)S(1)} fusion(f32[100,16,4]{2,1,0:T(8,128)S(1)} %slice.281, f32[100,16,128]{2,1,0:T(8,128)S(1)} %slice-done, f32[100,16,4]{2,1,0:T(8,128)S(1)} %slice.278), kind=kLoop, calls=%fused_computation.13 | loop fusion | flops 435200 | bytes 1740800 | tf_op jit(solution)/shard_map/concatenate | solution.py:77
  50.0 0.1 reduce-window_multiply_fusion.1
  50.2 1.0 %fusion.32 = (f32[1,25,12,132]{3,2,1,0:T(8,128)S(1)}, f32[1,25,12,132]{3,2,1,0:T(8,128)S(1)}, f32[25,12,132]{2,1,0:T(8,128)S(1)}, f32[25,12,132]{2,1,0:T(8,128)S(1)}) fusion(f32[25,16,136]{2,1,0:T(8,128)S(1)} %reduce-window_multiply_fusion.1, f32[4,25,16,136]{3,2,1,0:T(8,128)S(1)} %bitcast.52, f32[12]{0:T(128)S(1)} %get-tuple-element.35, ...), kind=kLoop, calls=%fused_computation.46 | loop fusion | flops 633600 | bytes 2217696 | tf_op jit(solution)/shard_map/stack | solution.py:105
  51.2 3.7 %fusion.8 = f32[4,25,12,132]{3,2,1,0:T(8,128)S(1)} fusion(f32[4,25,16,136]{3,2,1,0:T(8,128)S(1)} %bitcast.53, f32[1,25,12,132]{3,2,1,0:T(8,128)S(1)} %get-tuple-element.16, f32[1,25,12,132]{3,2,1,0:T(8,128)S(1)} %get-tuple-element.15, f32[4]{0:T(128)S(1)} %pad.3.clone, f32[25,12,132]{2,1,0:T(8,128)S(1)} %get-tuple-element.20, ...), kind=kLoop, calls=%fused_computation.9 | loop fusion | flops 3960000 | bytes 7128028 | tf_op jit(solution)/shard_map/jit(_where)/select_n | solution.py:128
  55.1 0.3 fusion.50
  55.4 1.7 %fusion.21 = f32[4,25,8,128]{3,2,1,0:T(8,128)} fusion(f32[4,25,12,132]{3,2,1,0:T(8,128)S(1)} %fusion.8, f32[1,25,8,128]{3,2,1,0:T(8,128)S(1)} %get-tuple-element.14, f32[1,25,8,128]{3,2,1,0:T(8,128)S(1)} %get-tuple-element.13, f32[4]{0:T(128)S(1)} %pad.3.clone, f32[25,8,128]{2,1,0:T(8,128)S(1)} %get-tuple-element.18, ...), kind=kLoop, calls=%fused_computation.31 | loop fusion | flops 2457600 | bytes 4608016 | tf_op jit(solution)/shard_map/mul | solution.py:108
  (38 shorter events, 1.2 us)
Async XLA Ops:
  0.0 10.6 %copy-start.4 = (f32[4]{0:T(128)S(1)}, f32[4]{0:T(128)}, u32[]{:S(2)}) copy-start(f32[4]{0:T(128)} %constant.111.clone) | copy-start | bytes 52
  0.0 4.8 %copy-start.1 = (f32[4,25,8,128]{3,2,1,0:T(8,128)S(1)}, f32[4,25,8,128]{3,2,1,0:T(8,128)}, u32[]{:S(2)}) copy-start(f32[4,25,8,128]{3,2,1,0:T(8,128)} %param.6) | copy-start | bytes 1228804
  0.0 4.9 %copy-start.3 = (s32[8,128]{1,0:T(8,128)S(1)}, s32[8,128]{1,0:T(8,128)}, u32[]{:S(2)}) copy-start(s32[8,128]{1,0:T(8,128)} %param.7) | copy-start | bytes 12292
  0.0 4.9 %copy-start.2 = (s32[8,128]{1,0:T(8,128)S(1)}, s32[8,128]{1,0:T(8,128)}, u32[]{:S(2)}) copy-start(s32[8,128]{1,0:T(8,128)} %param.8) | copy-start | bytes 12292
  2.1 25.9 %collective-permute-start = (f32[101,4,128]{2,1,0:T(4,128)S(1)}, f32[101,4,128]{2,1,0:T(4,128)S(1)}, u32[]{:S(2)}, u32[]{:S(2)}) collective-permute-start(f32[101,4,128]{2,1,0:T(4,128)S(1)} %maximum_select_fusion), channel_id=1, source_target_pairs={{0,1},{1,0},{2,3},{3,2},{4,5},{5,4},{6,7},{7,6},{8,9},{9,8},{10,11... | collective-permute-start | bytes 620552 | tf_op jit(solution)/shard_map/ppermute | solution.py:44
  5.0 22.6 %collective-permute-start.1 = (f32[101,4,128]{2,1,0:T(4,128)S(1)}, f32[101,4,128]{2,1,0:T(4,128)S(1)}, u32[]{:S(2)}, u32[]{:S(2)}) collective-permute-start(f32[101,4,128]{2,1,0:T(4,128)S(1)} %maximum_select_fusion.1), channel_id=1, source_target_pairs={{1,2},{3,4},{5,6},{2,1},{4,3},{6,5},{9,10},{11,12},{13,14},{10,9},... | collective-permute-start | bytes 620552 | tf_op jit(solution)/shard_map/ppermute | solution.py:55
  28.4 8.7 %copy-start = (f32[101,16,128]{2,1,0:T(8,128)}, f32[101,16,128]{2,1,0:T(8,128)S(1)}, u32[]{:S(2)}) copy-start(f32[101,16,128]{2,1,0:T(8,128)S(1)} %pad_maximum_fusion.1) | copy-start | bytes 2482180
  29.1 18.1 %collective-permute-start.3 = (f32[6464]{0:T(1024)S(1)}, f32[6464]{0:T(1024)S(1)}, u32[]{:S(2)}, u32[]{:S(2)}) collective-permute-start(f32[6464]{0:T(1024)S(1)} %select_n.131), channel_id=1, source_target_pairs={{8,16},{24,32},{40,48},{56,64},{72,80},{88,96},{104,112},{120,128}... | collective-permute-start | bytes 77576 | tf_op jit(solution)/shard_map/ppermute | solution.py:71
  35.1 3.1 %collective-permute-start.2 = (f32[6464]{0:T(1024)S(1)}, f32[6464]{0:T(1024)S(1)}, u32[]{:S(2)}, u32[]{:S(2)}) collective-permute-start(f32[6464]{0:T(1024)S(1)} %select_n.133), channel_id=1, source_target_pairs={{0,8},{8,0},{16,24},{24,16},{32,40},{40,32},{48,56},{56,48},{64,72... | collective-permute-start | bytes 77576 | tf_op jit(solution)/shard_map/ppermute | solution.py:74
  37.1 12.2 %slice-start = ((f32[101,16,128]{2,1,0:T(8,128)}), f32[100,16,128]{2,1,0:T(8,128)S(1)}, s32[]{:S(2)}) async-start(f32[101,16,128]{2,1,0:T(8,128)} %copy-done), calls=%async_computation | async-start | bytes 1638400 | tf_op jit(solution)/shard_map/slice | solution.py:77

commit v16 on v13

--- a/solution.py
+++ b/solution.py
@@ -54,10 +54,18 @@
     off_send, later = lax.optimization_barrier((off_send, lat_wide))
     on_send = jnp.where(lon_odd, later[..., :WIDE].reshape(-1), later[..., -WIDE:].reshape(-1))
     on_chip = lax.ppermute(on_send, "lon", [(m, m ^ 1) for m in range(n_lon)])
-    west = jnp.where(lon_odd, on_chip, off_chip).reshape(edge_shape)
-    east = jnp.where(lon_odd, off_chip, on_chip).reshape(edge_shape)
-    wide_state = jnp.concatenate([west[:-1], lat_wide[:-1], east[:-1]], axis=2)
-    wide_depth = jnp.concatenate([west[-1], lat_wide[-1], east[-1]], axis=1)
+    near = on_chip.reshape(edge_shape)
+    far = off_chip.reshape(edge_shape)
+    wide_state = jnp.where(
+        lon_odd,
+        jnp.concatenate([near[:-1], lat_wide[:-1], far[:-1]], axis=2),
+        jnp.concatenate([far[:-1], lat_wide[:-1], near[:-1]], axis=2),
+    )
+    wide_depth = jnp.where(
+        lon_odd,
+        jnp.concatenate([near[-1], lat_wide[-1], far[-1]], axis=1),
+        jnp.concatenate([far[-1], lat_wide[-1], near[-1]], axis=1),
+    )
     return wide_state, wide_depth
 
 

time: 56.8 us -> 60.2 us (1.060)
  local copies, waits for them, and re-layouts: 3.98 us -> 6.58 us
  other arithmetic: 11.4 us -> 13.9 us
  waiting for transfers between devices: 17.9 us -> 16.2 us
    select_n x1 -> x3, other arithmetic: 0.01 us -> 3.34 us  [the longest x2 3.25 us: gather_wide(): jnp.where(lon_odd, jnp.concatenate([near[:-1], lat_wide[:-1], far[:-1]],...]
    ppermute x1, waiting for transfers between devices: 9.26 us -> 7.57 us  [gather_wide(): off_chip = lax.ppermute(off_send, 'lon', across)]
    concatenate x0 -> x2, local copies, waits for them, and re-layouts: none -> 1.67 us  [gather_wide(): jnp.concatenate([near[:-1], lat_wide[:-1], far[:-1]], axis=2)]
    slice x8 -> x5, local copies, waits for them, and re-layouts: 1.85 us -> 2.63 us  [the longest x1 1.74 us: gather_wide(): far[:-1]]
    concatenate x2 -> x0, other arithmetic: 0.78 us -> none  [the longest x1 0.7 us: gather_wide(): wide_state = jnp.concatenate([west[:-1], lat_wide[:-1], east[:-1]], axis=2)]
  transfers between devices with their start and end apart: 4 -> 4, of which waited for: 3 -> 3; matrix products, arithmetic and copies ran while one was open for 4% -> 7% of each run, Pallas kernels for 0% -> 0%
where the time goes in v16:
time: 60.2 us; the launch traced here: 60 us
  starting transfers between devices  23.1 us (38%)
  waiting for transfers between devices  16.2 us (27%)
  other arithmetic  13.9 us (23%)
  local copies, waits for them, and re-layouts  6.58 us (11%)
    ppermute x1, starting transfers between devices, gather_wide(): lax.ppermute(jnp.where(odd, bottom_rows, top_rows), ('lon', 'lat'), [(l *...  14.1 us
    ppermute x1, waiting for transfers between devices, gather_wide(): off_chip = lax.ppermute(off_send, 'lon', across)  7.57 us
    ppermute x1, waiting for transfers between devices, gather_wide(): lax.ppermute(jnp.where(odd, bottom_rows, top_rows), ('lon', 'lat'), [(l *...  7.49 us
    ppermute x1, starting transfers between devices, gather_wide(): off_chip = lax.ppermute(off_send, 'lon', across)  5.04 us
    select_n x1, other arithmetic, shards(): once = jnp.where(south_edge[:, None], 0.0, once)  3.74 us
    select_n x2, other arithmetic, gather_wide(): jnp.where(lon_odd, jnp.concatenate([near[:-1], lat_wide[:-1], far[:-1]],...  3.25 us
    ppermute x1, starting transfers between devices, gather_wide(): lax.ppermute(jnp.where(odd, top_rows, bottom_rows), ('lon', 'lat'), pairs)  2.02 us
    ppermute x1, starting transfers between devices, gather_wide(): on_chip = lax.ppermute(on_send, 'lon', [(m, m ^ 1) for m in range(n_lon)])  1.91 us
  transfers between devices with their start and end apart: 4, of which 3 were waited for; matrix products, arithmetic and copies ran while one was open for 7% of the time, Pallas kernels for 0%

profile of v16, /device:TPU:192, one launch (start us, length us, event | category | flops | bytes accessed | tf_op | source)
XLA Modules:
  0.0 60.0 jit_solution(15698435406009579033)
XLA Ops:
  0.0 0.8 %select_convert_fusion = f32[8,128]{1,0:T(8,128)S(1)} fusion(s32[8,128]{1,0:T(8,128)} %param.8, s32[8,128]{1,0:T(8,128)} %param.7), kind=kLoop, calls=%fused_computation.103 | loop fusion | flops 3072 | bytes 12288 | tf_op jit(solution)/shard_map/convert_element_type | solution.py:103
  0.8 1.5 %broadcast_select_fusion.1 = (f32[101,4,128]{2,1,0:T(4,128)S(1)}, f32[101,4,128]{2,1,0:T(4,128)S(1)}) fusion(pred[]{:T(512)S(6)} %eq.25, f32[1,8,128]{2,1,0:T(8,128)S(1)} %bitcast.49, f32[100,8,128]{2,1,0:T(8,128)} %bitcast.43), kind=kLoop, calls=%fused_computation.76 | loop fusion | flops 258560 | bytes 827393 | tf_op jit(solution)/shard_map/jit(_where)/select_n | solution.py:34
  2.2 2.0 %collective-permute-start.1 = (f32[101,4,128]{2,1,0:T(4,128)S(1)}, f32[101,4,128]{2,1,0:T(4,128)S(1)}, u32[]{:S(2)}, u32[]{:S(2)}) collective-permute-start(f32[101,4,128]{2,1,0:T(4,128)S(1)} %get-tuple-element.17), channel_id=1, source_target_pairs={{1,2},{3,4},{5,6},{2,1},{4,3},{6,5},{9,10},{11,12},{13,14},{10,9},... | collective-permute-start | bytes 620552 | tf_op jit(solution)/shard_map/ppermute | solution.py:34
  4.3 14.1 %collective-permute-start = (f32[101,4,128]{2,1,0:T(4,128)S(1)}, f32[101,4,128]{2,1,0:T(4,128)S(1)}, u32[]{:S(2)}, u32[]{:S(2)}) collective-permute-start(f32[101,4,128]{2,1,0:T(4,128)S(1)} %get-tuple-element.18), channel_id=1, source_target_pairs={{0,1},{1,0},{2,3},{3,2},{4,5},{5,4},{6,7},{7,6},{8,9},{9,8},{10,11... | collective-permute-start | bytes 620552 | tf_op jit(solution)/shard_map/ppermute | solution.py:35
  18.4 0.7 %broadcast_in_dim.37 = f32[4,25]{1,0:T(4,128)S(1)} broadcast(f32[4]{0:T(128)} %constant.110.clone), dimensions={0} | broadcast | bytes 416 | tf_op jit(solution)/shard_map/broadcast_in_dim | solution.py:106
  19.5 0.4 rev.4
  20.0 7.5 %collective-permute-done = f32[101,4,128]{2,1,0:T(4,128)S(1)} collective-permute-done((f32[101,4,128]{2,1,0:T(4,128)S(1)}, f32[101,4,128]{2,1,0:T(4,128)S(1)}, u32[]{:S(2)}, u32[]{:S(2)}) %collective-permute-start) | collective-permute-done | bytes 206880 | tf_op jit(solution)/shard_map/ppermute | solution.py:35
  27.8 0.3 slice_select_fusion
  28.1 0.4 select_n.121
  28.5 5.0 %collective-permute-start.3 = (f32[6464]{0:T(1024)S(1)}, f32[6464]{0:T(1024)S(1)}, u32[]{:S(2)}, u32[]{:S(2)}) collective-permute-start(f32[6464]{0:T(1024)S(1)} %select_n.121), channel_id=1, source_target_pairs={{8,16},{24,32},{40,48},{56,64},{72,80},{88,96},{104,112},{120,128}... | collective-permute-start | bytes 77576 | tf_op jit(solution)/shard_map/ppermute | solution.py:53
  33.9 0.4 select_n.123
  34.3 1.9 %collective-permute-start.2 = (f32[6464]{0:T(1024)S(1)}, f32[6464]{0:T(1024)S(1)}, u32[]{:S(2)}, u32[]{:S(2)}) collective-permute-start(f32[6464]{0:T(1024)S(1)} %select_n.123), channel_id=1, source_target_pairs={{0,8},{8,0},{16,24},{24,16},{32,40},{40,32},{48,56},{56,48},{64,72... | collective-permute-start | bytes 77576 | tf_op jit(solution)/shard_map/ppermute | solution.py:56
  36.3 1.1 %collective-permute-done.2 = f32[6464]{0:T(1024)S(1)} collective-permute-done((f32[6464]{0:T(1024)S(1)}, f32[6464]{0:T(1024)S(1)}, u32[]{:S(2)}, u32[]{:S(2)}) %collective-permute-start.2) | collective-permute-done | bytes 25888 | tf_op jit(solution)/shard_map/ppermute | solution.py:56
  37.4 0.8 %slice.251 = f32[100,16,4]{2,1,0:T(8,128)S(1)} reshape(f32[6400]{0:T(1024)S(1)} %bitcast.47) | data formatting | bytes 51200 | tf_op jit(solution)/shard_map/slice | solution.py:61
  38.2 0.8 %concatenate.38 = f32[4,25,16,4]{3,2,1,0:T(8,128)S(1)} reshape(f32[6400]{0:T(1024)S(1)} %bitcast.48) | data formatting | bytes 51200 | tf_op jit(solution)/shard_map/concatenate | solution.py:61
  39.1 7.6 %collective-permute-done.3 = f32[6464]{0:T(1024)S(1)} collective-permute-done((f32[6464]{0:T(1024)S(1)}, f32[6464]{0:T(1024)S(1)}, u32[]{:S(2)}, u32[]{:S(2)}) %collective-permute-start.3) | collective-permute-done | bytes 25888 | tf_op jit(solution)/shard_map/ppermute | solution.py:53
  46.7 1.7 %slice.252 = f32[100,16,4]{2,1,0:T(8,128)} reshape(f32[6400]{0:T(1024)S(1)} %bitcast.45) | data formatting | bytes 51200 | tf_op jit(solution)/shard_map/slice | solution.py:61
  48.4 0.8 %concatenate.40 = f32[4,25,16,4]{3,2,1,0:T(8,128)S(1)} reshape(f32[6400]{0:T(1024)S(1)} %bitcast.46) | data formatting | bytes 51200 | tf_op jit(solution)/shard_map/concatenate | solution.py:61
  49.2 2.3 %fusion.1 = f32[100,16,136]{2,1,0:T(8,128)S(1)} fusion(f32[100,16,128]{2,1,0:T(8,128)S(1)} %slice.292, f32[100,16,4]{2,1,0:T(8,128)} %slice.252, f32[100,16,4]{2,1,0:T(8,128)S(1)} %slice.251, pred[]{:T(512)S(6)} %eq.24), kind=kLoop, calls=%fused_computation.5 | loop fusion | flops 1088000 | bytes 1740801 | tf_op jit(solution)/shard_map/jit(_where)/select_n | solution.py:59
  52.1 0.9 %fusion.4 = f32[4,25,16,136]{3,2,1,0:T(8,128)S(1)} fusion(f32[4,25,16,128]{3,2,1,0:T(8,128)S(1)} %bitcast.42, f32[4,25,16,4]{3,2,1,0:T(8,128)S(1)} %concatenate.40, f32[4,25,16,4]{3,2,1,0:T(8,128)S(1)} %concatenate.38, pred[]{:T(512)S(6)} %eq.24), kind=kLoop, calls=%fused_computation.8 | loop fusion | flops 1088000 | bytes 1740801 | tf_op jit(solution)/shard_map/jit(_where)/select_n | solution.py:59
  53.0 1.0 %fusion.38 = (f32[1,25,12,132]{3,2,1,0:T(8,128)S(1)}, f32[1,25,12,132]{3,2,1,0:T(8,128)S(1)}, f32[25,12,132]{2,1,0:T(8,128)S(1)}, f32[25,12,132]{2,1,0:T(8,128)S(1)}) fusion(f32[25,16,136]{2,1,0:T(8,128)S(1)} %reduce-window_multiply_fusion.1, f32[4,25,16,136]{3,2,1,0:T(8,128)S(1)} %fusion.4, f32[12]{0:T(128)S(1)} %get-tuple-element.21, ...), kind=kLoop, calls=%fused_computation.57 | loop fusion | flops 633600 | bytes 2217696 | tf_op jit(solution)/shard_map/stack | solution.py:95
  54.1 3.7 %fusion.14 = f32[4,25,12,132]{3,2,1,0:T(8,128)S(1)} fusion(f32[4,25,16,136]{3,2,1,0:T(8,128)S(1)} %fusion.4, f32[1,25,12,132]{3,2,1,0:T(8,128)S(1)} %get-tuple-element.10, f32[1,25,12,132]{3,2,1,0:T(8,128)S(1)} %get-tuple-element.9, f32[4]{0:T(128)S(1)} %pad.3.clone, f32[25,12,132]{2,1,0:T(8,128)S(1)} %get-tuple-element.14, ...), kind=kLoop, calls=%fused_computation.19 | loop fusion | flops 3960000 | bytes 7128028 | tf_op jit(solution)/shard_map/jit(_where)/select_n | solution.py:119
  58.0 0.3 fusion.57
  58.3 1.7 %fusion.27 = f32[4,25,8,128]{3,2,1,0:T(8,128)} fusion(f32[4,25,12,132]{3,2,1,0:T(8,128)S(1)} %fusion.14, f32[1,25,8,128]{3,2,1,0:T(8,128)S(1)} %get-tuple-element.8, f32[1,25,8,128]{3,2,1,0:T(8,128)S(1)} %get-tuple-element.7, f32[4]{0:T(128)S(1)} %pad.3.clone, f32[25,8,128]{2,1,0:T(8,128)S(1)} %get-tuple-element.12, f32[25,8,128]{2,1,0:T(8,128)S(1)} %get-tuple-element.11, ...), kind=kLoop, calls=%fused_computation.42 | loop fusion | flops 2457600 | bytes 4608016 | tf_op jit(solution)/shard_map/mul | solution.py:98
  (25 shorter events, 1.7 us)
Async XLA Ops:
  0.0 27.6 %copy-start = (f32[4,25,8,128]{3,2,1,0:T(8,128)S(1)}, f32[4,25,8,128]{3,2,1,0:T(8,128)}, u32[]{:S(2)}) copy-start(f32[4,25,8,128]{3,2,1,0:T(8,128)} %param.6) | copy-start | bytes 1228804
  2.2 17.3 %collective-permute-start.1 = (f32[101,4,128]{2,1,0:T(4,128)S(1)}, f32[101,4,128]{2,1,0:T(4,128)S(1)}, u32[]{:S(2)}, u32[]{:S(2)}) collective-permute-start(f32[101,4,128]{2,1,0:T(4,128)S(1)} %get-tuple-element.17), channel_id=1, source_target_pairs={{1,2},{3,4},{5,6},{2,1},{4,3},{6,5},{9,10},{11,12},{13,14},{10,9},... | collective-permute-start | bytes 620552 | tf_op jit(solution)/shard_map/ppermute | solution.py:34
  4.3 23.2 %collective-permute-start = (f32[101,4,128]{2,1,0:T(4,128)S(1)}, f32[101,4,128]{2,1,0:T(4,128)S(1)}, u32[]{:S(2)}, u32[]{:S(2)}) collective-permute-start(f32[101,4,128]{2,1,0:T(4,128)S(1)} %get-tuple-element.18), channel_id=1, source_target_pairs={{0,1},{1,0},{2,3},{3,2},{4,5},{5,4},{6,7},{7,6},{8,9},{9,8},{10,11... | collective-permute-start | bytes 620552 | tf_op jit(solution)/shard_map/ppermute | solution.py:35
  28.5 18.1 %collective-permute-start.3 = (f32[6464]{0:T(1024)S(1)}, f32[6464]{0:T(1024)S(1)}, u32[]{:S(2)}, u32[]{:S(2)}) collective-permute-start(f32[6464]{0:T(1024)S(1)} %select_n.121), channel_id=1, source_target_pairs={{8,16},{24,32},{40,48},{56,64},{72,80},{88,96},{104,112},{120,128}... | collective-permute-start | bytes 77576 | tf_op jit(solution)/shard_map/ppermute | solution.py:53
  34.3 3.1 %collective-permute-start.2 = (f32[6464]{0:T(1024)S(1)}, f32[6464]{0:T(1024)S(1)}, u32[]{:S(2)}, u32[]{:S(2)}) collective-permute-start(f32[6464]{0:T(1024)S(1)} %select_n.123), channel_id=1, source_target_pairs={{0,8},{8,0},{16,24},{24,16},{32,40},{40,32},{48,56},{56,48},{64,72... | collective-permute-start | bytes 77576 | tf_op jit(solution)/shard_map/ppermute | solution.py:56

commit v17 on v13

--- a/solution.py
+++ b/solution.py
@@ -44,18 +44,21 @@
 
     lon = lax.axis_index("lon")
     lon_odd = lon % 2 == 1
-    edge_shape = lat_wide[..., :WIDE].shape
-    east_cols = lat_wide[..., -WIDE:].reshape(-1)
-    west_cols = lat_wide[..., :WIDE].reshape(-1)
+    used = lat_wide[:, MARGIN:-MARGIN]
+    edge_shape = used[..., :WIDE].shape
+    east_cols = used[..., -WIDE:].reshape(-1)
+    west_cols = used[..., :WIDE].reshape(-1)
     across = [(m, (m + 1) % n_lon) for m in range(1, n_lon, 2)]
     across = across + [(j, i) for i, j in across]
     off_send = jnp.where(lon_odd, east_cols, west_cols)
     off_chip = lax.ppermute(off_send, "lon", across)
     off_send, later = lax.optimization_barrier((off_send, lat_wide))
+    later = later[:, MARGIN:-MARGIN]
     on_send = jnp.where(lon_odd, later[..., :WIDE].reshape(-1), later[..., -WIDE:].reshape(-1))
     on_chip = lax.ppermute(on_send, "lon", [(m, m ^ 1) for m in range(n_lon)])
-    west = jnp.where(lon_odd, on_chip, off_chip).reshape(edge_shape)
-    east = jnp.where(lon_odd, off_chip, on_chip).reshape(edge_shape)
+    rim = ((0, 0), (MARGIN, MARGIN), (0, 0))
+    west = jnp.pad(jnp.where(lon_odd, on_chip, off_chip).reshape(edge_shape), rim)
+    east = jnp.pad(jnp.where(lon_odd, off_chip, on_chip).reshape(edge_shape), rim)
     wide_state = jnp.concatenate([west[:-1], lat_wide[:-1], east[:-1]], axis=2)
     wide_depth = jnp.concatenate([west[-1], lat_wide[-1], east[-1]], axis=1)
     return wide_state, wide_depth

time: 56.8 us -> 56.1 us (0.988)
  local copies, waits for them, and re-layouts: 3.98 us -> 3.28 us
    slice x4 -> x3, local copies, waits for them, and re-layouts: 1.67 us -> 0.95 us  [gather_wide(): wide_state = jnp.concatenate([west[:-1], lat_wide[:-1], east[:-1]], axis=2)]
    reshape x0 -> x2, local copies, waits for them, and re-layouts: none -> 0.6 us  [the longest x1 0.3 us: gather_wide(): jnp.where(lon_odd, on_chip, off_chip).reshape(edge_shape)]
where the time goes in v17:
time: 56.1 us; the launch traced here: 55.8 us
  starting transfers between devices  23.3 us (42%)
  waiting for transfers between devices  17.6 us (31%)
  other arithmetic  11.4 us (20%)
  local copies, waits for them, and re-layouts  3.28 us (6%)
    ppermute x1, starting transfers between devices, gather_wide(): lax.ppermute(jnp.where(odd, bottom_rows, top_rows), ('lon', 'lat'), [(l *...  14.1 us
    ppermute x1, waiting for transfers between devices, gather_wide(): off_chip = lax.ppermute(off_send, 'lon', across)  9.2 us
    ppermute x1, waiting for transfers between devices, gather_wide(): lax.ppermute(jnp.where(odd, bottom_rows, top_rows), ('lon', 'lat'), [(l *...  7.31 us
    ppermute x1, starting transfers between devices, gather_wide(): off_chip = lax.ppermute(off_send, 'lon', across)  5.22 us
    select_n x1, other arithmetic, shards(): once = jnp.where(south_edge[:, None], 0.0, once)  3.74 us
    ppermute x1, starting transfers between devices, gather_wide(): lax.ppermute(jnp.where(odd, top_rows, bottom_rows), ('lon', 'lat'), pairs)  2.02 us
    ppermute x1, starting transfers between devices, gather_wide(): on_chip = lax.ppermute(on_send, 'lon', [(m, m ^ 1) for m in range(n_lon)])  1.92 us
    mul x1, other arithmetic, advance(): return wet * (centre + TIME_INCREMENT * (tendency + forcing))  1.68 us
  transfers between devices with their start and end apart: 4, of which 3 were waited for; matrix products, arithmetic and copies ran while one was open for 4% of the time, Pallas kernels for 0%

profile of v17, /device:TPU:192, one launch (start us, length us, event | category | flops | bytes accessed | tf_op | source)
XLA Modules:
  0.0 55.8 jit_solution(4358781507910554380)
XLA Ops:
  0.0 0.8 %select_convert_fusion = f32[8,128]{1,0:T(8,128)S(1)} fusion(s32[8,128]{1,0:T(8,128)} %param.8, s32[8,128]{1,0:T(8,128)} %param.7), kind=kLoop, calls=%fused_computation.99 | loop fusion | flops 3072 | bytes 12288 | tf_op jit(solution)/shard_map/convert_element_type | solution.py:98
  0.8 1.5 %broadcast_select_fusion.1 = (f32[101,4,128]{2,1,0:T(4,128)S(1)}, f32[101,4,128]{2,1,0:T(4,128)S(1)}) fusion(pred[]{:T(512)S(6)} %eq.25, f32[1,8,128]{2,1,0:T(8,128)S(1)} %bitcast.48, f32[100,8,128]{2,1,0:T(8,128)} %bitcast.46), kind=kLoop, calls=%fused_computation.71 | loop fusion | flops 258560 | bytes 827393 | tf_op jit(solution)/shard_map/jit(_where)/select_n | solution.py:34
  2.2 2.0 %collective-permute-start.1 = (f32[101,4,128]{2,1,0:T(4,128)S(1)}, f32[101,4,128]{2,1,0:T(4,128)S(1)}, u32[]{:S(2)}, u32[]{:S(2)}) collective-permute-start(f32[101,4,128]{2,1,0:T(4,128)S(1)} %get-tuple-element.17), channel_id=1, source_target_pairs={{1,2},{3,4},{5,6},{2,1},{4,3},{6,5},{9,10},{11,12},{13,14},{10,9},... | collective-permute-start | bytes 620552 | tf_op jit(solution)/shard_map/ppermute | solution.py:34
  4.3 14.1 %collective-permute-start = (f32[101,4,128]{2,1,0:T(4,128)S(1)}, f32[101,4,128]{2,1,0:T(4,128)S(1)}, u32[]{:S(2)}, u32[]{:S(2)}) collective-permute-start(f32[101,4,128]{2,1,0:T(4,128)S(1)} %get-tuple-element.18), channel_id=1, source_target_pairs={{0,1},{1,0},{2,3},{3,2},{4,5},{5,4},{6,7},{7,6},{8,9},{9,8},{10,11... | collective-permute-start | bytes 620552 | tf_op jit(solution)/shard_map/ppermute | solution.py:35
  18.4 0.7 %broadcast_in_dim.37 = f32[4,25]{1,0:T(4,128)S(1)} broadcast(f32[4]{0:T(128)} %constant.111.clone), dimensions={0} | broadcast | bytes 416 | tf_op jit(solution)/shard_map/broadcast_in_dim | solution.py:101
  19.5 0.4 rev.4
  20.0 7.3 %collective-permute-done = f32[101,4,128]{2,1,0:T(4,128)S(1)} collective-permute-done((f32[101,4,128]{2,1,0:T(4,128)S(1)}, f32[101,4,128]{2,1,0:T(4,128)S(1)}, u32[]{:S(2)}, u32[]{:S(2)}) %collective-permute-start) | collective-permute-done | bytes 206880 | tf_op jit(solution)/shard_map/ppermute | solution.py:35
  27.6 0.3 slice_select_fusion
  27.9 0.2 select_n.110
  28.2 5.2 %collective-permute-start.3 = (f32[4848]{0:T(1024)S(1)}, f32[4848]{0:T(1024)S(1)}, u32[]{:S(2)}, u32[]{:S(2)}) collective-permute-start(f32[4848]{0:T(1024)S(1)} %select_n.110), channel_id=1, source_target_pairs={{8,16},{24,32},{40,48},{56,64},{72,80},{88,96},{104,112},{120,128}... | collective-permute-start | bytes 58184 | tf_op jit(solution)/shard_map/ppermute | solution.py:54
  33.4 0.3 slice_select_fusion.1
  33.7 0.2 select_n.112
  33.9 1.9 %collective-permute-start.2 = (f32[4848]{0:T(1024)S(1)}, f32[4848]{0:T(1024)S(1)}, u32[]{:S(2)}, u32[]{:S(2)}) collective-permute-start(f32[4848]{0:T(1024)S(1)} %select_n.112), channel_id=1, source_target_pairs={{0,8},{8,0},{16,24},{24,16},{32,40},{40,32},{48,56},{56,48},{64,72... | collective-permute-start | bytes 58184 | tf_op jit(solution)/shard_map/ppermute | solution.py:58
  35.9 1.1 %collective-permute-done.2 = f32[4848]{0:T(1024)S(1)} collective-permute-done((f32[4848]{0:T(1024)S(1)}, f32[4848]{0:T(1024)S(1)}, u32[]{:S(2)}, u32[]{:S(2)}) %collective-permute-start.2) | collective-permute-done | bytes 19424 | tf_op jit(solution)/shard_map/ppermute | solution.py:58
  37.0 9.2 %collective-permute-done.3 = f32[4848]{0:T(1024)S(1)} collective-permute-done((f32[4848]{0:T(1024)S(1)}, f32[4848]{0:T(1024)S(1)}, u32[]{:S(2)}, u32[]{:S(2)}) %collective-permute-start.3) | collective-permute-done | bytes 19424 | tf_op jit(solution)/shard_map/ppermute | solution.py:54
  46.2 0.3 reshape.86
  46.5 0.3 reshape.87
  46.9 0.2 pad_slice_fusion
  47.3 0.7 %slice-done = f32[100,16,128]{2,1,0:T(8,128)S(1)} async-done(((f32[101,16,128]{2,1,0:T(8,128)}), f32[100,16,128]{2,1,0:T(8,128)S(1)}, s32[]{:S(2)}) %slice-start) | async-done | bytes 819224 | tf_op jit(solution)/shard_map/slice | solution.py:62
  48.0 0.7 %pad_maximum_fusion = f32[100,16,136]{2,1,0:T(8,128)S(1)} fusion(f32[100,16,4]{2,1,0:T(8,128)S(1)} %get-tuple-element.21, f32[100,16,128]{2,1,0:T(8,128)S(1)} %slice-done, f32[100,16,4]{2,1,0:T(8,128)S(1)} %get-tuple-element.22), kind=kLoop, calls=%fused_computation.13 | loop fusion | flops 435200 | bytes 1740800 | tf_op jit(solution)/shard_map/concatenate | solution.py:62
  48.9 1.0 %fusion.32 = (f32[1,25,12,132]{3,2,1,0:T(8,128)S(1)}, f32[1,25,12,132]{3,2,1,0:T(8,128)S(1)}, f32[25,12,132]{2,1,0:T(8,128)S(1)}, f32[25,12,132]{2,1,0:T(8,128)S(1)}) fusion(f32[25,16,136]{2,1,0:T(8,128)S(1)} %reduce-window_multiply_fusion.1, f32[4,25,16,136]{3,2,1,0:T(8,128)S(1)} %bitcast.44, f32[12]{0:T(128)S(1)} %get-tuple-element.25, ...), kind=kLoop, calls=%fused_computation.52 | loop fusion | flops 633600 | bytes 2217696 | tf_op jit(solution)/shard_map/stack | solution.py:90
  49.9 3.7 %fusion.8 = f32[4,25,12,132]{3,2,1,0:T(8,128)S(1)} fusion(f32[4,25,16,136]{3,2,1,0:T(8,128)S(1)} %bitcast.45, f32[1,25,12,132]{3,2,1,0:T(8,128)S(1)} %get-tuple-element.10, f32[1,25,12,132]{3,2,1,0:T(8,128)S(1)} %get-tuple-element.9, f32[4]{0:T(128)S(1)} %pad.12.clone, f32[25,12,132]{2,1,0:T(8,128)S(1)} %get-tuple-element.14, ...), kind=kLoop, calls=%fused_computation.9 | loop fusion | flops 3960000 | bytes 7128028 | tf_op jit(solution)/shard_map/jit(_where)/select_n | solution.py:114
  53.8 0.3 fusion.51
  54.1 1.7 %fusion.21 = f32[4,25,8,128]{3,2,1,0:T(8,128)} fusion(f32[4,25,12,132]{3,2,1,0:T(8,128)S(1)} %fusion.8, f32[1,25,8,128]{3,2,1,0:T(8,128)S(1)} %get-tuple-element.8, f32[1,25,8,128]{3,2,1,0:T(8,128)S(1)} %get-tuple-element.7, f32[4]{0:T(128)S(1)} %pad.12.clone, f32[25,8,128]{2,1,0:T(8,128)S(1)} %get-tuple-element.12, f32[25,8,128]{2,1,0:T(8,128)S(1)} %get-tuple-element.11, ...), kind=kLoop, calls=%fused_computation.37 | loop fusion | flops 2457600 | bytes 4608016 | tf_op jit(solution)/shard_map/mul | solution.py:93
  (24 shorter events, 1.2 us)
Async XLA Ops:
  0.0 27.5 %copy-start.1 = (f32[4,25,8,128]{3,2,1,0:T(8,128)S(1)}, f32[4,25,8,128]{3,2,1,0:T(8,128)}, u32[]{:S(2)}) copy-start(f32[4,25,8,128]{3,2,1,0:T(8,128)} %param.6) | copy-start | bytes 1228804
  2.2 17.3 %collective-permute-start.1 = (f32[101,4,128]{2,1,0:T(4,128)S(1)}, f32[101,4,128]{2,1,0:T(4,128)S(1)}, u32[]{:S(2)}, u32[]{:S(2)}) collective-permute-start(f32[101,4,128]{2,1,0:T(4,128)S(1)} %get-tuple-element.17), channel_id=1, source_target_pairs={{1,2},{3,4},{5,6},{2,1},{4,3},{6,5},{9,10},{11,12},{13,14},{10,9},... | collective-permute-start | bytes 620552 | tf_op jit(solution)/shard_map/ppermute | solution.py:34
  4.3 23.0 %collective-permute-start = (f32[101,4,128]{2,1,0:T(4,128)S(1)}, f32[101,4,128]{2,1,0:T(4,128)S(1)}, u32[]{:S(2)}, u32[]{:S(2)}) collective-permute-start(f32[101,4,128]{2,1,0:T(4,128)S(1)} %get-tuple-element.18), channel_id=1, source_target_pairs={{0,1},{1,0},{2,3},{3,2},{4,5},{5,4},{6,7},{7,6},{8,9},{9,8},{10,11... | collective-permute-start | bytes 620552 | tf_op jit(solution)/shard_map/ppermute | solution.py:35
  27.6 8.2 %copy-start = (f32[101,16,128]{2,1,0:T(8,128)}, f32[101,16,128]{2,1,0:T(8,128)S(1)}, u32[]{:S(2)}) copy-start(f32[101,16,128]{2,1,0:T(8,128)S(1)} %pad_maximum_fusion.1) | copy-start | bytes 2482180
  28.2 18.0 %collective-permute-start.3 = (f32[4848]{0:T(1024)S(1)}, f32[4848]{0:T(1024)S(1)}, u32[]{:S(2)}, u32[]{:S(2)}) collective-permute-start(f32[4848]{0:T(1024)S(1)} %select_n.110), channel_id=1, source_target_pairs={{8,16},{24,32},{40,48},{56,64},{72,80},{88,96},{104,112},{120,128}... | collective-permute-start | bytes 58184 | tf_op jit(solution)/shard_map/ppermute | solution.py:54
  33.9 3.1 %collective-permute-start.2 = (f32[4848]{0:T(1024)S(1)}, f32[4848]{0:T(1024)S(1)}, u32[]{:S(2)}, u32[]{:S(2)}) collective-permute-start(f32[4848]{0:T(1024)S(1)} %select_n.112), channel_id=1, source_target_pairs={{0,8},{8,0},{16,24},{24,16},{32,40},{40,32},{48,56},{56,48},{64,72... | collective-permute-start | bytes 58184 | tf_op jit(solution)/shard_map/ppermute | solution.py:58
  46.8 1.1 %slice-start = ((f32[101,16,128]{2,1,0:T(8,128)}), f32[100,16,128]{2,1,0:T(8,128)S(1)}, s32[]{:S(2)}) async-start(f32[101,16,128]{2,1,0:T(8,128)} %copy-done), calls=%async_computation | async-start | bytes 1638400 | tf_op jit(solution)/shard_map/slice | solution.py:62

commit v18 on v17

--- a/solution.py
+++ b/solution.py
@@ -59,8 +59,10 @@
     rim = ((0, 0), (MARGIN, MARGIN), (0, 0))
     west = jnp.pad(jnp.where(lon_odd, on_chip, off_chip).reshape(edge_shape), rim)
     east = jnp.pad(jnp.where(lon_odd, off_chip, on_chip).reshape(edge_shape), rim)
-    wide_state = jnp.concatenate([west[:-1], lat_wide[:-1], east[:-1]], axis=2)
-    wide_depth = jnp.concatenate([west[-1], lat_wide[-1], east[-1]], axis=1)
+    lat_state = jnp.concatenate([south[:-1], x[:-1], north[:-1]], axis=1)
+    lat_depth = jnp.concatenate([south[-1], x[-1], north[-1]], axis=0)
+    wide_state = jnp.concatenate([west[:-1], lat_state, east[:-1]], axis=2)
+    wide_depth = jnp.concatenate([west[-1], lat_depth, east[-1]], axis=1)
     return wide_state, wide_depth
 
 

time: 56.1 us -> 55.8 us (level)
  local copies, waits for them, and re-layouts: 3.28 us -> 2.6 us
    slice x3, local copies, waits for them, and re-layouts: 0.95 us -> 0.28 us  [the longest x1 0.25 us: gather_wide(): wide_state = jnp.concatenate([west[:-1], lat_state, east[:-1]], axis=2)]
where the time goes in v18:
time: 55.8 us; the launch traced here: 55.6 us
  starting transfers between devices  23.3 us (42%)
  waiting for transfers between devices  17.6 us (32%)
  other arithmetic  11.8 us (21%)
  local copies, waits for them, and re-layouts  2.6 us (5%)
    ppermute x1, starting transfers between devices, gather_wide(): lax.ppermute(jnp.where(odd, bottom_rows, top_rows), ('lon', 'lat'), [(l *...  14.1 us
    ppermute x1, waiting for transfers between devices, gather_wide(): off_chip = lax.ppermute(off_send, 'lon', across)  9.2 us
    ppermute x1, waiting for transfers between devices, gather_wide(): lax.ppermute(jnp.where(odd, bottom_rows, top_rows), ('lon', 'lat'), [(l *...  7.31 us
    ppermute x1, starting transfers between devices, gather_wide(): off_chip = lax.ppermute(off_send, 'lon', across)  5.22 us
    select_n x1, other arithmetic, shards(): once = jnp.where(south_edge[:, None], 0.0, once)  3.74 us
    ppermute x1, starting transfers between devices, gather_wide(): lax.ppermute(jnp.where(odd, top_rows, bottom_rows), ('lon', 'lat'), pairs)  2.02 us
    ppermute x1, starting transfers between devices, gather_wide(): on_chip = lax.ppermute(on_send, 'lon', [(m, m ^ 1) for m in range(n_lon)])  1.92 us
    mul x1, other arithmetic, advance(): return wet * (centre + TIME_INCREMENT * (tendency + forcing))  1.68 us
  transfers between devices with their start and end apart: 4, of which 3 were waited for; matrix products, arithmetic and copies ran while one was open for 4% of the time, Pallas kernels for 0%

profile of v18, /device:TPU:192, one launch (start us, length us, event | category | flops | bytes accessed | tf_op | source)
XLA Modules:
  0.0 55.6 jit_solution(8779419769788703099)
XLA Ops:
  0.0 0.8 %select_convert_fusion = f32[8,128]{1,0:T(8,128)S(1)} fusion(s32[8,128]{1,0:T(8,128)} %param.8, s32[8,128]{1,0:T(8,128)} %param.7), kind=kLoop, calls=%fused_computation.100 | loop fusion | flops 3072 | bytes 12288 | tf_op jit(solution)/shard_map/convert_element_type | solution.py:100
  0.8 1.5 %broadcast_select_fusion.1 = (f32[101,4,128]{2,1,0:T(4,128)S(1)}, f32[101,4,128]{2,1,0:T(4,128)S(1)}) fusion(pred[]{:T(512)S(6)} %eq.25, f32[1,8,128]{2,1,0:T(8,128)S(1)} %bitcast.51, f32[100,8,128]{2,1,0:T(8,128)} %bitcast.48), kind=kLoop, calls=%fused_computation.71 | loop fusion | flops 258560 | bytes 827393 | tf_op jit(solution)/shard_map/jit(_where)/select_n | solution.py:34
  2.2 2.0 %collective-permute-start.1 = (f32[101,4,128]{2,1,0:T(4,128)S(1)}, f32[101,4,128]{2,1,0:T(4,128)S(1)}, u32[]{:S(2)}, u32[]{:S(2)}) collective-permute-start(f32[101,4,128]{2,1,0:T(4,128)S(1)} %get-tuple-element.17), channel_id=1, source_target_pairs={{1,2},{3,4},{5,6},{2,1},{4,3},{6,5},{9,10},{11,12},{13,14},{10,9},... | collective-permute-start | bytes 620552 | tf_op jit(solution)/shard_map/ppermute | solution.py:34
  4.2 14.1 %collective-permute-start = (f32[101,4,128]{2,1,0:T(4,128)S(1)}, f32[101,4,128]{2,1,0:T(4,128)S(1)}, u32[]{:S(2)}, u32[]{:S(2)}) collective-permute-start(f32[101,4,128]{2,1,0:T(4,128)S(1)} %get-tuple-element.18), channel_id=1, source_target_pairs={{0,1},{1,0},{2,3},{3,2},{4,5},{5,4},{6,7},{7,6},{8,9},{9,8},{10,11... | collective-permute-start | bytes 620552 | tf_op jit(solution)/shard_map/ppermute | solution.py:35
  18.4 0.7 %broadcast_in_dim.37 = f32[4,25]{1,0:T(4,128)S(1)} broadcast(f32[4]{0:T(128)} %constant.111.clone), dimensions={0} | broadcast | bytes 416 | tf_op jit(solution)/shard_map/broadcast_in_dim | solution.py:103
  19.5 0.4 rev.4
  19.9 7.3 %collective-permute-done = f32[101,4,128]{2,1,0:T(4,128)S(1)} collective-permute-done((f32[101,4,128]{2,1,0:T(4,128)S(1)}, f32[101,4,128]{2,1,0:T(4,128)S(1)}, u32[]{:S(2)}, u32[]{:S(2)}) %collective-permute-start) | collective-permute-done | bytes 206880 | tf_op jit(solution)/shard_map/ppermute | solution.py:35
  27.3 0.2 broadcast_select_fusion
  27.6 0.3 slice_select_fusion
  27.9 0.2 select_n.110
  28.1 5.2 %collective-permute-start.3 = (f32[4848]{0:T(1024)S(1)}, f32[4848]{0:T(1024)S(1)}, u32[]{:S(2)}, u32[]{:S(2)}) collective-permute-start(f32[4848]{0:T(1024)S(1)} %select_n.110), channel_id=1, source_target_pairs={{8,16},{24,32},{40,48},{56,64},{72,80},{88,96},{104,112},{120,128}... | collective-permute-start | bytes 58184 | tf_op jit(solution)/shard_map/ppermute | solution.py:54
  33.4 0.3 slice_select_fusion.1
  33.7 0.2 select_n.112
  33.9 1.9 %collective-permute-start.2 = (f32[4848]{0:T(1024)S(1)}, f32[4848]{0:T(1024)S(1)}, u32[]{:S(2)}, u32[]{:S(2)}) collective-permute-start(f32[4848]{0:T(1024)S(1)} %select_n.112), channel_id=1, source_target_pairs={{0,8},{8,0},{16,24},{24,16},{32,40},{40,32},{48,56},{56,48},{64,72... | collective-permute-start | bytes 58184 | tf_op jit(solution)/shard_map/ppermute | solution.py:58
  35.9 1.1 %collective-permute-done.2 = f32[4848]{0:T(1024)S(1)} collective-permute-done((f32[4848]{0:T(1024)S(1)}, f32[4848]{0:T(1024)S(1)}, u32[]{:S(2)}, u32[]{:S(2)}) %collective-permute-start.2) | collective-permute-done | bytes 19424 | tf_op jit(solution)/shard_map/ppermute | solution.py:58
  37.0 9.2 %collective-permute-done.3 = f32[4848]{0:T(1024)S(1)} collective-permute-done((f32[4848]{0:T(1024)S(1)}, f32[4848]{0:T(1024)S(1)}, u32[]{:S(2)}, u32[]{:S(2)}) %collective-permute-start.3) | collective-permute-done | bytes 19424 | tf_op jit(solution)/shard_map/ppermute | solution.py:54
  46.2 0.3 reshape.86
  46.5 0.3 reshape.87
  46.8 0.2 pad_slice_fusion
  47.3 1.2 %pad_maximum_fusion = f32[100,16,136]{2,1,0:T(8,128)S(1)} fusion(f32[100,16,4]{2,1,0:T(8,128)S(1)} %get-tuple-element.23, f32[100,4,128]{2,1,0:T(4,128)S(1)} %slice.257, f32[100,8,128]{2,1,0:T(8,128)S(1)} %bitcast.50, f32[100,4,128]{2,1,0:T(4,128)S(1)} %slice.256, f32[100,16,4]{2,1,0:T(8,128)S(1)} %get-tuple-element.24), kind=kLoop, calls=%fused_computation.13 | loop fusion | flops 870400 | bytes 1740800 | tf_op jit(solution)/shard_map/concatenate | solution.py:64
  48.6 1.0 %fusion.32 = (f32[1,25,12,132]{3,2,1,0:T(8,128)S(1)}, f32[1,25,12,132]{3,2,1,0:T(8,128)S(1)}, f32[25,12,132]{2,1,0:T(8,128)S(1)}, f32[25,12,132]{2,1,0:T(8,128)S(1)}) fusion(f32[25,16,136]{2,1,0:T(8,128)S(1)} %reduce-window_multiply_fusion.1, f32[4,25,16,136]{3,2,1,0:T(8,128)S(1)} %bitcast.46, f32[12]{0:T(128)S(1)} %get-tuple-element.27, ...), kind=kLoop, calls=%fused_computation.52 | loop fusion | flops 633600 | bytes 2217696 | tf_op jit(solution)/shard_map/stack | solution.py:92
  49.6 3.7 %fusion.8 = f32[4,25,12,132]{3,2,1,0:T(8,128)S(1)} fusion(f32[4,25,16,136]{3,2,1,0:T(8,128)S(1)} %bitcast.47, f32[1,25,12,132]{3,2,1,0:T(8,128)S(1)} %get-tuple-element.10, f32[1,25,12,132]{3,2,1,0:T(8,128)S(1)} %get-tuple-element.9, f32[4]{0:T(128)S(1)} %pad.12.clone, f32[25,12,132]{2,1,0:T(8,128)S(1)} %get-tuple-element.14, ...), kind=kLoop, calls=%fused_computation.9 | loop fusion | flops 3960000 | bytes 7128028 | tf_op jit(solution)/shard_map/jit(_where)/select_n | solution.py:116
  53.6 0.3 fusion.51
  53.9 1.7 %fusion.21 = f32[4,25,8,128]{3,2,1,0:T(8,128)} fusion(f32[4,25,12,132]{3,2,1,0:T(8,128)S(1)} %fusion.8, f32[1,25,8,128]{3,2,1,0:T(8,128)S(1)} %get-tuple-element.8, f32[1,25,8,128]{3,2,1,0:T(8,128)S(1)} %get-tuple-element.7, f32[4]{0:T(128)S(1)} %pad.12.clone, f32[25,8,128]{2,1,0:T(8,128)S(1)} %get-tuple-element.12, f32[25,8,128]{2,1,0:T(8,128)S(1)} %get-tuple-element.11, ...), kind=kLoop, calls=%fused_computation.37 | loop fusion | flops 2457600 | bytes 4608016 | tf_op jit(solution)/shard_map/mul | solution.py:95
  (22 shorter events, 1.1 us)
Async XLA Ops:
  0.0 27.4 %copy-start = (f32[4,25,8,128]{3,2,1,0:T(8,128)S(1)}, f32[4,25,8,128]{3,2,1,0:T(8,128)}, u32[]{:S(2)}) copy-start(f32[4,25,8,128]{3,2,1,0:T(8,128)} %param.6) | copy-start | bytes 1228804
  2.2 17.3 %collective-permute-start.1 = (f32[101,4,128]{2,1,0:T(4,128)S(1)}, f32[101,4,128]{2,1,0:T(4,128)S(1)}, u32[]{:S(2)}, u32[]{:S(2)}) collective-permute-start(f32[101,4,128]{2,1,0:T(4,128)S(1)} %get-tuple-element.17), channel_id=1, source_target_pairs={{1,2},{3,4},{5,6},{2,1},{4,3},{6,5},{9,10},{11,12},{13,14},{10,9},... | collective-permute-start | bytes 620552 | tf_op jit(solution)/shard_map/ppermute | solution.py:34
  4.2 23.0 %collective-permute-start = (f32[101,4,128]{2,1,0:T(4,128)S(1)}, f32[101,4,128]{2,1,0:T(4,128)S(1)}, u32[]{:S(2)}, u32[]{:S(2)}) collective-permute-start(f32[101,4,128]{2,1,0:T(4,128)S(1)} %get-tuple-element.18), channel_id=1, source_target_pairs={{0,1},{1,0},{2,3},{3,2},{4,5},{5,4},{6,7},{7,6},{8,9},{9,8},{10,11... | collective-permute-start | bytes 620552 | tf_op jit(solution)/shard_map/ppermute | solution.py:35
  28.1 18.0 %collective-permute-start.3 = (f32[4848]{0:T(1024)S(1)}, f32[4848]{0:T(1024)S(1)}, u32[]{:S(2)}, u32[]{:S(2)}) collective-permute-start(f32[4848]{0:T(1024)S(1)} %select_n.110), channel_id=1, source_target_pairs={{8,16},{24,32},{40,48},{56,64},{72,80},{88,96},{104,112},{120,128}... | collective-permute-start | bytes 58184 | tf_op jit(solution)/shard_map/ppermute | solution.py:54
  33.9 3.1 %collective-permute-start.2 = (f32[4848]{0:T(1024)S(1)}, f32[4848]{0:T(1024)S(1)}, u32[]{:S(2)}, u32[]{:S(2)}) collective-permute-start(f32[4848]{0:T(1024)S(1)} %select_n.112), channel_id=1, source_target_pairs={{0,8},{8,0},{16,24},{24,16},{32,40},{40,32},{48,56},{56,48},{64,72... | collective-permute-start | bytes 58184 | tf_op jit(solution)/shard_map/ppermute | solution.py:58

commit v19 on v18

--- a/solution.py
+++ b/solution.py
@@ -52,7 +52,7 @@
     across = across + [(j, i) for i, j in across]
     off_send = jnp.where(lon_odd, east_cols, west_cols)
     off_chip = lax.ppermute(off_send, "lon", across)
-    off_send, later = lax.optimization_barrier((off_send, lat_wide))
+    off_send, later, south, x, north = lax.optimization_barrier((off_send, lat_wide, south, x, north))
     later = later[:, MARGIN:-MARGIN]
     on_send = jnp.where(lon_odd, later[..., :WIDE].reshape(-1), later[..., -WIDE:].reshape(-1))
     on_chip = lax.ppermute(on_send, "lon", [(m, m ^ 1) for m in range(n_lon)])
@@ -61,7 +61,9 @@
     east = jnp.pad(jnp.where(lon_odd, off_chip, on_chip).reshape(edge_shape), rim)
     lat_state = jnp.concatenate([south[:-1], x[:-1], north[:-1]], axis=1)
     lat_depth = jnp.concatenate([south[-1], x[-1], north[-1]], axis=0)
-    wide_state = jnp.concatenate([west[:-1], lat_state, east[:-1]], axis=2)
+    wide_state = jnp.pad(lat_state, ((0, 0), (0, 0), (WIDE, WIDE)))
+    wide_state = lax.dynamic_update_slice(wide_state, west[:-1], (0, 0, 0))
+    wide_state = lax.dynamic_update_slice(wide_state, east[:-1], (0, 0, wide_state.shape[2] - WIDE))
     wide_depth = jnp.concatenate([west[-1], lat_depth, east[-1]], axis=1)
     return wide_state, wide_depth
 

time: 55.8 us -> 94 us (1.68)
  local copies, waits for them, and re-layouts: 2.6 us -> 40.4 us
  other arithmetic: 11.8 us -> 13.5 us
  waiting for transfers between devices: 17.6 us -> 16.2 us
    dynamic_update_slice x0 -> x2, local copies, waits for them, and re-layouts: none -> 36.6 us  [the longest x1 22.9 us: gather_wide(): lax.dynamic_update_slice(wide_state, east[:-1], (0, 0, wide_state.shape[2...]
    slice x1 -> x2, local copies, waits for them, and re-layouts: 0.25 us -> 2.04 us  [the longest x1 1.02 us: gather_wide(): east[:-1]]
    concatenate x1 -> x2, other arithmetic: 1.2 us -> 1.95 us  [the longest x1 1.03 us: shards(): jnp.concatenate([state.reshape(n_fields * level_count, tile_rows, tile_co...]
where the time goes in v19:
time: 94 us; the launch traced here: 93.7 us
  local copies, waits for them, and re-layouts  40.4 us (43%)
  starting transfers between devices  23.3 us (25%)
  waiting for transfers between devices  16.2 us (17%)
  other arithmetic  13.5 us (14%)
    dynamic_update_slice x1, local copies, waits for them, and re-layouts, gather_wide(): lax.dynamic_update_slice(wide_state, east[:-1], (0, 0, wide_state.shape[2...  22.9 us
    ppermute x1, starting transfers between devices, gather_wide(): lax.ppermute(jnp.where(odd, bottom_rows, top_rows), ('lon', 'lat'), [(l *...  14.1 us
    dynamic_update_slice x1, local copies, waits for them, and re-layouts, gather_wide(): wide_state = lax.dynamic_update_slice(wide_state, west[:-1], (0, 0, 0))  13.7 us
    ppermute x1, waiting for transfers between devices, gather_wide(): off_chip = lax.ppermute(off_send, 'lon', across)  9.11 us
    ppermute x1, waiting for transfers between devices, gather_wide(): lax.ppermute(jnp.where(odd, bottom_rows, top_rows), ('lon', 'lat'), [(l *...  6.91 us
    ppermute x1, starting transfers between devices, gather_wide(): off_chip = lax.ppermute(off_send, 'lon', across)  5.22 us
    select_n x1, other arithmetic, shards(): once = jnp.where(south_edge[:, None], 0.0, once)  3.74 us
    ppermute x1, starting transfers between devices, gather_wide(): lax.ppermute(jnp.where(odd, top_rows, bottom_rows), ('lon', 'lat'), pairs)  2.02 us
  transfers between devices with their start and end apart: 4, of which 3 were waited for; matrix products, arithmetic and copies ran while one was open for 4% of the time, Pallas kernels for 0%

profile of v19, /device:TPU:192, one launch (start us, length us, event | category | flops | bytes accessed | tf_op | source)
XLA Modules:
  0.0 93.7 jit_solution(4022835177353636372)
XLA Ops:
  0.0 0.7 select_convert_fusion
  0.7 1.6 %broadcast_select_fusion.1 = (f32[101,4,128]{2,1,0:T(4,128)S(1)}, f32[101,4,128]{2,1,0:T(4,128)S(1)}) fusion(pred[]{:T(512)S(6)} %eq.25, f32[1,8,128]{2,1,0:T(8,128)S(1)} %bitcast.53, f32[100,8,128]{2,1,0:T(8,128)} %bitcast.50), kind=kLoop, calls=%fused_computation.78 | loop fusion | flops 310272 | bytes 827393 | tf_op jit(solution)/shard_map/jit(_where)/select_n | solution.py:34
  2.3 2.0 %collective-permute-start.1 = (f32[101,4,128]{2,1,0:T(4,128)S(1)}, f32[101,4,128]{2,1,0:T(4,128)S(1)}, u32[]{:S(2)}, u32[]{:S(2)}) collective-permute-start(f32[101,4,128]{2,1,0:T(4,128)S(1)} %get-tuple-element.23), channel_id=1, source_target_pairs={{1,2},{3,4},{5,6},{2,1},{4,3},{6,5},{9,10},{11,12},{13,14},{10,9},... | collective-permute-start | bytes 620552 | tf_op jit(solution)/shard_map/ppermute | solution.py:34
  4.4 14.1 %collective-permute-start = (f32[101,4,128]{2,1,0:T(4,128)S(1)}, f32[101,4,128]{2,1,0:T(4,128)S(1)}, u32[]{:S(2)}, u32[]{:S(2)}) collective-permute-start(f32[101,4,128]{2,1,0:T(4,128)S(1)} %get-tuple-element.24), channel_id=1, source_target_pairs={{0,1},{1,0},{2,3},{3,2},{4,5},{5,4},{6,7},{7,6},{8,9},{9,8},{10,11... | collective-permute-start | bytes 620552 | tf_op jit(solution)/shard_map/ppermute | solution.py:35
  18.5 1.0 %pad_maximum_fusion.1 = f32[101,8,128]{2,1,0:T(8,128)S(1)} fusion(f32[1,8,128]{2,1,0:T(8,128)S(1)} %bitcast.54, f32[100,8,128]{2,1,0:T(8,128)} %bitcast.51), kind=kLoop, calls=%fused_computation.29 | loop fusion | flops 103424 | bytes 827392 | tf_op jit(solution)/shard_map/concatenate | solution.py:103
  20.0 0.4 rev.4
  20.5 6.9 %collective-permute-done = f32[101,4,128]{2,1,0:T(4,128)S(1)} collective-permute-done((f32[101,4,128]{2,1,0:T(4,128)S(1)}, f32[101,4,128]{2,1,0:T(4,128)S(1)}, u32[]{:S(2)}, u32[]{:S(2)}) %collective-permute-start) | collective-permute-done | bytes 206880 | tf_op jit(solution)/shard_map/ppermute | solution.py:35
  27.8 0.3 slice_select_fusion
  28.3 5.2 %collective-permute-start.3 = (f32[4848]{0:T(1024)S(1)}, f32[4848]{0:T(1024)S(1)}, u32[]{:S(2)}, u32[]{:S(2)}) collective-permute-start(f32[4848]{0:T(1024)S(1)} %select_n.110), channel_id=1, source_target_pairs={{8,16},{24,32},{40,48},{56,64},{72,80},{88,96},{104,112},{120,128}... | collective-permute-start | bytes 58184 | tf_op jit(solution)/shard_map/ppermute | solution.py:54
  33.6 0.3 slice_select_fusion.1
  34.1 1.9 %collective-permute-start.2 = (f32[4848]{0:T(1024)S(1)}, f32[4848]{0:T(1024)S(1)}, u32[]{:S(2)}, u32[]{:S(2)}) collective-permute-start(f32[4848]{0:T(1024)S(1)} %select_n.112), channel_id=1, source_target_pairs={{0,8},{8,0},{16,24},{24,16},{32,40},{40,32},{48,56},{56,48},{64,72... | collective-permute-start | bytes 58184 | tf_op jit(solution)/shard_map/ppermute | solution.py:58
  36.1 0.9 select_maximum_fusion
  37.2 9.1 %collective-permute-done.3 = f32[4848]{0:T(1024)S(1)} collective-permute-done((f32[4848]{0:T(1024)S(1)}, f32[4848]{0:T(1024)S(1)}, u32[]{:S(2)}, u32[]{:S(2)}) %collective-permute-start.3) | collective-permute-done | bytes 19424 | tf_op jit(solution)/shard_map/ppermute | solution.py:54
  46.3 0.3 reshape.86
  46.6 0.3 reshape.87
  46.9 1.0 %pad_slice_fusion.2 = f32[100,16,4]{2,1,0:T(8,128)} fusion(f32[101,12,4]{2,1,0:T(8,128)S(1)} %reshape.86), kind=kLoop, calls=%fused_computation.25 | loop fusion | bytes 44992 | tf_op jit(solution)/shard_map/slice | solution.py:65
  48.0 1.0 %pad_slice_fusion = f32[100,16,4]{2,1,0:T(8,128)} fusion(f32[101,12,4]{2,1,0:T(8,128)S(1)} %reshape.87), kind=kLoop, calls=%fused_computation.23 | loop fusion | bytes 44992 | tf_op jit(solution)/shard_map/slice | solution.py:66
  49.1 0.9 compare_convert_fusion
  49.9 13.7 %dynamic_update_slice.6 = f32[100,16,136]{2,1,0:T(8,128)S(1)} dynamic-update-slice(f32[100,16,136]{2,1,0:T(8,128)S(1)} %select_maximum_fusion, f32[100,16,4]{2,1,0:T(8,128)S(1)} %copy-done.1, s32[]{:T(128)} %constant.37.clone.1, s32[]{:T(128)} %constant.37.clone.1, s32[]{:T(128)} %constant.37.clone.1) | dynamic-update-slice | bytes 51204 | tf_op jit(solution)/shard_map/dynamic_update_slice | solution.py:65
  63.7 22.9 %dynamic_update_slice.7 = f32[100,16,136]{2,1,0:T(8,128)S(1)} dynamic-update-slice(f32[100,16,136]{2,1,0:T(8,128)S(1)} %dynamic_update_slice.6, f32[100,16,4]{2,1,0:T(8,128)S(1)} %copy-done.2, s32[]{:T(128)} %constant.37.clone.1, s32[]{:T(128)} %constant.37.clone.1, s32[]{:T(128)} %constant.47.clone.1) | dynamic-update-slice | bytes 51204 | tf_op jit(solution)/shard_map/dynamic_update_slice | solution.py:66
  86.8 1.0 %fusion.33 = (f32[1,25,12,132]{3,2,1,0:T(8,128)S(1)}, f32[1,25,12,132]{3,2,1,0:T(8,128)S(1)}, f32[25,12,132]{2,1,0:T(8,128)S(1)}, f32[25,12,132]{2,1,0:T(8,128)S(1)}) fusion(f32[25,16,136]{2,1,0:T(8,128)S(1)} %reduce-window_multiply_fusion.1, f32[4,25,16,136]{3,2,1,0:T(8,128)S(1)} %bitcast.48, f32[12]{0:T(128)S(1)} %get-tuple-element.31, ...), kind=kLoop, calls=%fused_computation.57 | loop fusion | flops 633600 | bytes 2217696 | tf_op jit(solution)/shard_map/stack | solution.py:94
  87.8 3.7 %fusion.8 = f32[4,25,12,132]{3,2,1,0:T(8,128)S(1)} fusion(f32[4,25,16,136]{3,2,1,0:T(8,128)S(1)} %bitcast.49, f32[1,25,12,132]{3,2,1,0:T(8,128)S(1)} %get-tuple-element.16, f32[1,25,12,132]{3,2,1,0:T(8,128)S(1)} %get-tuple-element.15, f32[4]{0:T(128)S(1)} %pad.17.clone, f32[25,12,132]{2,1,0:T(8,128)S(1)} %get-tuple-element.20, ...), kind=kLoop, calls=%fused_computation.11 | loop fusion | flops 3960000 | bytes 7128028 | tf_op jit(solution)/shard_map/jit(_where)/select_n | solution.py:118
  91.7 0.3 fusion.53
  92.0 1.7 %fusion.22 = f32[4,25,8,128]{3,2,1,0:T(8,128)} fusion(f32[4,25,12,132]{3,2,1,0:T(8,128)S(1)} %fusion.8, f32[1,25,8,128]{3,2,1,0:T(8,128)S(1)} %get-tuple-element.14, f32[1,25,8,128]{3,2,1,0:T(8,128)S(1)} %get-tuple-element.13, f32[4]{0:T(128)S(1)} %pad.17.clone, f32[25,8,128]{2,1,0:T(8,128)S(1)} %get-tuple-element.18, ...), kind=kLoop, calls=%fused_computation.42 | loop fusion | flops 2457600 | bytes 4608016 | tf_op jit(solution)/shard_map/mul | solution.py:97
  (39 shorter events, 2.0 us)
Async XLA Ops:
  0.0 19.6 %copy-start.5 = (f32[4]{0:T(128)S(1)}, f32[4]{0:T(128)}, u32[]{:S(2)}) copy-start(f32[4]{0:T(128)} %constant.113.clone) | copy-start | bytes 52
  0.7 26.9 %copy-start = (f32[4,25,8,128]{3,2,1,0:T(8,128)S(1)}, f32[4,25,8,128]{3,2,1,0:T(8,128)}, u32[]{:S(2)}) copy-start(f32[4,25,8,128]{3,2,1,0:T(8,128)} %param.6) | copy-start | bytes 1228804
  2.3 17.7 %collective-permute-start.1 = (f32[101,4,128]{2,1,0:T(4,128)S(1)}, f32[101,4,128]{2,1,0:T(4,128)S(1)}, u32[]{:S(2)}, u32[]{:S(2)}) collective-permute-start(f32[101,4,128]{2,1,0:T(4,128)S(1)} %get-tuple-element.23), channel_id=1, source_target_pairs={{1,2},{3,4},{5,6},{2,1},{4,3},{6,5},{9,10},{11,12},{13,14},{10,9},... | collective-permute-start | bytes 620552 | tf_op jit(solution)/shard_map/ppermute | solution.py:34
  4.4 23.0 %collective-permute-start = (f32[101,4,128]{2,1,0:T(4,128)S(1)}, f32[101,4,128]{2,1,0:T(4,128)S(1)}, u32[]{:S(2)}, u32[]{:S(2)}) collective-permute-start(f32[101,4,128]{2,1,0:T(4,128)S(1)} %get-tuple-element.24), channel_id=1, source_target_pairs={{0,1},{1,0},{2,3},{3,2},{4,5},{5,4},{6,7},{7,6},{8,9},{9,8},{10,11... | collective-permute-start | bytes 620552 | tf_op jit(solution)/shard_map/ppermute | solution.py:35
  19.5 14.0 %copy-start.3 = (f32[101,8,128]{2,1,0:T(8,128)}, f32[101,8,128]{2,1,0:T(8,128)S(1)}, u32[]{:S(2)}) copy-start(f32[101,8,128]{2,1,0:T(8,128)S(1)} %pad_maximum_fusion.1) | copy-start | bytes 1241092
  28.3 18.0 %collective-permute-start.3 = (f32[4848]{0:T(1024)S(1)}, f32[4848]{0:T(1024)S(1)}, u32[]{:S(2)}, u32[]{:S(2)}) collective-permute-start(f32[4848]{0:T(1024)S(1)} %select_n.110), channel_id=1, source_target_pairs={{8,16},{24,32},{40,48},{56,64},{72,80},{88,96},{104,112},{120,128}... | collective-permute-start | bytes 58184 | tf_op jit(solution)/shard_map/ppermute | solution.py:54
  33.6 2.5 %slice-start = ((f32[101,8,128]{2,1,0:T(8,128)}), f32[100,8,128]{2,1,0:T(8,128)S(1)}, s32[]{:S(2)}) async-start(f32[101,8,128]{2,1,0:T(8,128)} %copy-done.3), calls=%async_computation | async-start | bytes 819200 | tf_op jit(solution)/shard_map/slice | solution.py:62
  34.1 3.1 %collective-permute-start.2 = (f32[4848]{0:T(1024)S(1)}, f32[4848]{0:T(1024)S(1)}, u32[]{:S(2)}, u32[]{:S(2)}) collective-permute-start(f32[4848]{0:T(1024)S(1)} %select_n.112), channel_id=1, source_target_pairs={{0,8},{8,0},{16,24},{24,16},{32,40},{40,32},{48,56},{56,48},{64,72... | collective-permute-start | bytes 58184 | tf_op jit(solution)/shard_map/ppermute | solution.py:58
  48.0 2.0 %copy-start.1 = (f32[100,16,4]{2,1,0:T(8,128)S(1)}, f32[100,16,4]{2,1,0:T(8,128)}, u32[]{:S(2)}) copy-start(f32[100,16,4]{2,1,0:T(8,128)} %pad_slice_fusion.2) | copy-start | bytes 76804
  49.0 14.7 %copy-start.2 = (f32[100,16,4]{2,1,0:T(8,128)S(1)}, f32[100,16,4]{2,1,0:T(8,128)}, u32[]{:S(2)}) copy-start(f32[100,16,4]{2,1,0:T(8,128)} %pad_slice_fusion) | copy-start | bytes 76804
  86.8 1.0 %copy-start.4 = (f32[25,12,132]{2,1,0:T(8,128)S(1)}, f32[25,12,132]{2,1,0:T(8,128)}, u32[]{:S(2)}) copy-start(f32[25,12,132]{2,1,0:T(8,128)} %compare_convert_fusion) | copy-start | bytes 475204

commit v20 on v18

--- a/solution.py
+++ b/solution.py
@@ -18,14 +18,13 @@
     return (1.2 * jnp.sin(-1.3 + 2.8 * (mirrored.astype(jnp.float32) + 0.5) / total))[:, None]
 
 
-def gather_wide(x, signs):
+def gather_wide(x, signs, edge_rows):
     n_lon = lax.axis_size("lon")
     n_lat = lax.axis_size("lat")
 
     lat = lax.axis_index("lat")
     odd = lat % 2 == 1
-    top_rows = x[:, -WIDE:, :]
-    bottom_rows = x[:, :WIDE, :]
+    top_rows, bottom_rows = edge_rows
     inner = [(i, i + 1) for i in range(1, n_lat - 1, 2)]
     inner = inner + [(j, i) for i, j in inner]
     top = n_lat - 1
@@ -101,7 +100,14 @@
     channels = jnp.concatenate([state.reshape(n_fields * level_count, tile_rows, tile_cols), depth[None]])
     signs = jnp.array([1.0, 1.0, -1.0, -1.0], dtype=jnp.float32)
     signs = jnp.concatenate([jnp.repeat(signs, level_count), jnp.ones((1,), jnp.float32)])
-    wide_state, wide_depth = gather_wide(channels, signs[:, None, None])
+    def edge(first):
+        rows = slice(first, first + WIDE)
+        own = state.reshape(n_fields * level_count, tile_rows, tile_cols)[:, rows]
+        deep = jnp.where(sea_mask[rows] == 1, levels[rows], 0).astype(jnp.float32)
+        return jnp.concatenate([own, deep[None]])
+
+    edge_rows = (edge(tile_rows - WIDE), edge(0))
+    wide_state, wide_depth = gather_wide(channels, signs[:, None, None], edge_rows)
 
     lat = lax.axis_index("lat")
     total = lax.axis_size("lat") * tile_rows

time: 55.8 us -> 55.7 us (level)
  other arithmetic: 11.8 us -> 10.5 us
  local copies, waits for them, and re-layouts: 2.6 us -> 3.21 us
  waiting for transfers between devices: 17.6 us -> 18.2 us
    select_n x1, other arithmetic: 1.45 us -> 0.09 us  [gather_wide(): jnp.where(odd, top_rows, bottom_rows)]
    slice x0 -> x1, local copies, waits for them, and re-layouts: none -> 1.25 us  [edge(): own = state.reshape(n_fields * level_count, tile_rows, tile_cols)[:, rows]]
    broadcast_in_dim x0 -> x1, other arithmetic: none -> 0.77 us  [edge(): return jnp.concatenate([own, deep[None]])]
    convert_element_type x1, other arithmetic: 0.76 us -> 0.01 us  [shards(): depth = jnp.where(sea_mask == 1, levels, 0).astype(jnp.float32)]
    broadcast_in_dim x1, local copies, waits for them, and re-layouts: 0.73 us -> 0.07 us  [shards(): jnp.repeat(signs, level_count)]
    ppermute x1, waiting for transfers between devices: 7.31 us -> 7.93 us  [gather_wide(): lax.ppermute(jnp.where(odd, bottom_rows, top_rows), ('lon', 'lat'), [(l *...]
  transfers between devices with their start and end apart: 4 -> 4, of which waited for: 3 -> 3; matrix products, arithmetic and copies ran while one was open for 4% -> 3% of each run, Pallas kernels for 0% -> 0%
where the time goes in v20:
time: 55.7 us; the launch traced here: 55.5 us
  starting transfers between devices  23.3 us (42%)
  waiting for transfers between devices  18.2 us (33%)
  other arithmetic  10.5 us (19%)
  local copies, waits for them, and re-layouts  3.21 us (6%)
    ppermute x1, starting transfers between devices, gather_wide(): lax.ppermute(jnp.where(odd, bottom_rows, top_rows), ('lon', 'lat'), [(l *...  14.1 us
    ppermute x1, waiting for transfers between devices, gather_wide(): off_chip = lax.ppermute(off_send, 'lon', across)  9.2 us
    ppermute x1, waiting for transfers between devices, gather_wide(): lax.ppermute(jnp.where(odd, bottom_rows, top_rows), ('lon', 'lat'), [(l *...  7.93 us
    ppermute x1, starting transfers between devices, gather_wide(): off_chip = lax.ppermute(off_send, 'lon', across)  5.22 us
    select_n x1, other arithmetic, shards(): once = jnp.where(south_edge[:, None], 0.0, once)  3.74 us
    ppermute x1, starting transfers between devices, gather_wide(): lax.ppermute(jnp.where(odd, top_rows, bottom_rows), ('lon', 'lat'), pairs)  2.02 us
    ppermute x1, starting transfers between devices, gather_wide(): on_chip = lax.ppermute(on_send, 'lon', [(m, m ^ 1) for m in range(n_lon)])  1.92 us
    mul x1, other arithmetic, advance(): return wet * (centre + TIME_INCREMENT * (tendency + forcing))  1.68 us
  transfers between devices with their start and end apart: 4, of which 3 were waited for; matrix products, arithmetic and copies ran while one was open for 3% of the time, Pallas kernels for 0%

profile of v20, /device:TPU:192, one launch (start us, length us, event | category | flops | bytes accessed | tf_op | source)
XLA Modules:
  0.0 55.5 jit_solution(11109610830723648094)
XLA Ops:
  0.0 1.3 %fusion.76 = (f32[100,4,128]{2,1,0:T(4,128)S(1)}, f32[100,4,128]{2,1,0:T(4,128)S(1)}) fusion(f32[100,8,128]{2,1,0:T(8,128)} %bitcast.52), kind=kLoop, calls=%fused_computation.129 | loop fusion | bytes 819200 | tf_op jit(solution)/shard_map/slice | solution.py:105
  1.3 0.8 %convert_bitcast_fusion.1 = (f32[1,4,128]{2,1,0:T(4,128)S(1)}, f32[1,4,128]{2,1,0:T(4,128)S(1)}) fusion(s32[8,128]{1,0:T(8,128)} %param.8, s32[8,128]{1,0:T(8,128)} %param.7), kind=kLoop, calls=%fused_computation.105 | loop fusion | flops 3072 | bytes 12288 | tf_op jit(solution)/shard_map/broadcast_in_dim | solution.py:107
  2.2 2.0 %collective-permute-start.1 = (f32[101,4,128]{2,1,0:T(4,128)S(1)}, f32[101,4,128]{2,1,0:T(4,128)S(1)}, u32[]{:S(2)}, u32[]{:S(2)}) collective-permute-start(f32[101,4,128]{2,1,0:T(4,128)S(1)} %get-tuple-element.17), channel_id=1, source_target_pairs={{1,2},{3,4},{5,6},{2,1},{4,3},{6,5},{9,10},{11,12},{13,14},{10,9},... | collective-permute-start | bytes 620552 | tf_op jit(solution)/shard_map/ppermute | solution.py:33
  4.2 14.1 %collective-permute-start = (f32[101,4,128]{2,1,0:T(4,128)S(1)}, f32[101,4,128]{2,1,0:T(4,128)S(1)}, u32[]{:S(2)}, u32[]{:S(2)}) collective-permute-start(f32[101,4,128]{2,1,0:T(4,128)S(1)} %get-tuple-element.18), channel_id=1, source_target_pairs={{0,1},{1,0},{2,3},{3,2},{4,5},{5,4},{6,7},{7,6},{8,9},{9,8},{10,11... | collective-permute-start | bytes 620552 | tf_op jit(solution)/shard_map/ppermute | solution.py:34
  18.8 0.4 rev.4
  19.3 7.9 %collective-permute-done = f32[101,4,128]{2,1,0:T(4,128)S(1)} collective-permute-done((f32[101,4,128]{2,1,0:T(4,128)S(1)}, f32[101,4,128]{2,1,0:T(4,128)S(1)}, u32[]{:S(2)}, u32[]{:S(2)}) %collective-permute-start) | collective-permute-done | bytes 206880 | tf_op jit(solution)/shard_map/ppermute | solution.py:34
  27.2 0.2 broadcast_select_fusion
  27.4 0.2 pad_maximum_fusion.1
  27.6 0.3 slice_select_fusion
  27.8 0.2 select_n.119
  28.1 5.2 %collective-permute-start.3 = (f32[4848]{0:T(1024)S(1)}, f32[4848]{0:T(1024)S(1)}, u32[]{:S(2)}, u32[]{:S(2)}) collective-permute-start(f32[4848]{0:T(1024)S(1)} %select_n.119), channel_id=1, source_target_pairs={{8,16},{24,32},{40,48},{56,64},{72,80},{88,96},{104,112},{120,128}... | collective-permute-start | bytes 58184 | tf_op jit(solution)/shard_map/ppermute | solution.py:53
  33.3 0.3 slice_select_fusion.1
  33.6 0.2 select_n.121
  33.8 1.9 %collective-permute-start.2 = (f32[4848]{0:T(1024)S(1)}, f32[4848]{0:T(1024)S(1)}, u32[]{:S(2)}, u32[]{:S(2)}) collective-permute-start(f32[4848]{0:T(1024)S(1)} %select_n.121), channel_id=1, source_target_pairs={{0,8},{8,0},{16,24},{24,16},{32,40},{40,32},{48,56},{56,48},{64,72... | collective-permute-start | bytes 58184 | tf_op jit(solution)/shard_map/ppermute | solution.py:57
  35.8 1.1 %collective-permute-done.2 = f32[4848]{0:T(1024)S(1)} collective-permute-done((f32[4848]{0:T(1024)S(1)}, f32[4848]{0:T(1024)S(1)}, u32[]{:S(2)}, u32[]{:S(2)}) %collective-permute-start.2) | collective-permute-done | bytes 19424 | tf_op jit(solution)/shard_map/ppermute | solution.py:57
  36.9 9.2 %collective-permute-done.3 = f32[4848]{0:T(1024)S(1)} collective-permute-done((f32[4848]{0:T(1024)S(1)}, f32[4848]{0:T(1024)S(1)}, u32[]{:S(2)}, u32[]{:S(2)}) %collective-permute-start.3) | collective-permute-done | bytes 19424 | tf_op jit(solution)/shard_map/ppermute | solution.py:53
  46.1 0.3 reshape.88
  46.4 0.3 reshape.89
  46.8 0.2 pad_slice_fusion
  47.2 1.2 %pad_maximum_fusion = f32[100,16,136]{2,1,0:T(8,128)S(1)} fusion(f32[100,16,4]{2,1,0:T(8,128)S(1)} %get-tuple-element.27, f32[100,4,128]{2,1,0:T(4,128)S(1)} %slice.273, f32[100,8,128]{2,1,0:T(8,128)S(1)} %bitcast.54, f32[100,4,128]{2,1,0:T(4,128)S(1)} %slice.272, f32[100,16,4]{2,1,0:T(8,128)S(1)} %get-tuple-element.28), kind=kLoop, calls=%fused_computation.13 | loop fusion | flops 870400 | bytes 1740800 | tf_op jit(solution)/shard_map/concatenate | solution.py:63
  48.6 1.0 %fusion.32 = (f32[1,25,12,132]{3,2,1,0:T(8,128)S(1)}, f32[1,25,12,132]{3,2,1,0:T(8,128)S(1)}, f32[25,12,132]{2,1,0:T(8,128)S(1)}, f32[25,12,132]{2,1,0:T(8,128)S(1)}) fusion(f32[25,16,136]{2,1,0:T(8,128)S(1)} %reduce-window_multiply_fusion.1, f32[4,25,16,136]{3,2,1,0:T(8,128)S(1)} %bitcast.50, f32[12]{0:T(128)S(1)} %get-tuple-element.31, ...), kind=kLoop, calls=%fused_computation.50 | loop fusion | flops 633600 | bytes 2217696 | tf_op jit(solution)/shard_map/stack | solution.py:91
  49.6 3.7 %fusion.8 = f32[4,25,12,132]{3,2,1,0:T(8,128)S(1)} fusion(f32[4,25,16,136]{3,2,1,0:T(8,128)S(1)} %bitcast.51, f32[1,25,12,132]{3,2,1,0:T(8,128)S(1)} %get-tuple-element.10, f32[1,25,12,132]{3,2,1,0:T(8,128)S(1)} %get-tuple-element.9, f32[4]{0:T(128)S(1)} %pad.12.clone, f32[25,12,132]{2,1,0:T(8,128)S(1)} %get-tuple-element.14, ...), kind=kLoop, calls=%fused_computation.9 | loop fusion | flops 3960000 | bytes 7128028 | tf_op jit(solution)/shard_map/jit(_where)/select_n | solution.py:122
  53.5 0.3 fusion.52
  53.8 1.7 %fusion.21 = f32[4,25,8,128]{3,2,1,0:T(8,128)} fusion(f32[4,25,12,132]{3,2,1,0:T(8,128)S(1)} %fusion.8, f32[1,25,8,128]{3,2,1,0:T(8,128)S(1)} %get-tuple-element.8, f32[1,25,8,128]{3,2,1,0:T(8,128)S(1)} %get-tuple-element.7, f32[4]{0:T(128)S(1)} %pad.12.clone, f32[25,8,128]{2,1,0:T(8,128)S(1)} %get-tuple-element.12, f32[25,8,128]{2,1,0:T(8,128)S(1)} %get-tuple-element.11, ...), kind=kLoop, calls=%fused_computation.35 | loop fusion | flops 2457600 | bytes 4608016 | tf_op jit(solution)/shard_map/mul | solution.py:94
  (30 shorter events, 1.1 us)
Async XLA Ops:
  0.0 18.4 %copy-start.3 = (f32[4]{0:T(128)S(1)}, f32[4]{0:T(128)}, u32[]{:S(2)}) copy-start(f32[4]{0:T(128)} %constant.112.clone) | copy-start | bytes 52
  0.0 18.3 %copy-start.2 = (s32[8,128]{1,0:T(8,128)S(1)}, s32[8,128]{1,0:T(8,128)}, u32[]{:S(2)}) copy-start(s32[8,128]{1,0:T(8,128)} %param.7) | copy-start | bytes 12292
  0.0 18.3 %copy-start.1 = (s32[8,128]{1,0:T(8,128)S(1)}, s32[8,128]{1,0:T(8,128)}, u32[]{:S(2)}) copy-start(s32[8,128]{1,0:T(8,128)} %param.8) | copy-start | bytes 12292
  0.0 27.4 %copy-start = (f32[4,25,8,128]{3,2,1,0:T(8,128)S(1)}, f32[4,25,8,128]{3,2,1,0:T(8,128)}, u32[]{:S(2)}) copy-start(f32[4,25,8,128]{3,2,1,0:T(8,128)} %param.6) | copy-start | bytes 1228804
  2.2 16.7 %collective-permute-start.1 = (f32[101,4,128]{2,1,0:T(4,128)S(1)}, f32[101,4,128]{2,1,0:T(4,128)S(1)}, u32[]{:S(2)}, u32[]{:S(2)}) collective-permute-start(f32[101,4,128]{2,1,0:T(4,128)S(1)} %get-tuple-element.17), channel_id=1, source_target_pairs={{1,2},{3,4},{5,6},{2,1},{4,3},{6,5},{9,10},{11,12},{13,14},{10,9},... | collective-permute-start | bytes 620552 | tf_op jit(solution)/shard_map/ppermute | solution.py:33
  4.2 23.0 %collective-permute-start = (f32[101,4,128]{2,1,0:T(4,128)S(1)}, f32[101,4,128]{2,1,0:T(4,128)S(1)}, u32[]{:S(2)}, u32[]{:S(2)}) collective-permute-start(f32[101,4,128]{2,1,0:T(4,128)S(1)} %get-tuple-element.18), channel_id=1, source_target_pairs={{0,1},{1,0},{2,3},{3,2},{4,5},{5,4},{6,7},{7,6},{8,9},{9,8},{10,11... | collective-permute-start | bytes 620552 | tf_op jit(solution)/shard_map/ppermute | solution.py:34
  28.1 18.0 %collective-permute-start.3 = (f32[4848]{0:T(1024)S(1)}, f32[4848]{0:T(1024)S(1)}, u32[]{:S(2)}, u32[]{:S(2)}) collective-permute-start(f32[4848]{0:T(1024)S(1)} %select_n.119), channel_id=1, source_target_pairs={{8,16},{24,32},{40,48},{56,64},{72,80},{88,96},{104,112},{120,128}... | collective-permute-start | bytes 58184 | tf_op jit(solution)/shard_map/ppermute | solution.py:53
  33.8 3.1 %collective-permute-start.2 = (f32[4848]{0:T(1024)S(1)}, f32[4848]{0:T(1024)S(1)}, u32[]{:S(2)}, u32[]{:S(2)}) collective-permute-start(f32[4848]{0:T(1024)S(1)} %select_n.121), channel_id=1, source_target_pairs={{0,8},{8,0},{16,24},{24,16},{32,40},{40,32},{48,56},{56,48},{64,72... | collective-permute-start | bytes 58184 | tf_op jit(solution)/shard_map/ppermute | solution.py:57
